TPU v7x, 128 devices: a whole 4x4x4 slice. The times are simulated.
128 devices in a mesh: seq: 32 (over z, x, core), store: 4 (over y).
Axes of the slice: x: 4, y: 4, z: 4, core: 2. Of those that a mesh axis runs over, the one named last changes fastest.
Arguments:
- queries: bfloat16 [4, 4096, 4096], P('store', 'seq'), may hold values from -12 to 12
- keys: bfloat16 [4, 4096, 512], P('store', 'seq'), may hold values from -6 to 6
- values: bfloat16 [4, 4096, 512], P('store', 'seq'), may hold values from -6 to 6
- segment_ids: int32 [4, 4096], P('store', 'seq'), may hold values from 0 to 3, never falling along the last dimension, each value on 1 to 2048 neighbouring positions
- route_ids: int32 [4, 4096], P('store', 'seq'), may hold values from 0 to 2047, as said below
- adapter_down: bfloat16 [4096, 131072], P(None, ('seq', 'store')), may hold values from -0.09375 to 0.09375
- adapter_up: bfloat16 [131072, 4096], P(('seq', 'store')), may hold values from -0.75 to 0.75
Outputs:
- mixed: bfloat16 [4, 4096, 4096], P('store', 'seq')
Inputs may be any that keep to these rules, and one draw needn't show every extreme that they name: `route_ids`: among the 128 tokens of one device (positions j * 128 to j * 128 + 127 of one sequence), at most 2 name adapters of any one owner, the owner of adapter e being the device of flat index e // 16 over seq then store; in every draw some owner gets exactly 2 tokens from every device.
All inputs are finite; a program needn't handle non-finite values.
Results may differ from a plain program's by a relative error of at most 0.006.
Values may be sent and summed in bfloat16 or wider, within the bound.
No kernel may reach another device: no remote copies, remote signals or barrier semaphores. Data moves between devices by JAX's collectives and lax.ppermute only.
A program may use at most 128 MiB of HBM per device.

v0:
```python
import jax
import jax.numpy as jnp
from jax import lax
from jax.sharding import PartitionSpec as P

HEAD_DIM = 128
HEADS = 32
KV_HEADS = 4
RANK = 64
EXP_DEV = 16


def attend(queries, key_rows, value_rows, segments):
    length = queries.shape[0]
    block = min(512, length)
    scale = queries.shape[2] ** (-0.5)
    key_pos = jnp.arange(length, dtype=jnp.int32)

    def one_block(index):
        start = index * block
        q_block = lax.dynamic_slice_in_dim(queries, start, block, 0)
        seg_block = lax.dynamic_slice_in_dim(segments, start, block, 0)
        scores = (
            jnp.einsum("qhd,nd->hqn", q_block, key_rows, preferred_element_type=jnp.float32) * scale
        )
        q_pos = start + jnp.arange(block, dtype=jnp.int32)
        allowed = (key_pos[None, :] <= q_pos[:, None]) & (segments[None, :] == seg_block[:, None])
        scores = jnp.where(allowed[None], scores, jnp.float32(-1e30))
        top = jnp.max(scores, axis=-1, keepdims=True)
        expo = jnp.exp(scores - top)
        total = jnp.sum(expo, axis=-1)
        summed = jnp.einsum(
            "hqn,nd->qhd", expo.astype(jnp.bfloat16), value_rows, preferred_element_type=jnp.float32
        )
        out = summed / jnp.transpose(total)[:, :, None]
        return out.astype(jnp.bfloat16).reshape(block, -1)

    blocks = lax.map(one_block, jnp.arange(length // block, dtype=jnp.int32))
    return blocks.reshape(length, -1)


def local(queries, keys, values, segment_ids, route_ids, adapter_down, adapter_up):
    n_seq = lax.axis_size("seq")
    n_store = lax.axis_size("store")
    tok_rows = queries.shape[1]
    width = queries.shape[2]
    length = tok_rows * n_seq
    heads_here = HEADS // n_seq
    q_send = queries.reshape(tok_rows, n_seq, heads_here * HEAD_DIM)
    paired = jnp.concatenate(
        [keys.reshape(tok_rows, KV_HEADS, HEAD_DIM), values.reshape(tok_rows, KV_HEADS, HEAD_DIM)],
        axis=2,
    )
    kv_send = jnp.repeat(paired, n_seq // KV_HEADS, axis=1)
    q_all, kv_all = (
        lax.all_to_all(q_send, "seq", split_axis=1, concat_axis=0, tiled=True),
        lax.all_to_all(kv_send, "seq", split_axis=1, concat_axis=0, tiled=True),
    )
    segments = lax.all_gather(segment_ids, "seq", axis=1, tiled=True)[0]
    context = attend(q_all, kv_all[:, 0, :HEAD_DIM], kv_all[:, 0, HEAD_DIM:], segments)
    returned_ctx = lax.all_to_all(
        context.reshape(length, 1, heads_here * HEAD_DIM),
        "seq",
        split_axis=0,
        concat_axis=1,
        tiled=True,
    )
    tok_ctx = returned_ctx.reshape(tok_rows, width)
    devices = n_seq * n_store
    capacity = max(2, 2 * tok_rows // devices)
    chosen = route_ids[0]
    owners = chosen // EXP_DEV
    one_hot = (owners[:, None] == jnp.arange(devices, dtype=jnp.int32)[None, :]).astype(jnp.int32)
    slot_of = jnp.sum(jnp.cumsum(one_hot, axis=0) * one_hot, axis=1) - 1
    placed = owners * capacity + slot_of
    send_rows = jnp.zeros((devices * capacity, width), jnp.bfloat16).at[placed].set(tok_ctx)
    send_tags = (
        jnp.full((devices * capacity,), -1.0, jnp.float32)
        .at[placed]
        .set((chosen % EXP_DEV).astype(jnp.float32))
        .astype(jnp.bfloat16)
    )
    got_rows = lax.all_to_all(
        send_rows.reshape(devices, capacity, width),
        ("seq", "store"),
        split_axis=0,
        concat_axis=0,
        tiled=True,
    )
    flat_rows = got_rows.reshape(-1, width)
    low = jnp.dot(flat_rows, adapter_down, preferred_element_type=jnp.float32)
    lane_owner = (jnp.arange(low.shape[1], dtype=jnp.int32) // RANK).astype(jnp.float32)
    keep_mask = (
        lax.all_to_all(
            send_tags.reshape(devices, capacity),
            ("seq", "store"),
            split_axis=0,
            concat_axis=0,
            tiled=True,
        )
        .reshape(-1, 1)
        .astype(jnp.float32)
        == lane_owner[None, :]
    )
    low = jnp.where(keep_mask, low, 0.0).astype(jnp.bfloat16)
    delta = jnp.dot(low, adapter_up, preferred_element_type=jnp.float32).astype(jnp.bfloat16)
    answer = lax.all_to_all(
        delta.reshape(got_rows.shape), ("seq", "store"), split_axis=0, concat_axis=0, tiled=True
    )
    delta_rows = answer.reshape(devices * capacity, width)[placed]
    mixed = (tok_ctx.astype(jnp.float32) + delta_rows.astype(jnp.float32)).astype(jnp.bfloat16)
    return mixed[None]


def solution(mesh):
    return jax.shard_map(
        local,
        mesh=mesh,
        in_specs=(
            P("store", "seq", None),
            P("store", "seq", None),
            P("store", "seq", None),
            P("store", "seq"),
            P("store", "seq"),
            P(None, ("seq", "store")),
            P(("seq", "store"), None),
        ),
        out_specs=P("store", "seq", None),
        check_vma=False,
    )
```

profile of v0, /device:TPU:1, one launch (start us, length us, event | category | flops | bytes accessed | tf_op | source)
XLA Modules:
  0.0 287.5 jit_solution(14617275699483279833)
XLA Ops:
  0.0 2.3 copy.30
  2.3 9.4 %all-to-all-start = ((bf16[128,32,128]{0,2,1:T(8,128)(2,1)}), bf16[128,32,128]{0,2,1:T(8,128)(2,1)S(1)}, u32[]{:S(2)}, u32[]{:S(2)}) async-start(bf16[128,32,128]{0,2,1:T(8,128)(2,1)} %bitcast.1), calls=%async_computation | async-start | bytes 2097152 | tf_op jit(solution)/shard_map/all_to_all | solution.py:56
  12.0 16.8 %all-to-all-done = bf16[128,32,128]{0,2,1:T(8,128)(2,1)S(1)} async-done(((bf16[128,32,128]{0,2,1:T(8,128)(2,1)}), bf16[128,32,128]{0,2,1:T(8,128)(2,1)S(1)}, u32[]{:S(2)}, u32[]{:S(2)}) %all-to-all-start) | async-done | bytes 1048608 | tf_op jit(solution)/shard_map/all_to_all | solution.py:56
  30.4 4.1 %all-to-all-start.1 = ((bf16[128,32,256]{2,0,1:T(8,128)(2,1)}), bf16[128,32,256]{2,0,1:T(8,128)(2,1)S(1)}, u32[]{:S(2)}, u32[]{:S(2)}) async-start(bf16[128,32,256]{2,0,1:T(8,128)(2,1)} %bitcast.127), calls=%async_computation.1 | async-start | bytes 4194304 | tf_op jit(solution)/shard_map/all_to_all | solution.py:57
  34.5 41.3 %all_gather.3 = s32[1,4096]{1,0:T(1,128)S(1)} all-gather(s32[1,128]{1,0:T(1,128)S(1)} %copy-done.2), channel_id=1, replica_groups=mesh['seq'=32,'store'=4] {'seq'}, dimensions={1}, use_global_device_ids=true | all-gather | bytes 16896 | tf_op jit(solution)/shard_map/all_gather | solution.py:59
  78.3 68.4 %while.11 = (s32[]{:T(128)}, bf16[8,512,128]{2,1,0:T(8,128)(2,1)}, s32[8]{0:T(128)S(1)}, s32[1,4096]{1,0:T(1,128)S(1)}, s32[4096]{0:T(1024)S(1)}, /*index=5*/bf1...) while((s32[]{:T(128)}, bf16[8,512,128]{2,1,0:T(8,128)(2,1)}, ...), condition=%wide.region_3.4_spmd.clone, body=%wide.region_0.3_spmd.clone.sunk | while | flops 1094843904 | bytes 27562184 | solution.py:38
  79.7 3.8 %fusion.59 = (f32[512]{0:T(512)S(1)}, f32[1,512,4096]{2,1,0:T(8,128)S(1)}) fusion(bf16[4096,128]{1,0:T(8,128)(2,1)} %get-tuple-element.176, bf16[4096,1,128]{2,0,1:T(8,128)(2,1)} %get-tuple-element.175, s32[]{:T(128)S(6)} %select_n.85, s32[512]{0:T(512)S(1)} %dynamic_slice.24, s32[4096]{0:T(1024)S(1)} %get-tuple-element.174, s32[512]{0:T(512)S(1)} %iota_add_fusion.2), kind=kOutput, calls=%fused_computation.66.clone.1 | convolution fusion | flops 549453312 | bytes 9590788 | tf_op jit(solution)/shard_map/while/body/eval_jaxpr/qhd,nd->hqn/dot_general | solution.py:24
  88.3 3.8 %fusion.59 = (f32[512]{0:T(512)S(1)}, f32[1,512,4096]{2,1,0:T(8,128)S(1)}) fusion(bf16[4096,128]{1,0:T(8,128)(2,1)} %get-tuple-element.176, bf16[4096,1,128]{2,0,1:T(8,128)(2,1)} %get-tuple-element.175, s32[]{:T(128)S(6)} %select_n.85, s32[512]{0:T(512)S(1)} %dynamic_slice.24, s32[4096]{0:T(1024)S(1)} %get-tuple-element.174, s32[512]{0:T(512)S(1)} %iota_add_fusion.2), kind=kOutput, calls=%fused_computation.66.clone.1 | convolution fusion | flops 549453312 | bytes 9590788 | tf_op jit(solution)/shard_map/while/body/eval_jaxpr/qhd,nd->hqn/dot_general | solution.py:24
  93.4 2.0 fusion.61
  96.8 3.8 %fusion.59 = (f32[512]{0:T(512)S(1)}, f32[1,512,4096]{2,1,0:T(8,128)S(1)}) fusion(bf16[4096,128]{1,0:T(8,128)(2,1)} %get-tuple-element.176, bf16[4096,1,128]{2,0,1:T(8,128)(2,1)} %get-tuple-element.175, s32[]{:T(128)S(6)} %select_n.85, s32[512]{0:T(512)S(1)} %dynamic_slice.24, s32[4096]{0:T(1024)S(1)} %get-tuple-element.174, s32[512]{0:T(512)S(1)} %iota_add_fusion.2), kind=kOutput, calls=%fused_computation.66.clone.1 | convolution fusion | flops 549453312 | bytes 9590788 | tf_op jit(solution)/shard_map/while/body/eval_jaxpr/qhd,nd->hqn/dot_general | solution.py:24
  101.9 2.0 fusion.61
  105.4 3.8 %fusion.59 = (f32[512]{0:T(512)S(1)}, f32[1,512,4096]{2,1,0:T(8,128)S(1)}) fusion(bf16[4096,128]{1,0:T(8,128)(2,1)} %get-tuple-element.176, bf16[4096,1,128]{2,0,1:T(8,128)(2,1)} %get-tuple-element.175, s32[]{:T(128)S(6)} %select_n.85, s32[512]{0:T(512)S(1)} %dynamic_slice.24, s32[4096]{0:T(1024)S(1)} %get-tuple-element.174, s32[512]{0:T(512)S(1)} %iota_add_fusion.2), kind=kOutput, calls=%fused_computation.66.clone.1 | convolution fusion | flops 549453312 | bytes 9590788 | tf_op jit(solution)/shard_map/while/body/eval_jaxpr/qhd,nd->hqn/dot_general | solution.py:24
  110.5 2.0 fusion.61
  113.9 3.8 %fusion.59 = (f32[512]{0:T(512)S(1)}, f32[1,512,4096]{2,1,0:T(8,128)S(1)}) fusion(bf16[4096,128]{1,0:T(8,128)(2,1)} %get-tuple-element.176, bf16[4096,1,128]{2,0,1:T(8,128)(2,1)} %get-tuple-element.175, s32[]{:T(128)S(6)} %select_n.85, s32[512]{0:T(512)S(1)} %dynamic_slice.24, s32[4096]{0:T(1024)S(1)} %get-tuple-element.174, s32[512]{0:T(512)S(1)} %iota_add_fusion.2), kind=kOutput, calls=%fused_computation.66.clone.1 | convolution fusion | flops 549453312 | bytes 9590788 | tf_op jit(solution)/shard_map/while/body/eval_jaxpr/qhd,nd->hqn/dot_general | solution.py:24
  122.5 3.8 %fusion.59 = (f32[512]{0:T(512)S(1)}, f32[1,512,4096]{2,1,0:T(8,128)S(1)}) fusion(bf16[4096,128]{1,0:T(8,128)(2,1)} %get-tuple-element.176, bf16[4096,1,128]{2,0,1:T(8,128)(2,1)} %get-tuple-element.175, s32[]{:T(128)S(6)} %select_n.85, s32[512]{0:T(512)S(1)} %dynamic_slice.24, s32[4096]{0:T(1024)S(1)} %get-tuple-element.174, s32[512]{0:T(512)S(1)} %iota_add_fusion.2), kind=kOutput, calls=%fused_computation.66.clone.1 | convolution fusion | flops 549453312 | bytes 9590788 | tf_op jit(solution)/shard_map/while/body/eval_jaxpr/qhd,nd->hqn/dot_general | solution.py:24
  131.0 3.8 %fusion.59 = (f32[512]{0:T(512)S(1)}, f32[1,512,4096]{2,1,0:T(8,128)S(1)}) fusion(bf16[4096,128]{1,0:T(8,128)(2,1)} %get-tuple-element.176, bf16[4096,1,128]{2,0,1:T(8,128)(2,1)} %get-tuple-element.175, s32[]{:T(128)S(6)} %select_n.85, s32[512]{0:T(512)S(1)} %dynamic_slice.24, s32[4096]{0:T(1024)S(1)} %get-tuple-element.174, s32[512]{0:T(512)S(1)} %iota_add_fusion.2), kind=kOutput, calls=%fused_computation.66.clone.1 | convolution fusion | flops 549453312 | bytes 9590788 | tf_op jit(solution)/shard_map/while/body/eval_jaxpr/qhd,nd->hqn/dot_general | solution.py:24
  139.5 3.8 %fusion.59 = (f32[512]{0:T(512)S(1)}, f32[1,512,4096]{2,1,0:T(8,128)S(1)}) fusion(bf16[4096,128]{1,0:T(8,128)(2,1)} %get-tuple-element.176, bf16[4096,1,128]{2,0,1:T(8,128)(2,1)} %get-tuple-element.175, s32[]{:T(128)S(6)} %select_n.85, s32[512]{0:T(512)S(1)} %dynamic_slice.24, s32[4096]{0:T(1024)S(1)} %get-tuple-element.174, s32[512]{0:T(512)S(1)} %iota_add_fusion.2), kind=kOutput, calls=%fused_computation.66.clone.1 | convolution fusion | flops 549453312 | bytes 9590788 | tf_op jit(solution)/shard_map/while/body/eval_jaxpr/qhd,nd->hqn/dot_general | solution.py:24
  147.2 2.7 reduce.6
  151.1 6.4 %all-to-all-start.2 = ((bf16[32,2,8192]{2,1,0:T(2,128)(2,1)}), bf16[32,2,8192]{2,1,0:T(2,128)(2,1)S(1)}, u32[]{:S(2)}, u32[]{:S(2)}) async-start(bf16[32,2,8192]{2,1,0:T(2,128)(2,1)} %reshape.356), calls=%async_computation.2 | async-start | bytes 2097152 | tf_op jit(solution)/shard_map/all_to_all | solution.py:61
  159.8 14.8 %all-to-all-done.2 = bf16[32,2,8192]{2,1,0:T(2,128)(2,1)S(1)} async-done(((bf16[32,2,8192]{2,1,0:T(2,128)(2,1)}), bf16[32,2,8192]{2,1,0:T(2,128)(2,1)S(1)}, u32[]{:S(2)}, u32[]{:S(2)}) %all-to-all-start.2) | async-done | bytes 1048608 | tf_op jit(solution)/shard_map/all_to_all | solution.py:61
  174.6 5.8 %all-to-all-start.3 = ((bf16[128,1,2]{2,1,0:T(2,128)(2,1)}), bf16[128,1,2]{2,1,0:T(2,128)(2,1)S(1)}, u32[]{:S(2)}, u32[]{:S(2)}) async-start(bf16[128,1,2]{2,1,0:T(2,128)(2,1)} %all_to_all.64), calls=%async_computation.3 | async-start | bytes 131072 | tf_op jit(solution)/shard_map/all_to_all | solution.py:94
  183.6 3.4 %scatter_custom_fusion.1 = bf16[256,4096]{1,0:T(8,128)(2,1)S(1)} fusion(s32[128]{0:T(128)S(1)} %fusion.40, bf16[128,4096]{1,0:T(8,128)(2,1)} %copy.37, bf16[]{:T(256)} %constant.71.clone.1), kind=kCustom, calls=%fused_computation.29 | custom fusion | bytes 2097664 | tf_op jit(solution)/shard_map/scatter | solution.py:76
  187.0 2.7 reshape.312
  190.0 9.4 %all-to-all-start.4 = ((bf16[128,2,4096]{2,1,0:T(2,128)(2,1)}), bf16[128,2,4096]{2,1,0:T(2,128)(2,1)S(1)}, u32[]{:S(2)}, u32[]{:S(2)}) async-start(bf16[128,2,4096]{2,1,0:T(2,128)(2,1)} %reshape.312), calls=%async_computation.4 | async-start | bytes 4194304 | tf_op jit(solution)/shard_map/all_to_all | solution.py:83
  199.8 30.2 %all-to-all-done.4 = bf16[128,2,4096]{2,1,0:T(2,128)(2,1)S(1)} async-done(((bf16[128,2,4096]{2,1,0:T(2,128)(2,1)}), bf16[128,2,4096]{2,1,0:T(2,128)(2,1)S(1)}, u32[]{:S(2)}, u32[]{:S(2)}) %all-to-all-start.4) | async-done | bytes 2097184 | tf_op jit(solution)/shard_map/all_to_all | solution.py:83
  229.9 2.2 reshape.313
  232.2 10.9 %convolution_convert_fusion = bf16[256,4096]{1,0:T(8,128)(2,1)S(1)} fusion(bf16[1024,4096]{1,0:T(8,128)(2,1)} %param.15, bf16[256,4096]{1,0:T(8,128)(2,1)} %reshape.313, bf16[4096,1024]{1,0:T(8,128)(2,1)} %param.14, f32[1024]{0:T(1024)S(1)} %fusion.35, f32[256]{0:T(256)S(1)} %reshape.317), kind=kOutput, calls=%fused_computation.22 | convolution fusion | flops 4296802304 | bytes 20976640 | tf_op jit(solution)/shard_map/dot_general | solution.py:106
  243.0 2.7 reshape.314
  245.7 4.7 %all-to-all-start.5 = ((bf16[128,2,4096]{2,1,0:T(2,128)(2,1)}), bf16[128,2,4096]{2,1,0:T(2,128)(2,1)}, u32[]{:S(2)}, u32[]{:S(2)}) async-start(bf16[128,2,4096]{2,1,0:T(2,128)(2,1)} %reshape.314), calls=%async_computation.5 | async-start | bytes 4194304 | tf_op jit(solution)/shard_map/all_to_all | solution.py:107
  252.6 28.2 %all-to-all-done.5 = bf16[128,2,4096]{2,1,0:T(2,128)(2,1)} async-done(((bf16[128,2,4096]{2,1,0:T(2,128)(2,1)}), bf16[128,2,4096]{2,1,0:T(2,128)(2,1)}, u32[]{:S(2)}, u32[]{:S(2)}) %all-to-all-start.5) | async-done | bytes 2097184 | tf_op jit(solution)/shard_map/all_to_all | solution.py:107
  280.8 2.7 reshape.315
  284.7 2.8 fusion.27
  (77 shorter events, 41.6 us)
Async XLA Ops:
  0.0 11.7 %copy-start = (bf16[1,128,512]{2,1,0:T(8,128)(2,1)S(1)}, bf16[1,128,512]{2,1,0:T(8,128)(2,1)}, u32[]{:S(2)}) copy-start(bf16[1,128,512]{2,1,0:T(8,128)(2,1)} %param.11) | copy-start | bytes 393220
  0.0 11.8 %copy-start.1 = (bf16[1,128,512]{2,1,0:T(8,128)(2,1)S(1)}, bf16[1,128,512]{2,1,0:T(8,128)(2,1)}, u32[]{:S(2)}) copy-start(bf16[1,128,512]{2,1,0:T(8,128)(2,1)} %param.10) | copy-start | bytes 393220
  2.3 26.5 %all-to-all-start = ((bf16[128,32,128]{0,2,1:T(8,128)(2,1)}), bf16[128,32,128]{0,2,1:T(8,128)(2,1)S(1)}, u32[]{:S(2)}, u32[]{:S(2)}) async-start(bf16[128,32,128]{0,2,1:T(8,128)(2,1)} %bitcast.1), calls=%async_computation | async-start | bytes 2097152 | tf_op jit(solution)/shard_map/all_to_all | solution.py:56
  11.7 22.7 %copy-start.2 = (s32[1,128]{1,0:T(1,128)S(1)}, s32[1,128]{1,0:T(1,128)}, u32[]{:S(2)}) copy-start(s32[1,128]{1,0:T(1,128)} %param.12) | copy-start | bytes 1540
  30.4 46.7 %all-to-all-start.1 = ((bf16[128,32,256]{2,0,1:T(8,128)(2,1)}), bf16[128,32,256]{2,0,1:T(8,128)(2,1)S(1)}, u32[]{:S(2)}, u32[]{:S(2)}) async-start(bf16[128,32,256]{2,0,1:T(8,128)(2,1)} %bitcast.127), calls=%async_computation.1 | async-start | bytes 4194304 | tf_op jit(solution)/shard_map/all_to_all | solution.py:57
  146.7 10.9 %copy-start.3 = (s32[1,128]{1,0:T(1,128)S(1)}, s32[1,128]{1,0:T(1,128)}, u32[]{:S(2)}) copy-start(s32[1,128]{1,0:T(1,128)} %param.13) | copy-start | bytes 1540
  151.1 23.5 %all-to-all-start.2 = ((bf16[32,2,8192]{2,1,0:T(2,128)(2,1)}), bf16[32,2,8192]{2,1,0:T(2,128)(2,1)S(1)}, u32[]{:S(2)}, u32[]{:S(2)}) async-start(bf16[32,2,8192]{2,1,0:T(2,128)(2,1)} %reshape.356), calls=%async_computation.2 | async-start | bytes 2097152 | tf_op jit(solution)/shard_map/all_to_all | solution.py:61
  174.6 15.4 %all-to-all-start.3 = ((bf16[128,1,2]{2,1,0:T(2,128)(2,1)}), bf16[128,1,2]{2,1,0:T(2,128)(2,1)S(1)}, u32[]{:S(2)}, u32[]{:S(2)}) async-start(bf16[128,1,2]{2,1,0:T(2,128)(2,1)} %all_to_all.64), calls=%async_computation.3 | async-start | bytes 131072 | tf_op jit(solution)/shard_map/all_to_all | solution.py:94
  190.0 40.0 %all-to-all-start.4 = ((bf16[128,2,4096]{2,1,0:T(2,128)(2,1)}), bf16[128,2,4096]{2,1,0:T(2,128)(2,1)S(1)}, u32[]{:S(2)}, u32[]{:S(2)}) async-start(bf16[128,2,4096]{2,1,0:T(2,128)(2,1)} %reshape.312), calls=%async_computation.4 | async-start | bytes 4194304 | tf_op jit(solution)/shard_map/all_to_all | solution.py:83
  245.7 35.1 %all-to-all-start.5 = ((bf16[128,2,4096]{2,1,0:T(2,128)(2,1)}), bf16[128,2,4096]{2,1,0:T(2,128)(2,1)}, u32[]{:S(2)}, u32[]{:S(2)}) async-start(bf16[128,2,4096]{2,1,0:T(2,128)(2,1)} %reshape.314), calls=%async_computation.5 | async-start | bytes 4194304 | tf_op jit(solution)/shard_map/all_to_all | solution.py:107
where the time goes:
time: 289 us; the launch traced here: 287 us
  waiting for transfers between devices  90.3 us (31%)
  matrix products  57.4 us (20%)
  blocking collectives  41.3 us (14%)
  starting transfers between devices  39.9 us (14%)
  local copies, waits for them, and re-layouts  36.2 us (13%)
  other arithmetic  16.6 us (6%)
  loops' own time  5.64 us (2%)
    all_gather x1, blocking collectives, local(): segments = lax.all_gather(segment_ids, 'seq', axis=1, tiled=True)[0]  41.3 us
    dot_general x8, matrix products, one_block(): jnp.einsum('qhd,nd->hqn', q_block, key_rows, preferred_element_type=jnp.f...  30.5 us
    all_to_all x1, waiting for transfers between devices, local(): lax.all_to_all(send_rows.reshape(devices, capacity, width), ('seq', 'stor...  30.2 us
    all_to_all x1, waiting for transfers between devices, local(): lax.all_to_all(delta.reshape(got_rows.shape), ('seq', 'store'), split_axi...  28.2 us
    all_to_all x1, waiting for transfers between devices, local(): lax.all_to_all(q_send, 'seq', split_axis=1, concat_axis=0, tiled=True)  16.8 us
    dot_general x8, matrix products, one_block(): jnp.einsum('hqn,nd->qhd', expo.astype(jnp.bfloat16), value_rows, preferre...  16.1 us
    all_to_all x1, waiting for transfers between devices, local(): lax.all_to_all(context.reshape(length, 1, heads_here * HEAD_DIM), 'seq',...  14.8 us
    dot_general x1, matrix products, local(): jnp.dot(low, adapter_up, preferred_element_type=jnp.float32)  10.9 us
  transfers between devices with their start and end apart: 6, of which 5 were waited for; matrix products, arithmetic and copies ran while one was open for 5% of the time, Pallas kernels for 0%

commit v1 on v0

--- a/solution.py
+++ b/solution.py
@@ -8,6 +8,7 @@
 KV_HEADS = 4
 RANK = 64
 EXP_DEV = 16
+MAX_DOC = 2048
 
 
 def attend(queries, key_rows, value_rows, segments):
@@ -15,28 +16,40 @@
     block = min(512, length)
     scale = queries.shape[2] ** (-0.5)
     key_pos = jnp.arange(length, dtype=jnp.int32)
+    n_blocks = length // block
+    reach = min(n_blocks, (MAX_DOC + block - 1) // block + 1)
 
-    def one_block(index):
-        start = index * block
+    def one_block(start, k_lo, width):
         q_block = lax.dynamic_slice_in_dim(queries, start, block, 0)
         seg_block = lax.dynamic_slice_in_dim(segments, start, block, 0)
+        k_rows = lax.dynamic_slice_in_dim(key_rows, k_lo, width, 0)
+        v_rows = lax.dynamic_slice_in_dim(value_rows, k_lo, width, 0)
+        k_seg = lax.dynamic_slice_in_dim(segments, k_lo, width, 0)
+        k_pos = k_lo + jnp.arange(width, dtype=jnp.int32)
         scores = (
-            jnp.einsum("qhd,nd->hqn", q_block, key_rows, preferred_element_type=jnp.float32) * scale
+            jnp.einsum("qhd,nd->hqn", q_block, k_rows, preferred_element_type=jnp.float32) * scale
         )
         q_pos = start + jnp.arange(block, dtype=jnp.int32)
-        allowed = (key_pos[None, :] <= q_pos[:, None]) & (segments[None, :] == seg_block[:, None])
+        allowed = (k_pos[None, :] <= q_pos[:, None]) & (k_seg[None, :] == seg_block[:, None])
         scores = jnp.where(allowed[None], scores, jnp.float32(-1e30))
         top = jnp.max(scores, axis=-1, keepdims=True)
         expo = jnp.exp(scores - top)
         total = jnp.sum(expo, axis=-1)
         summed = jnp.einsum(
-            "hqn,nd->qhd", expo.astype(jnp.bfloat16), value_rows, preferred_element_type=jnp.float32
+            "hqn,nd->qhd", expo.astype(jnp.bfloat16), v_rows, preferred_element_type=jnp.float32
         )
         out = summed / jnp.transpose(total)[:, :, None]
         return out.astype(jnp.bfloat16).reshape(block, -1)
 
-    blocks = lax.map(one_block, jnp.arange(length // block, dtype=jnp.int32))
-    return blocks.reshape(length, -1)
+    outs = [one_block(i * block, 0, (i + 1) * block) for i in range(min(reach - 1, n_blocks))]
+    if n_blocks >= reach:
+        width = reach * block
+        rest = lax.map(
+            lambda i: one_block(i * block, (i + 1) * block - width, width),
+            jnp.arange(reach - 1, n_blocks, dtype=jnp.int32),
+        )
+        outs.append(rest.reshape((n_blocks - reach + 1) * block, -1))
+    return jnp.concatenate(outs, axis=0)
 
 
 def local(queries, keys, values, segment_ids, route_ids, adapter_down, adapter_up):
@@ -56,7 +69,10 @@
         lax.all_to_all(q_send, "seq", split_axis=1, concat_axis=0, tiled=True),
         lax.all_to_all(kv_send, "seq", split_axis=1, concat_axis=0, tiled=True),
     )
-    segments = lax.all_gather(segment_ids, "seq", axis=1, tiled=True)[0]
+    seg_send = jnp.broadcast_to(segment_ids, (n_seq, tok_rows))
+    segments = lax.all_to_all(seg_send, "seq", split_axis=0, concat_axis=0, tiled=True).reshape(
+        length
+    )
     context = attend(q_all, kv_all[:, 0, :HEAD_DIM], kv_all[:, 0, HEAD_DIM:], segments)
     returned_ctx = lax.all_to_all(
         context.reshape(length, 1, heads_here * HEAD_DIM),

time: 289 us -> 263 us (0.910)
  blocking collectives: 41.3 us -> 0 us
  waiting for transfers between devices: 90.3 us -> 115 us
  matrix products: 57.4 us -> 37 us
  local copies, waits for them, and re-layouts: 36.2 us -> 48.9 us
  other arithmetic: 16.6 us -> 12.1 us
  starting transfers between devices: 39.9 us -> 43.4 us
    all_gather x1 -> x0, blocking collectives: 41.3 us -> none  [local(): segments = lax.all_gather(segment_ids, 'seq', axis=1, tiled=True)[0]]
    dot_general x16, matrix products: 46.5 us -> 26.1 us  [the longest x8 18.9 us: one_block(): jnp.einsum('qhd,nd->hqn', q_block, k_rows, preferred_element_type=jnp.flo...]
    all_to_all x1, waiting for transfers between devices: 0.01 us -> 19.4 us  [local(): lax.all_to_all(kv_send, 'seq', split_axis=1, concat_axis=0, tiled=True)]
    all_to_all x0 -> x1, starting transfers between devices: none -> 9.42 us  [local(): lax.all_to_all(seg_send, 'seq', split_axis=0, concat_axis=0, tiled=True)]
    reduce_sum x8, other arithmetic: 10.3 us -> 4.77 us  [one_block(): total = jnp.sum(expo, axis=-1)]
    all_to_all x1, starting transfers between devices: 9.42 us -> 4.23 us  [local(): lax.all_to_all(q_send, 'seq', split_axis=1, concat_axis=0, tiled=True)]
    dynamic_slice x8 -> x18, local copies, waits for them, and re-layouts: 5.28 us -> 10.2 us  [the longest x4 5.24 us: attend(): lax.map(lambda i: one_block(i * block, (i + 1) * block - width, width), j...]
    all_to_all x0 -> x1, waiting for transfers between devices: none -> 4.64 us  [local(): lax.all_to_all(seg_send, 'seq', split_axis=0, concat_axis=0, tiled=True)]
  transfers between devices with their start and end apart: 6 -> 7, of which waited for: 5 -> 7; matrix products, arithmetic and copies ran while one was open for 5% -> 9% of each run, Pallas kernels for 0% -> 0%
where the time goes in v1:
time: 263 us; the launch traced here: 262 us
  waiting for transfers between devices  115 us (44%)
  local copies, waits for them, and re-layouts  48.9 us (19%)
  starting transfers between devices  43.4 us (17%)
  matrix products  37 us (14%)
  other arithmetic  12.1 us (5%)
  loops' own time  5.71 us (2%)
    all_to_all x1, waiting for transfers between devices, local(): lax.all_to_all(send_rows.reshape(devices, capacity, width), ('seq', 'stor...  30.2 us
    all_to_all x1, waiting for transfers between devices, local(): lax.all_to_all(delta.reshape(got_rows.shape), ('seq', 'store'), split_axi...  28.2 us
    all_to_all x1, waiting for transfers between devices, local(): lax.all_to_all(kv_send, 'seq', split_axis=1, concat_axis=0, tiled=True)  19.4 us
    dot_general x8, matrix products, one_block(): jnp.einsum('qhd,nd->hqn', q_block, k_rows, preferred_element_type=jnp.flo...  18.9 us
    all_to_all x1, waiting for transfers between devices, local(): lax.all_to_all(q_send, 'seq', split_axis=1, concat_axis=0, tiled=True)  16.9 us
    all_to_all x1, waiting for transfers between devices, local(): lax.all_to_all(context.reshape(length, 1, heads_here * HEAD_DIM), 'seq',...  14.9 us
    dot_general x1, matrix products, local(): jnp.dot(low, adapter_up, preferred_element_type=jnp.float32)  10.9 us
    all_to_all x1, starting transfers between devices, local(): lax.all_to_all(seg_send, 'seq', split_axis=0, concat_axis=0, tiled=True)  9.42 us
  transfers between devices with their start and end apart: 7, of which 7 were waited for; matrix products, arithmetic and copies ran while one was open for 9% of the time, Pallas kernels for 0%

profile of v1, /device:TPU:1, one launch (start us, length us, event | category | flops | bytes accessed | tf_op | source)
XLA Modules:
  0.0 262.1 jit_solution(5756609164957032231)
XLA Ops:
  1.3 9.4 %all-to-all-start.1 = ((s32[32,1,128]{2,1,0:T(1,128)}), s32[32,1,128]{2,1,0:T(1,128)S(1)}, u32[]{:S(2)}, u32[]{:S(2)}) async-start(s32[32,1,128]{2,1,0:T(1,128)} %broadcast_in_dim.56), calls=%async_computation.1 | async-start | bytes 32768 | tf_op jit(solution)/shard_map/all_to_all | solution.py:73
  10.7 2.3 copy.47
  13.0 4.6 %all-to-all-done.1 = s32[32,1,128]{2,1,0:T(1,128)S(1)} async-done(((s32[32,1,128]{2,1,0:T(1,128)}), s32[32,1,128]{2,1,0:T(1,128)S(1)}, u32[]{:S(2)}, u32[]{:S(2)}) %all-to-all-start.1) | async-done | bytes 16416 | tf_op jit(solution)/shard_map/all_to_all | solution.py:73
  17.7 4.2 %all-to-all-start.2 = ((bf16[128,32,128]{0,2,1:T(8,128)(2,1)}), bf16[128,32,128]{0,2,1:T(8,128)(2,1)S(1)}, u32[]{:S(2)}, u32[]{:S(2)}) async-start(bf16[128,32,128]{0,2,1:T(8,128)(2,1)} %bitcast.20), calls=%async_computation.2 | async-start | bytes 2097152 | tf_op jit(solution)/shard_map/all_to_all | solution.py:69
  22.2 16.9 %all-to-all-done.2 = bf16[128,32,128]{0,2,1:T(8,128)(2,1)S(1)} async-done(((bf16[128,32,128]{0,2,1:T(8,128)(2,1)}), bf16[128,32,128]{0,2,1:T(8,128)(2,1)S(1)}, u32[]{:S(2)}, u32[]{:S(2)}) %all-to-all-start.2) | async-done | bytes 1048608 | tf_op jit(solution)/shard_map/all_to_all | solution.py:69
  39.1 1.6 broadcast_in_dim.55
  40.6 4.1 %all-to-all-start = ((bf16[128,32,256]{2,0,1:T(8,128)(2,1)}), bf16[128,32,256]{2,0,1:T(8,128)(2,1)S(1)}, u32[]{:S(2)}, u32[]{:S(2)}) async-start(bf16[128,32,256]{2,0,1:T(8,128)(2,1)} %bitcast.267), calls=%async_computation | async-start | bytes 4194304 | tf_op jit(solution)/shard_map/all_to_all | solution.py:70
  50.3 1.7 copy.49
  53.6 19.4 %all-to-all-done = bf16[128,32,256]{2,0,1:T(8,128)(2,1)S(1)} async-done(((bf16[128,32,256]{2,0,1:T(8,128)(2,1)}), bf16[128,32,256]{2,0,1:T(8,128)(2,1)S(1)}, u32[]{:S(2)}, u32[]{:S(2)}) %all-to-all-start) | async-done | bytes 2097184 | tf_op jit(solution)/shard_map/all_to_all | solution.py:70
  80.0 1.5 fusion.106
  82.8 2.0 fusion.107
  86.5 35.5 %while.14 = (s32[]{:T(128)}, bf16[4,512,128]{2,1,0:T(8,128)(2,1)}, s32[4]{0:T(128)}, bf16[4096,128]{1,0:T(8,128)(2,1)S(1)}, s32[4096]{0:T(1024)S(1)}, /*index=5*...) while((s32[]{:T(128)}, bf16[4,512,128]{2,1,0:T(8,128)(2,1)}, ...), condition=%wide.region_11.12_spmd, body=%wide.region_8.11_spmd.sunk | while | flops 684328960 | bytes 17898272 | solution.py:47
  89.4 3.4 %fusion.122 = (f32[512]{0:T(512)S(1)}, f32[1,512,2560]{1,2,0:T(8,128)S(1)}) fusion(bf16[4096,1,128]{2,0,1:T(8,128)(2,1)} %get-tuple-element.264, s32[]{:T(128)S(6)} %select_n.131, bf16[4096,128]{1,0:T(8,128)(2,1)} %get-tuple-element.263, s32[]{:T(128)S(6)} %select_n.132, s32[512]{0:T(512)S(1)} %dynamic_slice.230, s32[2560]{0:T(1024)S(1)} %dynamic_slice.231, ...), kind=kOutput, calls=%fused_computation.139.clone.1 | convolution fusion | flops 343408128 | bytes 6055944 | tf_op jit(solution)/shard_map/while/body/eval_jaxpr/qhd,nd->hqn/dot_general | solution.py:30
  98.3 3.4 %fusion.122 = (f32[512]{0:T(512)S(1)}, f32[1,512,2560]{1,2,0:T(8,128)S(1)}) fusion(bf16[4096,1,128]{2,0,1:T(8,128)(2,1)} %get-tuple-element.264, s32[]{:T(128)S(6)} %select_n.131, bf16[4096,128]{1,0:T(8,128)(2,1)} %get-tuple-element.263, s32[]{:T(128)S(6)} %select_n.132, s32[512]{0:T(512)S(1)} %dynamic_slice.230, s32[2560]{0:T(1024)S(1)} %dynamic_slice.231, ...), kind=kOutput, calls=%fused_computation.139.clone.1 | convolution fusion | flops 343408128 | bytes 6055944 | tf_op jit(solution)/shard_map/while/body/eval_jaxpr/qhd,nd->hqn/dot_general | solution.py:30
  107.1 3.4 %fusion.122 = (f32[512]{0:T(512)S(1)}, f32[1,512,2560]{1,2,0:T(8,128)S(1)}) fusion(bf16[4096,1,128]{2,0,1:T(8,128)(2,1)} %get-tuple-element.264, s32[]{:T(128)S(6)} %select_n.131, bf16[4096,128]{1,0:T(8,128)(2,1)} %get-tuple-element.263, s32[]{:T(128)S(6)} %select_n.132, s32[512]{0:T(512)S(1)} %dynamic_slice.230, s32[2560]{0:T(1024)S(1)} %dynamic_slice.231, ...), kind=kOutput, calls=%fused_computation.139.clone.1 | convolution fusion | flops 343408128 | bytes 6055944 | tf_op jit(solution)/shard_map/while/body/eval_jaxpr/qhd,nd->hqn/dot_general | solution.py:30
  116.0 3.4 %fusion.122 = (f32[512]{0:T(512)S(1)}, f32[1,512,2560]{1,2,0:T(8,128)S(1)}) fusion(bf16[4096,1,128]{2,0,1:T(8,128)(2,1)} %get-tuple-element.264, s32[]{:T(128)S(6)} %select_n.131, bf16[4096,128]{1,0:T(8,128)(2,1)} %get-tuple-element.263, s32[]{:T(128)S(6)} %select_n.132, s32[512]{0:T(512)S(1)} %dynamic_slice.230, s32[2560]{0:T(1024)S(1)} %dynamic_slice.231, ...), kind=kOutput, calls=%fused_computation.139.clone.1 | convolution fusion | flops 343408128 | bytes 6055944 | tf_op jit(solution)/shard_map/while/body/eval_jaxpr/qhd,nd->hqn/dot_general | solution.py:30
  123.7 1.4 reduce.28
  126.2 5.7 %all-to-all-start.3 = ((bf16[32,2,8192]{2,1,0:T(2,128)(2,1)}), bf16[32,2,8192]{2,1,0:T(2,128)(2,1)S(1)}, u32[]{:S(2)}, u32[]{:S(2)}) async-start(bf16[32,2,8192]{2,1,0:T(2,128)(2,1)} %reshape.914), calls=%async_computation.3 | async-start | bytes 2097152 | tf_op jit(solution)/shard_map/all_to_all | solution.py:77
  134.2 14.9 %all-to-all-done.3 = bf16[32,2,8192]{2,1,0:T(2,128)(2,1)S(1)} async-done(((bf16[32,2,8192]{2,1,0:T(2,128)(2,1)}), bf16[32,2,8192]{2,1,0:T(2,128)(2,1)S(1)}, u32[]{:S(2)}, u32[]{:S(2)}) %all-to-all-start.3) | async-done | bytes 1048608 | tf_op jit(solution)/shard_map/all_to_all | solution.py:77
  149.1 5.8 %all-to-all-start.4 = ((bf16[128,1,2]{2,1,0:T(2,128)(2,1)}), bf16[128,1,2]{2,1,0:T(2,128)(2,1)S(1)}, u32[]{:S(2)}, u32[]{:S(2)}) async-start(bf16[128,1,2]{2,1,0:T(2,128)(2,1)} %all_to_all.69), calls=%async_computation.4 | async-start | bytes 131072 | tf_op jit(solution)/shard_map/all_to_all | solution.py:110
  158.1 3.4 %scatter_custom_fusion.1 = bf16[256,4096]{1,0:T(8,128)(2,1)S(1)} fusion(s32[128]{0:T(128)S(1)} %fusion.97, bf16[128,4096]{1,0:T(8,128)(2,1)} %copy.62, bf16[]{:T(256)} %constant.155.clone.1), kind=kCustom, calls=%fused_computation.76 | custom fusion | bytes 2097664 | tf_op jit(solution)/shard_map/scatter | solution.py:92
  161.6 2.7 %reshape.871 = bf16[128,2,4096]{2,1,0:T(2,128)(2,1)} reshape(bf16[256,4096]{1,0:T(8,128)(2,1)S(1)} %scatter_custom_fusion.1) | data formatting | bytes 4194304 | tf_op jit(solution)/shard_map/reshape | solution.py:100
  164.6 9.4 %all-to-all-start.5 = ((bf16[128,2,4096]{2,1,0:T(2,128)(2,1)}), bf16[128,2,4096]{2,1,0:T(2,128)(2,1)S(1)}, u32[]{:S(2)}, u32[]{:S(2)}) async-start(bf16[128,2,4096]{2,1,0:T(2,128)(2,1)} %reshape.871), calls=%async_computation.5 | async-start | bytes 4194304 | tf_op jit(solution)/shard_map/all_to_all | solution.py:99
  174.3 30.2 %all-to-all-done.5 = bf16[128,2,4096]{2,1,0:T(2,128)(2,1)S(1)} async-done(((bf16[128,2,4096]{2,1,0:T(2,128)(2,1)}), bf16[128,2,4096]{2,1,0:T(2,128)(2,1)S(1)}, u32[]{:S(2)}, u32[]{:S(2)}) %all-to-all-start.5) | async-done | bytes 2097184 | tf_op jit(solution)/shard_map/all_to_all | solution.py:99
  204.5 2.2 reshape.872
  206.8 10.9 %convolution_convert_fusion = bf16[256,4096]{1,0:T(8,128)(2,1)S(1)} fusion(bf16[1024,4096]{1,0:T(8,128)(2,1)} %param.15, bf16[256,4096]{1,0:T(8,128)(2,1)} %reshape.872, bf16[4096,1024]{1,0:T(8,128)(2,1)} %param.14, f32[1024]{0:T(1024)S(1)} %fusion.92, f32[256]{0:T(256)S(1)} %reshape.876), kind=kOutput, calls=%fused_computation.23 | convolution fusion | flops 4296802304 | bytes 20976640 | tf_op jit(solution)/shard_map/dot_general | solution.py:122
  217.6 2.7 %reshape.873 = bf16[128,2,4096]{2,1,0:T(2,128)(2,1)} reshape(bf16[256,4096]{1,0:T(8,128)(2,1)S(1)} %convolution_convert_fusion) | data formatting | bytes 4194304 | tf_op jit(solution)/shard_map/reshape | solution.py:124
  220.3 4.7 %all-to-all-start.6 = ((bf16[128,2,4096]{2,1,0:T(2,128)(2,1)}), bf16[128,2,4096]{2,1,0:T(2,128)(2,1)}, u32[]{:S(2)}, u32[]{:S(2)}) async-start(bf16[128,2,4096]{2,1,0:T(2,128)(2,1)} %reshape.873), calls=%async_computation.6 | async-start | bytes 4194304 | tf_op jit(solution)/shard_map/all_to_all | solution.py:123
  225.7 1.5 reshape.875
  227.2 28.2 %all-to-all-done.6 = bf16[128,2,4096]{2,1,0:T(2,128)(2,1)} async-done(((bf16[128,2,4096]{2,1,0:T(2,128)(2,1)}), bf16[128,2,4096]{2,1,0:T(2,128)(2,1)}, u32[]{:S(2)}, u32[]{:S(2)}) %all-to-all-start.6) | async-done | bytes 2097184 | tf_op jit(solution)/shard_map/all_to_all | solution.py:123
  255.4 2.7 %reshape.874 = bf16[256,4096]{1,0:T(8,128)(2,1)S(1)} reshape(bf16[128,2,4096]{2,1,0:T(2,128)(2,1)} %all-to-all-done.6) | data formatting | bytes 4194304 | tf_op jit(solution)/shard_map/reshape | solution.py:126
  259.3 2.8 %fusion.35 = bf16[1,128,4096]{2,1,0:T(8,128)(2,1)} fusion(f32[1,128,4096]{2,1,0:T(8,128)} %reshape.875, bf16[128,4096]{1,0:T(8,128)(2,1)S(1)} %gather_fusion), kind=kLoop, calls=%fused_computation.41 | loop fusion | flops 1572864 | bytes 4194304 | tf_op jit(solution)/shard_map/convert_element_type | solution.py:127
  (120 shorter events, 45.5 us)
Async XLA Ops:
  1.3 16.4 %all-to-all-start.1 = ((s32[32,1,128]{2,1,0:T(1,128)}), s32[32,1,128]{2,1,0:T(1,128)S(1)}, u32[]{:S(2)}, u32[]{:S(2)}) async-start(s32[32,1,128]{2,1,0:T(1,128)} %broadcast_in_dim.56), calls=%async_computation.1 | async-start | bytes 32768 | tf_op jit(solution)/shard_map/all_to_all | solution.py:73
  10.7 11.2 %copy-start.3 = (bf16[1,128,512]{2,1,0:T(8,128)(2,1)S(1)}, bf16[1,128,512]{2,1,0:T(8,128)(2,1)}, u32[]{:S(2)}) copy-start(bf16[1,128,512]{2,1,0:T(8,128)(2,1)} %param.10) | copy-start | bytes 393220
  10.7 11.2 %copy-start.4 = (bf16[1,128,512]{2,1,0:T(8,128)(2,1)S(1)}, bf16[1,128,512]{2,1,0:T(8,128)(2,1)}, u32[]{:S(2)}) copy-start(bf16[1,128,512]{2,1,0:T(8,128)(2,1)} %param.11) | copy-start | bytes 393220
  17.7 30.0 %copy-start.1 = (s32[32,1,128]{2,1,0:T(1,128)}, s32[32,1,128]{2,1,0:T(1,128)S(1)}, u32[]{:S(2)}) copy-start(s32[32,1,128]{2,1,0:T(1,128)S(1)} %all-to-all-done.1) | copy-start | bytes 49156
  17.7 21.4 %all-to-all-start.2 = ((bf16[128,32,128]{0,2,1:T(8,128)(2,1)}), bf16[128,32,128]{0,2,1:T(8,128)(2,1)S(1)}, u32[]{:S(2)}, u32[]{:S(2)}) async-start(bf16[128,32,128]{0,2,1:T(8,128)(2,1)} %bitcast.20), calls=%async_computation.2 | async-start | bytes 2097152 | tf_op jit(solution)/shard_map/all_to_all | solution.py:69
  40.6 32.4 %all-to-all-start = ((bf16[128,32,256]{2,0,1:T(8,128)(2,1)}), bf16[128,32,256]{2,0,1:T(8,128)(2,1)S(1)}, u32[]{:S(2)}, u32[]{:S(2)}) async-start(bf16[128,32,256]{2,0,1:T(8,128)(2,1)} %bitcast.267), calls=%async_computation | async-start | bytes 4194304 | tf_op jit(solution)/shard_map/all_to_all | solution.py:70
  73.0 1.1 slice-start
  73.0 1.1 copy-start.5
  73.0 1.1 copy-start.7
  73.0 1.1 copy-start.9
  74.8 1.0 copy-start.8
  75.8 4.1 %copy-start.6 = (s32[12,128]{1,0:T(8,128)S(1)}, s32[12,128]{1,0:T(8,128)}, u32[]{:S(2)}) copy-start(s32[12,128]{1,0:T(8,128)} %slice_reduce_fusion) | copy-start | bytes 18436
  82.0 0.8 slice-start.1
  85.4 1.0 copy-start.2
  86.5 35.5 %copy-start = (bf16[4096,128]{1,0:T(8,128)(2,1)S(1)}, bf16[4096,128]{1,0:T(8,128)(2,1)}, u32[]{:S(2)}) copy-start(bf16[4096,128]{1,0:T(8,128)(2,1)} %constant_dynamic-update-slice_fusion.5) | copy-start | bytes 3145732
  125.1 6.9 %copy-start.10 = (s32[1,128]{1,0:T(1,128)S(1)}, s32[1,128]{1,0:T(1,128)}, u32[]{:S(2)}) copy-start(s32[1,128]{1,0:T(1,128)} %param.13) | copy-start | bytes 1540
  126.2 22.9 %all-to-all-start.3 = ((bf16[32,2,8192]{2,1,0:T(2,128)(2,1)}), bf16[32,2,8192]{2,1,0:T(2,128)(2,1)S(1)}, u32[]{:S(2)}, u32[]{:S(2)}) async-start(bf16[32,2,8192]{2,1,0:T(2,128)(2,1)} %reshape.914), calls=%async_computation.3 | async-start | bytes 2097152 | tf_op jit(solution)/shard_map/all_to_all | solution.py:77
  149.1 15.5 %all-to-all-start.4 = ((bf16[128,1,2]{2,1,0:T(2,128)(2,1)}), bf16[128,1,2]{2,1,0:T(2,128)(2,1)S(1)}, u32[]{:S(2)}, u32[]{:S(2)}) async-start(bf16[128,1,2]{2,1,0:T(2,128)(2,1)} %all_to_all.69), calls=%async_computation.4 | async-start | bytes 131072 | tf_op jit(solution)/shard_map/all_to_all | solution.py:110
  164.6 40.0 %all-to-all-start.5 = ((bf16[128,2,4096]{2,1,0:T(2,128)(2,1)}), bf16[128,2,4096]{2,1,0:T(2,128)(2,1)S(1)}, u32[]{:S(2)}, u32[]{:S(2)}) async-start(bf16[128,2,4096]{2,1,0:T(2,128)(2,1)} %reshape.871), calls=%async_computation.5 | async-start | bytes 4194304 | tf_op jit(solution)/shard_map/all_to_all | solution.py:99
  220.3 35.1 %all-to-all-start.6 = ((bf16[128,2,4096]{2,1,0:T(2,128)(2,1)}), bf16[128,2,4096]{2,1,0:T(2,128)(2,1)}, u32[]{:S(2)}, u32[]{:S(2)}) async-start(bf16[128,2,4096]{2,1,0:T(2,128)(2,1)} %reshape.873), calls=%async_computation.6 | async-start | bytes 4194304 | tf_op jit(solution)/shard_map/all_to_all | solution.py:123

commit v2 on v1

v2 whole, which is shorter than its diff:
```python
import jax
import jax.numpy as jnp
from jax import lax
from jax.sharding import PartitionSpec as P

HEAD_DIM = 128
HEADS = 32
KV_HEADS = 4
RANK = 64
EXP_DEV = 16
MAX_DOC = 2048


def attend(queries, key_rows, value_rows, segments):
    length = queries.shape[0]
    block = min(512, length)
    scale = queries.shape[2] ** (-0.5)
    key_pos = jnp.arange(length, dtype=jnp.int32)
    n_blocks = length // block
    reach = min(n_blocks, (MAX_DOC + block - 1) // block + 1)

    def one_block(start, k_lo, width):
        q_block = lax.dynamic_slice_in_dim(queries, start, block, 0)
        seg_block = lax.dynamic_slice_in_dim(segments, start, block, 0)
        k_rows = lax.dynamic_slice_in_dim(key_rows, k_lo, width, 0)
        v_rows = lax.dynamic_slice_in_dim(value_rows, k_lo, width, 0)
        k_seg = lax.dynamic_slice_in_dim(segments, k_lo, width, 0)
        k_pos = k_lo + jnp.arange(width, dtype=jnp.int32)
        scores = (
            jnp.einsum("qhd,nd->hqn", q_block, k_rows, preferred_element_type=jnp.float32) * scale
        )
        q_pos = start + jnp.arange(block, dtype=jnp.int32)
        allowed = (k_pos[None, :] <= q_pos[:, None]) & (k_seg[None, :] == seg_block[:, None])
        scores = jnp.where(allowed[None], scores, jnp.float32(-1e30))
        top = jnp.max(scores, axis=-1, keepdims=True)
        expo = jnp.exp(scores - top)
        total = jnp.sum(expo, axis=-1)
        summed = jnp.einsum(
            "hqn,nd->qhd", expo.astype(jnp.bfloat16), v_rows, preferred_element_type=jnp.float32
        )
        out = summed / jnp.transpose(total)[:, :, None]
        return out.astype(jnp.bfloat16).reshape(block, -1)

    outs = [one_block(i * block, 0, (i + 1) * block) for i in range(min(reach - 1, n_blocks))]
    if n_blocks >= reach:
        width = reach * block
        rest = lax.map(
            lambda i: one_block(i * block, (i + 1) * block - width, width),
            jnp.arange(reach - 1, n_blocks, dtype=jnp.int32),
        )
        outs.append(rest.reshape((n_blocks - reach + 1) * block, -1))
    return jnp.concatenate(outs, axis=0)


def local(queries, keys, values, segment_ids, route_ids, adapter_down, adapter_up):
    n_seq = lax.axis_size("seq")
    n_store = lax.axis_size("store")
    tok_rows = queries.shape[1]
    width = queries.shape[2]
    length = tok_rows * n_seq
    heads_here = HEADS // n_seq
    feat = heads_here * HEAD_DIM
    group = HEADS // KV_HEADS
    devices = n_seq * n_store
    capacity = max(2, 2 * tok_rows // devices)
    slots = n_seq * capacity

    q_send = queries[0].reshape(tok_rows, n_seq, feat)
    paired = jnp.concatenate(
        [keys[0].reshape(tok_rows, KV_HEADS, HEAD_DIM), values[0].reshape(tok_rows, KV_HEADS, HEAD_DIM)],
        axis=2,
    )
    kv_send = jnp.take(paired, (jnp.arange(n_seq) * heads_here) // group, axis=1)
    chosen = route_ids[0]
    meta = jnp.concatenate(
        [segment_ids[0], chosen // EXP_DEV, chosen % EXP_DEV]
    ).astype(jnp.bfloat16)
    meta_w = feat + 2 * HEAD_DIM
    meta = jnp.pad(meta, (0, meta_w - meta.shape[0]))
    payload = jnp.concatenate(
        [
            jnp.concatenate([q_send, kv_send], axis=2),
            jnp.broadcast_to(meta[None, None, :], (1, n_seq, meta_w)),
        ],
        axis=0,
    )
    got_in = lax.all_to_all(payload, "seq", split_axis=1, concat_axis=0, tiled=True)
    got_in = got_in.reshape(n_seq, tok_rows + 1, meta_w)
    q_all = got_in[:, :tok_rows, :feat].reshape(length, heads_here, HEAD_DIM)
    k_all = got_in[:, :tok_rows, feat : feat + HEAD_DIM].reshape(length, HEAD_DIM)
    v_all = got_in[:, :tok_rows, feat + HEAD_DIM :].reshape(length, HEAD_DIM)
    meta_all = got_in[:, tok_rows, : 3 * tok_rows].astype(jnp.int32)
    segments = meta_all[:, :tok_rows].reshape(length)
    owner_all = meta_all[:, tok_rows : 2 * tok_rows]
    adapter_all = meta_all[:, 2 * tok_rows :].reshape(length)

    context = attend(q_all, k_all, v_all, segments).reshape(length, feat)

    def ranks(owner_rows):
        one_hot = (owner_rows[..., None] == jnp.arange(devices, dtype=jnp.int32)).astype(jnp.int32)
        return jnp.sum(jnp.cumsum(one_hot, axis=-2) * one_hot, axis=-1) - 1

    slot_all = (
        jnp.arange(n_seq, dtype=jnp.int32)[:, None] * capacity + ranks(owner_all)
    ).reshape(length)
    target = owner_all.reshape(length) * slots + slot_all
    pick = jnp.full((devices * slots,), length, jnp.int32).at[target].set(
        jnp.arange(length, dtype=jnp.int32)
    )
    tags = jnp.full((devices * slots,), -1, jnp.int32).at[target].set(adapter_all)
    ctx_ext = jnp.concatenate([context, jnp.zeros((1, feat), context.dtype)], axis=0)
    send = ctx_ext[pick].reshape(devices, slots, feat)
    tag_row = jnp.pad(tags.reshape(devices, slots).astype(jnp.bfloat16), ((0, 0), (0, feat - slots)))
    send = jnp.concatenate([send, tag_row[:, None, :]], axis=1)
    got = lax.all_to_all(send, ("seq", "store"), split_axis=0, concat_axis=0, tiled=True)
    got = got.reshape(n_seq, n_store, slots + 1, feat)
    rows = jnp.transpose(got[:, :, :slots, :], (1, 2, 0, 3)).reshape(n_store * slots, width)
    row_tags = got[0, :, slots, :slots].reshape(n_store * slots, 1).astype(jnp.float32)

    low = jnp.dot(rows, adapter_down, preferred_element_type=jnp.float32)
    lane_owner = (jnp.arange(low.shape[1], dtype=jnp.int32) // RANK).astype(jnp.float32)
    low = jnp.where(row_tags == lane_owner[None, :], low, 0.0).astype(jnp.bfloat16)
    delta = jnp.dot(low, adapter_up, preferred_element_type=jnp.float32).astype(jnp.bfloat16)
    mixed_rows = (rows.astype(jnp.float32) + delta.astype(jnp.float32)).astype(jnp.bfloat16)
    ret = jnp.transpose(
        mixed_rows.reshape(n_store, n_seq, capacity, width), (1, 0, 2, 3)
    ).reshape(devices, capacity, width)
    back = lax.all_to_all(ret, ("seq", "store"), split_axis=0, concat_axis=0, tiled=True)
    owners = chosen // EXP_DEV
    placed = owners * capacity + ranks(owners)
    mixed = back.reshape(devices * capacity, width)[placed]
    return mixed[None]


def solution(mesh):
    return jax.shard_map(
        local,
        mesh=mesh,
        in_specs=(
            P("store", "seq", None),
            P("store", "seq", None),
            P("store", "seq", None),
            P("store", "seq"),
            P("store", "seq"),
            P(None, ("seq", "store")),
            P(("seq", "store"), None),
        ),
        out_specs=P("store", "seq", None),
        check_vma=False,
    )
```

time: 263 us -> 281 us (1.068)
  local copies, waits for them, and re-layouts: 48.9 us -> 102 us
  starting transfers between devices: 43.4 us -> 21.6 us
  waiting for transfers between devices: 115 us -> 102 us
  matrix products: 37 us -> 30.4 us
  other arithmetic: 12.1 us -> 17.6 us
    scatter x2, local copies, waits for them, and re-layouts: 4.39 us -> 31.3 us  [the longest x1 15.7 us: local(): jnp.full((devices * slots,), -1, jnp.int32).at[target].set(adapter_all)]
    gather x1 -> x3, local copies, waits for them, and re-layouts: 1.19 us -> 26.9 us  [the longest x1 24 us: local(): send = ctx_ext[pick].reshape(devices, slots, feat)]
    all_to_all x7 -> x3, starting transfers between devices: 43.4 us -> 21.6 us  [the longest x1 9.42 us: local(): lax.all_to_all(payload, 'seq', split_axis=1, concat_axis=0, tiled=True)]
    all_to_all x7 -> x3, waiting for transfers between devices: 115 us -> 102 us  [the longest x1 39.3 us: local(): lax.all_to_all(payload, 'seq', split_axis=1, concat_axis=0, tiled=True)]
    dot_general x8, matrix products: 18.9 us -> 11.8 us  [one_block(): jnp.einsum('qhd,nd->hqn', q_block, k_rows, preferred_element_type=jnp.flo...]
    concatenate x1 -> x5, other arithmetic: 0.13 us -> 4.36 us  [the longest x1 1.96 us: local(): jnp.concatenate([jnp.concatenate([q_send, kv_send], axis=2), jnp.broadcas...]
    another operation x1 -> x3, other arithmetic: 0.17 us -> 4.17 us  [the longest x2 3.51 us: ranks(): return jnp.sum(jnp.cumsum(one_hot, axis=-2) * one_hot, axis=-1) - 1]
    dynamic_slice x5 -> x1, local copies, waits for them, and re-layouts: 4.01 us -> 0.91 us  [one_block(): q_block = lax.dynamic_slice_in_dim(queries, start, block, 0)]
  transfers between devices with their start and end apart: 7 -> 3, of which waited for: 7 -> 3; matrix products, arithmetic and copies ran while one was open for 9% -> 1% of each run, Pallas kernels for 0% -> 0%
where the time goes in v2:
time: 281 us; the launch traced here: 280 us
  local copies, waits for them, and re-layouts  102 us (36%)
  waiting for transfers between devices  102 us (36%)
  matrix products  30.4 us (11%)
  starting transfers between devices  21.6 us (8%)
  other arithmetic  17.6 us (6%)
  loops' own time  5.24 us (2%)
    all_to_all x1, waiting for transfers between devices, local(): lax.all_to_all(payload, 'seq', split_axis=1, concat_axis=0, tiled=True)  39.3 us
    all_to_all x1, waiting for transfers between devices, local(): lax.all_to_all(send, ('seq', 'store'), split_axis=0, concat_axis=0, tiled...  33.3 us
    all_to_all x1, waiting for transfers between devices, local(): lax.all_to_all(ret, ('seq', 'store'), split_axis=0, concat_axis=0, tiled=...  29.8 us
    gather x1, local copies, waits for them, and re-layouts, local(): send = ctx_ext[pick].reshape(devices, slots, feat)  24 us
    scatter x1, local copies, waits for them, and re-layouts, local(): jnp.full((devices * slots,), -1, jnp.int32).at[target].set(adapter_all)  15.7 us
    scatter x1, local copies, waits for them, and re-layouts, local(): jnp.full((devices * slots,), length, jnp.int32).at[target]  15.5 us
    dot_general x1, matrix products, local(): jnp.dot(low, adapter_up, preferred_element_type=jnp.float32)  12.2 us
    dot_general x8, matrix products, one_block(): jnp.einsum('qhd,nd->hqn', q_block, k_rows, preferred_element_type=jnp.flo...  11.8 us
  transfers between devices with their start and end apart: 3, of which 3 were waited for; matrix products, arithmetic and copies ran while one was open for 1% of the time, Pallas kernels for 0%

profile of v2, /device:TPU:1, one launch (start us, length us, event | category | flops | bytes accessed | tf_op | source)
XLA Modules:
  0.0 279.8 jit_solution(10323037537316509986)
XLA Ops:
  3.7 1.6 copy.41
  7.1 2.0 pad_maximum_fusion
  9.0 9.4 %all-to-all-start = ((bf16[129,32,384]{2,0,1:T(8,128)(2,1)}), bf16[129,32,384]{2,0,1:T(8,128)(2,1)S(1)}, u32[]{:S(2)}, u32[]{:S(2)}) async-start(bf16[129,32,384]{2,0,1:T(8,128)(2,1)} %pad_maximum_fusion), calls=%async_computation | async-start | bytes 6684672 | tf_op jit(solution)/shard_map/all_to_all | solution.py:87
  20.7 39.3 %all-to-all-done = bf16[129,32,384]{2,0,1:T(8,128)(2,1)S(1)} async-done(((bf16[129,32,384]{2,0,1:T(8,128)(2,1)}), bf16[129,32,384]{2,0,1:T(8,128)(2,1)S(1)}, u32[]{:S(2)}, u32[]{:S(2)}) %all-to-all-start) | async-done | bytes 3170336 | tf_op jit(solution)/shard_map/all_to_all | solution.py:87
  61.8 1.1 fusion.123
  64.4 2.3 fusion.120
  66.7 1.1 fusion.128
  76.3 3.3 %select_reduce_fusion = s32[32,128]{0,1:T(8,128)S(1)} fusion(s32[32,128]{0,1:T(8,128)S(1)} %copy.52), kind=kOutput, calls=%fused_computation.52 | output fusion | flops 69201920 | bytes 32768 | tf_op jit(solution)/shard_map/jit(cumsum)/reduce_window_sum | solution.py:101
  80.4 35.7 %while.14 = (s32[]{:T(128)}, bf16[4,512,128]{2,1,0:T(8,128)(2,1)}, s32[4]{0:T(128)}, bf16[4096,128]{1,0:T(8,128)(2,1)S(1)}, s32[4096]{0:T(1024)}, /*index=5*/bf1...) while((s32[]{:T(128)}, bf16[4,512,128]{2,1,0:T(8,128)(2,1)}, ...), condition=%wide.region_11.12_spmd, body=%wide.region_8.11_spmd.sunk | while | flops 684328960 | bytes 17902368 | solution.py:47
  80.4 1.3 dynamic_slice.215
  84.5 2.2 fusion.150
  89.3 1.3 dynamic_slice.215
  93.4 2.2 fusion.150
  98.2 1.3 dynamic_slice.215
  102.3 2.2 fusion.150
  107.2 1.3 dynamic_slice.215
  111.3 2.2 fusion.150
  118.0 1.1 constant_dynamic-update-slice_fusion.2
  119.8 15.5 %scatter_custom_fusion = s32[8192]{0:T(1024)S(1)} fusion(s32[4096]{0:T(1024)S(1)} %bitcast.304, s32[4096]{0:T(1024)S(1)} %iota.108, s32[]{:T(128)} %constant.207.clone.1), kind=kCustom, calls=%fused_computation.115 | custom fusion | bytes 32772 | tf_op jit(solution)/shard_map/scatter | solution.py:107
  135.4 15.7 %scatter_custom_fusion.1 = s32[8192]{0:T(1024)S(1)} fusion(s32[4096]{0:T(1024)S(1)} %bitcast.305, s32[4096]{0:T(1024)} %get-tuple-element.182, s32[]{:T(128)} %constant.194.clone.1), kind=kCustom, calls=%fused_computation.112 | custom fusion | bytes 33280 | tf_op jit(solution)/shard_map/scatter | solution.py:110
  151.3 24.0 %gather_fusion.1 = bf16[8192,128]{1,0:T(8,128)(2,1)S(1)} fusion(bf16[4097,128]{1,0:T(8,128)(2,1)S(1)} %constant_dynamic-update-slice_fusion.1, s32[8192]{0:T(1024)S(1)} %fusion.105), kind=kCustom, calls=%fused_computation.1 | custom fusion | bytes 4227072 | tf_op jit(solution)/shard_map/gather | solution.py:112
  175.4 1.7 pad_maximum_fusion.1
  177.0 7.4 %all-to-all-start.1 = ((bf16[128,65,128]{2,1,0:T(8,128)(2,1)}), bf16[128,65,128]{2,1,0:T(8,128)(2,1)S(1)}, u32[]{:S(2)}, u32[]{:S(2)}) async-start(bf16[128,65,128]{2,1,0:T(8,128)(2,1)} %pad_maximum_fusion.1), calls=%async_computation.1 | async-start | bytes 4718592 | tf_op jit(solution)/shard_map/all_to_all | solution.py:115
  184.4 33.3 %all-to-all-done.1 = bf16[128,65,128]{2,1,0:T(8,128)(2,1)S(1)} async-done(((bf16[128,65,128]{2,1,0:T(8,128)(2,1)}), bf16[128,65,128]{2,1,0:T(8,128)(2,1)S(1)}, u32[]{:S(2)}, u32[]{:S(2)}) %all-to-all-start.1) | async-done | bytes 2129952 | tf_op jit(solution)/shard_map/all_to_all | solution.py:115
  218.3 1.6 slice_bitcast_fusion
  220.3 12.2 %fusion.26 = bf16[256,4096]{1,0:T(8,128)(2,1)} fusion(bf16[1024,4096]{1,0:T(8,128)(2,1)} %param.15, bf16[32,8,32,128]{3,2,1,0:T(8,128)(2,1)S(1)} %bitcast.279, bf16[4096,1024]{1,0:T(8,128)(2,1)} %param.14, f32[1024]{0:T(1024)S(1)} %fusion.110, f32[256]{0:T(256)S(1)} %reshape.961), kind=kOutput, calls=%fused_computation.28 | convolution fusion | flops 4300996608 | bytes 20976640 | tf_op jit(solution)/shard_map/dot_general | solution.py:123
  232.5 3.2 %reshape.957 = bf16[4,32,2,4096]{3,2,1,0:T(2,128)(2,1)S(1)} reshape(bf16[256,4096]{1,0:T(8,128)(2,1)} %fusion.26) | data formatting | bytes 4194304 | tf_op jit(solution)/shard_map/reshape | solution.py:126
  235.6 4.1 %copy.57 = bf16[4,32,2,4096]{3,2,0,1:T(2,128)(2,1)} copy(bf16[4,32,2,4096]{3,2,1,0:T(2,128)(2,1)S(1)} %reshape.957) | data formatting | bytes 4194304 | tf_op jit(solution)/shard_map/reshape | solution.py:126
  239.7 4.8 %all-to-all-start.2 = ((bf16[128,2,4096]{2,1,0:T(2,128)(2,1)}), bf16[128,2,4096]{2,1,0:T(2,128)(2,1)}, u32[]{:S(2)}, u32[]{:S(2)}) async-start(bf16[128,2,4096]{2,1,0:T(2,128)(2,1)} %bitcast.78), calls=%async_computation.2 | async-start | bytes 4194304 | tf_op jit(solution)/shard_map/all_to_all | solution.py:128
  245.0 29.8 %all-to-all-done.2 = bf16[128,2,4096]{2,1,0:T(2,128)(2,1)} async-done(((bf16[128,2,4096]{2,1,0:T(2,128)(2,1)}), bf16[128,2,4096]{2,1,0:T(2,128)(2,1)}, u32[]{:S(2)}, u32[]{:S(2)}) %all-to-all-start.2) | async-done | bytes 2097184 | tf_op jit(solution)/shard_map/all_to_all | solution.py:128
  274.9 2.7 reshape.959
  277.6 2.2 gather_fusion.2
  (141 shorter events, 40.7 us)
Async XLA Ops:
  9.0 50.9 %all-to-all-start = ((bf16[129,32,384]{2,0,1:T(8,128)(2,1)}), bf16[129,32,384]{2,0,1:T(8,128)(2,1)S(1)}, u32[]{:S(2)}, u32[]{:S(2)}) async-start(bf16[129,32,384]{2,0,1:T(8,128)(2,1)} %pad_maximum_fusion), calls=%async_computation | async-start | bytes 6684672 | tf_op jit(solution)/shard_map/all_to_all | solution.py:87
  68.4 1.0 copy-start.4
  68.4 1.0 copy-start.10
  68.4 1.0 copy-start.13
  68.5 1.0 copy-start.16
  70.3 1.0 copy-start.1
  70.8 1.9 copy-start.5
  70.9 1.9 copy-start.9
  70.9 1.9 copy-start.11
  70.9 1.9 copy-start.12
  70.9 1.9 copy-start.15
  72.8 1.0 copy-start.2
  73.4 1.7 copy-start.7
  73.5 1.7 copy-start.8
  73.5 1.7 copy-start.14
  73.8 1.9 copy-start.6
  75.1 4.6 %copy-start.17 = (s32[32]{0:T(128)S(1)}, s32[32]{0:T(128)}, u32[]{:S(2)}) copy-start(s32[32]{0:T(128)} %iota_multiply_fusion) | copy-start | bytes 388
  75.1 5.3 %copy-start = (bf16[32,128,128]{2,1,0:T(8,128)(2,1)S(1)}, bf16[32,128,128]{2,1,0:T(8,128)(2,1)}, u32[]{:S(2)}) copy-start(bf16[32,128,128]{2,1,0:T(8,128)(2,1)} %get-tuple-element.167) | copy-start | bytes 3145732
  75.1 5.3 %copy-start.3 = (bf16[32,128,128]{2,1,0:T(8,128)(2,1)S(1)}, bf16[32,128,128]{2,1,0:T(8,128)(2,1)}, u32[]{:S(2)}) copy-start(bf16[32,128,128]{2,1,0:T(8,128)(2,1)} %get-tuple-element.166) | copy-start | bytes 3145732
  177.0 40.7 %all-to-all-start.1 = ((bf16[128,65,128]{2,1,0:T(8,128)(2,1)}), bf16[128,65,128]{2,1,0:T(8,128)(2,1)S(1)}, u32[]{:S(2)}, u32[]{:S(2)}) async-start(bf16[128,65,128]{2,1,0:T(8,128)(2,1)} %pad_maximum_fusion.1), calls=%async_computation.1 | async-start | bytes 4718592 | tf_op jit(solution)/shard_map/all_to_all | solution.py:115
  239.7 5.3 %copy-start.18 = (s32[1,128]{1,0:T(1,128)S(1)}, s32[1,128]{1,0:T(1,128)}, u32[]{:S(2)}) copy-start(s32[1,128]{1,0:T(1,128)} %param.13) | copy-start | bytes 1540
  239.7 35.2 %all-to-all-start.2 = ((bf16[128,2,4096]{2,1,0:T(2,128)(2,1)}), bf16[128,2,4096]{2,1,0:T(2,128)(2,1)}, u32[]{:S(2)}, u32[]{:S(2)}) async-start(bf16[128,2,4096]{2,1,0:T(2,128)(2,1)} %bitcast.78), calls=%async_computation.2 | async-start | bytes 4194304 | tf_op jit(solution)/shard_map/all_to_all | solution.py:128

commit v3 on v2

--- a/solution.py
+++ b/solution.py
@@ -92,7 +92,7 @@
     meta_all = got_in[:, tok_rows, : 3 * tok_rows].astype(jnp.int32)
     segments = meta_all[:, :tok_rows].reshape(length)
     owner_all = meta_all[:, tok_rows : 2 * tok_rows]
-    adapter_all = meta_all[:, 2 * tok_rows :].reshape(length)
+    adapter_all = meta_all[:, 2 * tok_rows :]
 
     context = attend(q_all, k_all, v_all, segments).reshape(length, feat)
 
@@ -100,17 +100,24 @@
         one_hot = (owner_rows[..., None] == jnp.arange(devices, dtype=jnp.int32)).astype(jnp.int32)
         return jnp.sum(jnp.cumsum(one_hot, axis=-2) * one_hot, axis=-1) - 1
 
-    slot_all = (
-        jnp.arange(n_seq, dtype=jnp.int32)[:, None] * capacity + ranks(owner_all)
-    ).reshape(length)
-    target = owner_all.reshape(length) * slots + slot_all
-    pick = jnp.full((devices * slots,), length, jnp.int32).at[target].set(
-        jnp.arange(length, dtype=jnp.int32)
-    )
-    tags = jnp.full((devices * slots,), -1, jnp.int32).at[target].set(adapter_all)
-    ctx_ext = jnp.concatenate([context, jnp.zeros((1, feat), context.dtype)], axis=0)
-    send = ctx_ext[pick].reshape(devices, slots, feat)
-    tag_row = jnp.pad(tags.reshape(devices, slots).astype(jnp.bfloat16), ((0, 0), (0, feat - slots)))
+    pick = (
+        owner_all * capacity + ranks(owner_all)
+    )[:, None, :] == jnp.arange(devices * capacity, dtype=jnp.int32)[None, :, None]
+    pick = pick.astype(jnp.bfloat16)
+    send = jnp.einsum(
+        "jmt,jtf->mjf",
+        pick,
+        context.reshape(n_seq, tok_rows, feat),
+        preferred_element_type=jnp.float32,
+    ).astype(jnp.bfloat16)
+    send = send.reshape(devices, slots, feat)
+    tags = jnp.einsum(
+        "jmt,jt->mj",
+        pick,
+        (adapter_all.reshape(n_seq, tok_rows) + 1).astype(jnp.bfloat16),
+        preferred_element_type=jnp.float32,
+    ).reshape(devices, slots) - 1.0
+    tag_row = jnp.pad(tags.astype(jnp.bfloat16), ((0, 0), (0, feat - slots)))
     send = jnp.concatenate([send, tag_row[:, None, :]], axis=1)
     got = lax.all_to_all(send, ("seq", "store"), split_axis=0, concat_axis=0, tiled=True)
     got = got.reshape(n_seq, n_store, slots + 1, feat)
@@ -123,7 +130,7 @@
     delta = jnp.dot(low, adapter_up, preferred_element_type=jnp.float32).astype(jnp.bfloat16)
     mixed_rows = (rows.astype(jnp.float32) + delta.astype(jnp.float32)).astype(jnp.bfloat16)
     ret = jnp.transpose(
-        mixed_rows.reshape(n_store, n_seq, capacity, width), (1, 0, 2, 3)
+        mixed_rows.reshape(n_store, capacity, n_seq, width), (2, 0, 1, 3)
     ).reshape(devices, capacity, width)
     back = lax.all_to_all(ret, ("seq", "store"), split_axis=0, concat_axis=0, tiled=True)
     owners = chosen // EXP_DEV

time: 281 us -> 223 us (0.79)
  local copies, waits for them, and re-layouts: 102 us -> 41.2 us
  matrix products: 30.4 us -> 34.3 us
    scatter x2 -> x0, local copies, waits for them, and re-layouts: 31.3 us -> none  [the longest x1 15.7 us: local(): jnp.full((devices * slots,), -1, jnp.int32).at[target].set(adapter_all)]
    gather x1 -> x0, local copies, waits for them, and re-layouts: 24 us -> none  [local(): send = ctx_ext[pick].reshape(devices, slots, feat)]
    dot_general x0 -> x2, matrix products: none -> 3.98 us  [the longest x1 3.24 us: local(): jnp.einsum('jmt,jtf->mjf', pick, context.reshape(n_seq, tok_rows, feat),...]
    convert_element_type x1 -> x2, local copies, waits for them, and re-layouts: 0.08 us -> 3.54 us  [the longest x1 3.44 us: local(): send = jnp.einsum('jmt,jtf->mjf', pick, context.reshape(n_seq, tok_rows,...]
    dynamic_slice x4, local copies, waits for them, and re-layouts: 3.17 us -> 0.32 us  [one_block(): k_seg = lax.dynamic_slice_in_dim(segments, k_lo, width, 0)]
    reshape x2 -> x1, local copies, waits for them, and re-layouts: 7.23 us -> 5.12 us  [local(): mixed_rows.reshape(n_store, capacity, n_seq, width)]
    unnamed x47 -> x44, local copies, waits for them, and re-layouts: 7.18 us -> 5.63 us
  transfers between devices with their start and end apart: 3 -> 3, of which waited for: 3 -> 3; matrix products, arithmetic and copies ran while one was open for 1% -> 0% of each run, Pallas kernels for 0% -> 0%
where the time goes in v3:
time: 223 us; the launch traced here: 222 us
  waiting for transfers between devices  104 us (47%)
  local copies, waits for them, and re-layouts  41.2 us (18%)
  matrix products  34.3 us (15%)
  starting transfers between devices  21.6 us (10%)
  other arithmetic  15.7 us (7%)
  loops' own time  4.64 us (2%)
    all_to_all x1, waiting for transfers between devices, local(): lax.all_to_all(payload, 'seq', split_axis=1, concat_axis=0, tiled=True)  41 us
    all_to_all x1, waiting for transfers between devices, local(): lax.all_to_all(send, ('seq', 'store'), split_axis=0, concat_axis=0, tiled...  33.3 us
    all_to_all x1, waiting for transfers between devices, local(): lax.all_to_all(ret, ('seq', 'store'), split_axis=0, concat_axis=0, tiled=...  29.8 us
    dot_general x1, matrix products, local(): jnp.dot(low, adapter_up, preferred_element_type=jnp.float32)  12.1 us
    dot_general x8, matrix products, one_block(): jnp.einsum('qhd,nd->hqn', q_block, k_rows, preferred_element_type=jnp.flo...  11.7 us
    all_to_all x1, starting transfers between devices, local(): lax.all_to_all(payload, 'seq', split_axis=1, concat_axis=0, tiled=True)  9.42 us
    all_to_all x1, starting transfers between devices, local(): lax.all_to_all(send, ('seq', 'store'), split_axis=0, concat_axis=0, tiled...  7.35 us
    dot_general x8, matrix products, one_block(): jnp.einsum('hqn,nd->qhd', expo.astype(jnp.bfloat16), v_rows, preferred_el...  6.52 us
  transfers between devices with their start and end apart: 3, of which 3 were waited for; matrix products, arithmetic and copies ran while one was open for 0% of the time, Pallas kernels for 0%

profile of v3, /device:TPU:1, one launch (start us, length us, event | category | flops | bytes accessed | tf_op | source)
XLA Modules:
  0.0 222.0 jit_solution(541933084152615582)
XLA Ops:
  0.0 1.2 fusion.122
  4.3 1.6 copy.47
  7.6 2.0 pad_maximum_fusion
  9.6 9.4 %all-to-all-start = ((bf16[129,32,384]{2,0,1:T(8,128)(2,1)}), bf16[129,32,384]{2,0,1:T(8,128)(2,1)S(1)}, u32[]{:S(2)}, u32[]{:S(2)}) async-start(bf16[129,32,384]{2,0,1:T(8,128)(2,1)} %pad_maximum_fusion), calls=%async_computation | async-start | bytes 6684672 | tf_op jit(solution)/shard_map/all_to_all | solution.py:87
  19.6 41.0 %all-to-all-done = bf16[129,32,384]{2,0,1:T(8,128)(2,1)S(1)} async-done(((bf16[129,32,384]{2,0,1:T(8,128)(2,1)}), bf16[129,32,384]{2,0,1:T(8,128)(2,1)S(1)}, u32[]{:S(2)}, u32[]{:S(2)}) %all-to-all-start) | async-done | bytes 3170336 | tf_op jit(solution)/shard_map/all_to_all | solution.py:87
  62.4 1.1 fusion.127
  64.5 2.3 %fusion.124 = (bf16[32,128,128]{2,1,0:T(8,128)(2,1)}, bf16[32,128,128]{2,1,0:T(8,128)(2,1)}, bf16[32,128,128]{2,1,0:T(8,128)(2,1)}) fusion(bf16[32,129,384]{2,1,0:T(8,128)(2,1)S(1)} %bitcast.284), kind=kLoop, calls=%fused_computation.178 | loop fusion | bytes 6291456 | tf_op jit(solution)/shard_map/slice | solution.py:89
  66.7 1.1 fusion.132
  75.8 3.3 %select_reduce_fusion = s32[32,128]{0,1:T(8,128)S(1)} fusion(s32[32,128]{0,1:T(8,128)S(1)} %copy.58), kind=kOutput, calls=%fused_computation.55 | output fusion | flops 69201920 | bytes 32768 | tf_op jit(solution)/shard_map/jit(cumsum)/reduce_window_sum | solution.py:101
  79.8 29.3 %while.14 = (s32[]{:T(128)}, bf16[4,512,128]{2,1,0:T(8,128)(2,1)}, s32[4]{0:T(128)}, bf16[4096,128]{1,0:T(8,128)(2,1)S(1)}, s32[4096]{0:T(1024)S(1)}, /*index=5*...) while((s32[]{:T(128)}, bf16[4,512,128]{2,1,0:T(8,128)(2,1)}, ...), condition=%wide.region_11.12_spmd, body=%wide.region_8.11_spmd.sunk | while | flops 684328960 | bytes 17902368 | solution.py:47
  79.8 1.2 dynamic_slice.215
  82.3 2.2 fusion.155
  87.1 1.2 dynamic_slice.215
  89.6 2.2 fusion.155
  94.4 1.2 dynamic_slice.215
  96.9 2.2 fusion.155
  99.9 1.0 fusion.157
  101.7 1.2 dynamic_slice.215
  104.2 2.2 fusion.155
  110.9 1.1 constant_dynamic-update-slice_fusion.1
  112.1 3.2 %convert_bitcast_fusion = bf16[256,32,128]{0,2,1:T(8,128)(2,1)} fusion(bf16[32,128,128]{2,1,0:T(8,128)(2,1)S(1)} %bitcast.294, s32[32,128]{1,0:T(8,128)} %get-tuple-element.181), kind=kOutput, calls=%fused_computation.52 | convolution fusion | flops 270532608 | bytes 3162112 | tf_op jit(solution)/shard_map/jmt,jtf->mjf/dot_general | solution.py:107
  115.3 3.4 %copy.61 = bf16[256,32,128]{2,1,0:T(8,128)(2,1)S(1)} copy(bf16[256,32,128]{0,2,1:T(8,128)(2,1)} %convert_bitcast_fusion) | data formatting | bytes 4194304 | tf_op jit(solution)/shard_map/convert_element_type | solution.py:112
  119.8 1.7 pad_maximum_fusion.1
  121.5 7.3 %all-to-all-start.1 = ((bf16[128,65,128]{2,1,0:T(8,128)(2,1)}), bf16[128,65,128]{2,1,0:T(8,128)(2,1)S(1)}, u32[]{:S(2)}, u32[]{:S(2)}) async-start(bf16[128,65,128]{2,1,0:T(8,128)(2,1)} %pad_maximum_fusion.1), calls=%async_computation.1 | async-start | bytes 4718592 | tf_op jit(solution)/shard_map/all_to_all | solution.py:122
  128.9 33.3 %all-to-all-done.1 = bf16[128,65,128]{2,1,0:T(8,128)(2,1)S(1)} async-done(((bf16[128,65,128]{2,1,0:T(8,128)(2,1)}), bf16[128,65,128]{2,1,0:T(8,128)(2,1)S(1)}, u32[]{:S(2)}, u32[]{:S(2)}) %all-to-all-start.1) | async-done | bytes 2129952 | tf_op jit(solution)/shard_map/all_to_all | solution.py:122
  162.7 1.6 slice_bitcast_fusion
  164.7 12.1 %fusion.26 = bf16[256,4096]{1,0:T(8,128)(2,1)} fusion(bf16[1024,4096]{1,0:T(8,128)(2,1)} %param.15, bf16[32,8,32,128]{3,2,1,0:T(8,128)(2,1)S(1)} %bitcast.290, bf16[4096,1024]{1,0:T(8,128)(2,1)} %param.14, f32[1024]{0:T(1024)S(1)} %fusion.114, f32[256]{0:T(256)S(1)} %reshape.907), kind=kOutput, calls=%fused_computation.25 | convolution fusion | flops 4300996608 | bytes 20976640 | tf_op jit(solution)/shard_map/dot_general | solution.py:130
  176.8 5.1 %copy.65 = bf16[4,2,32,4096]{3,1,0,2:T(2,128)(2,1)} copy(bf16[4,2,32,4096]{3,2,1,0:T(8,128)(2,1)} %bitcast.291) | data formatting | bytes 4194304 | tf_op jit(solution)/shard_map/reshape | solution.py:133
  182.0 4.8 %all-to-all-start.2 = ((bf16[128,2,4096]{2,1,0:T(2,128)(2,1)}), bf16[128,2,4096]{2,1,0:T(2,128)(2,1)}, u32[]{:S(2)}, u32[]{:S(2)}) async-start(bf16[128,2,4096]{2,1,0:T(2,128)(2,1)} %bitcast.81), calls=%async_computation.2 | async-start | bytes 4194304 | tf_op jit(solution)/shard_map/all_to_all | solution.py:135
  187.3 29.8 %all-to-all-done.2 = bf16[128,2,4096]{2,1,0:T(2,128)(2,1)} async-done(((bf16[128,2,4096]{2,1,0:T(2,128)(2,1)}), bf16[128,2,4096]{2,1,0:T(2,128)(2,1)}, u32[]{:S(2)}, u32[]{:S(2)}) %all-to-all-start.2) | async-done | bytes 2097184 | tf_op jit(solution)/shard_map/all_to_all | solution.py:135
  217.1 2.7 %reshape.905 = bf16[256,4096]{1,0:T(8,128)(2,1)S(1)} reshape(bf16[128,2,4096]{2,1,0:T(2,128)(2,1)} %all-to-all-done.2) | data formatting | bytes 4194304 | tf_op jit(solution)/shard_map/reshape | solution.py:138
  219.9 2.2 gather_fusion.1
  (134 shorter events, 30.8 us)
Async XLA Ops:
  9.6 50.9 %all-to-all-start = ((bf16[129,32,384]{2,0,1:T(8,128)(2,1)}), bf16[129,32,384]{2,0,1:T(8,128)(2,1)S(1)}, u32[]{:S(2)}, u32[]{:S(2)}) async-start(bf16[129,32,384]{2,0,1:T(8,128)(2,1)} %pad_maximum_fusion), calls=%async_computation | async-start | bytes 6684672 | tf_op jit(solution)/shard_map/all_to_all | solution.py:87
  61.5 3.0 %copy-start.4 = (s32[32,1,384]{2,0,1:T(8,128)}, s32[32,1,384]{2,0,1:T(8,128)S(1)}, u32[]{:S(2)}) copy-start(s32[32,1,384]{2,0,1:T(8,128)S(1)} %copy.88) | copy-start | bytes 147460
  68.4 1.0 copy-start.6
  68.4 1.0 copy-start.12
  69.5 1.4 copy-start.1
  70.3 2.0 copy-start.7
  70.3 2.0 copy-start.11
  71.5 1.8 copy-start.2
  72.9 1.7 copy-start.9
  72.9 1.7 copy-start.10
  72.9 1.7 copy-start.16
  73.3 1.9 copy-start.8
  73.8 5.3 %copy-start.5 = (s32[32,1,384]{2,0,1:T(8,128)S(1)}, s32[32,1,384]{2,0,1:T(8,128)}, u32[]{:S(2)}) copy-start(s32[32,1,384]{2,0,1:T(8,128)} %copy-done.4) | copy-start | bytes 147460
  73.8 5.9 %copy-start = (bf16[32,128,128]{2,1,0:T(8,128)(2,1)S(1)}, bf16[32,128,128]{2,1,0:T(8,128)(2,1)}, u32[]{:S(2)}) copy-start(bf16[32,128,128]{2,1,0:T(8,128)(2,1)} %get-tuple-element.167) | copy-start | bytes 3145732
  73.8 5.9 %copy-start.3 = (bf16[32,128,128]{2,1,0:T(8,128)(2,1)S(1)}, bf16[32,128,128]{2,1,0:T(8,128)(2,1)}, u32[]{:S(2)}) copy-start(bf16[32,128,128]{2,1,0:T(8,128)(2,1)} %get-tuple-element.166) | copy-start | bytes 3145732
  112.0 6.7 %copy-start.13 = (s32[32,128]{1,0:T(8,128)S(1)}, s32[32,128]{1,0:T(8,128)}, u32[]{:S(2)}) copy-start(s32[32,128]{1,0:T(8,128)} %get-tuple-element.181) | copy-start | bytes 49156
  112.0 6.7 %copy-start.14 = (bf16[32,128,1]{1,0,2:T(8,128)(2,1)S(1)}, bf16[32,128,1]{1,0,2:T(8,128)(2,1)}, u32[]{:S(2)}) copy-start(bf16[32,128,1]{1,0,2:T(8,128)(2,1)} %get-tuple-element.182) | copy-start | bytes 24580
  121.5 40.7 %all-to-all-start.1 = ((bf16[128,65,128]{2,1,0:T(8,128)(2,1)}), bf16[128,65,128]{2,1,0:T(8,128)(2,1)S(1)}, u32[]{:S(2)}, u32[]{:S(2)}) async-start(bf16[128,65,128]{2,1,0:T(8,128)(2,1)} %pad_maximum_fusion.1), calls=%async_computation.1 | async-start | bytes 4718592 | tf_op jit(solution)/shard_map/all_to_all | solution.py:122
  182.0 4.9 %copy-start.15 = (s32[128]{0:T(128)S(1)}, s32[128]{0:T(128)}, u32[]{:S(2)}) copy-start(s32[128]{0:T(128)} %get-tuple-element.162) | copy-start | bytes 1540
  182.0 5.3 %copy-start.17 = (s32[1,128]{1,0:T(1,128)S(1)}, s32[1,128]{1,0:T(1,128)}, u32[]{:S(2)}) copy-start(s32[1,128]{1,0:T(1,128)} %param.13) | copy-start | bytes 1540
  182.0 35.2 %all-to-all-start.2 = ((bf16[128,2,4096]{2,1,0:T(2,128)(2,1)}), bf16[128,2,4096]{2,1,0:T(2,128)(2,1)}, u32[]{:S(2)}, u32[]{:S(2)}) async-start(bf16[128,2,4096]{2,1,0:T(2,128)(2,1)} %bitcast.81), calls=%async_computation.2 | async-start | bytes 4194304 | tf_op jit(solution)/shard_map/all_to_all | solution.py:135

commit v4 on v3

--- a/solution.py
+++ b/solution.py
@@ -1,6 +1,10 @@
+import functools
+
 import jax
 import jax.numpy as jnp
 from jax import lax
+from jax.experimental import pallas as pl
+from jax.experimental.pallas import tpu as pltpu
 from jax.sharding import PartitionSpec as P
 
 HEAD_DIM = 128
@@ -11,45 +15,82 @@
 MAX_DOC = 2048
 
 
+def _attn_kernel(lo_ref, q_ref, k_ref, v_ref, qs_ref, o_ref, *, bq, bk, scale):
+    i = pl.program_id(0)
+    q = q_ref[...]
+    qs = qs_ref[...]
+    qpos = i * bq + lax.broadcasted_iota(jnp.int32, (bq, 1), 0)
+    lo = lo_ref[i]
+    hi = (i * bq + bq + bk - 1) // bk
+
+    def scores(kb):
+        start = pl.multiple_of(kb * bk, bk)
+        k = k_ref[pl.ds(start, bk), :]
+        s = lax.dot_general(
+            q, k, (((1,), (1,)), ((), ())), preferred_element_type=jnp.float32
+        ) * scale
+        kpos = start + lax.broadcasted_iota(jnp.int32, (1, bk), 1)
+        ok = (kpos >= qs) & (kpos <= qpos)
+        return jnp.where(ok, s, jnp.float32(-1e30)), start
+
+    def max_body(kb, m):
+        s, _ = scores(kb)
+        return jnp.maximum(m, jnp.max(s, axis=1, keepdims=True))
+
+    m = lax.fori_loop(lo, hi, max_body, jnp.full((bq, 1), -1e30, jnp.float32))
+
+    def sum_body(kb, carry):
+        total, acc = carry
+        s, start = scores(kb)
+        p = jnp.exp(s - m)
+        total = total + jnp.sum(p, axis=1, keepdims=True)
+        v = v_ref[pl.ds(start, bk), :]
+        acc = acc + jnp.dot(p.astype(jnp.bfloat16), v, preferred_element_type=jnp.float32)
+        return total, acc
+
+    total, acc = lax.fori_loop(
+        lo,
+        hi,
+        sum_body,
+        (jnp.zeros((bq, 1), jnp.float32), jnp.zeros((bq, q.shape[1]), jnp.float32)),
+    )
+    o_ref[...] = (acc / total).astype(o_ref.dtype)
+
+
 def attend(queries, key_rows, value_rows, segments):
-    length = queries.shape[0]
-    block = min(512, length)
-    scale = queries.shape[2] ** (-0.5)
-    key_pos = jnp.arange(length, dtype=jnp.int32)
-    n_blocks = length // block
-    reach = min(n_blocks, (MAX_DOC + block - 1) // block + 1)
-
-    def one_block(start, k_lo, width):
-        q_block = lax.dynamic_slice_in_dim(queries, start, block, 0)
-        seg_block = lax.dynamic_slice_in_dim(segments, start, block, 0)
-        k_rows = lax.dynamic_slice_in_dim(key_rows, k_lo, width, 0)
-        v_rows = lax.dynamic_slice_in_dim(value_rows, k_lo, width, 0)
-        k_seg = lax.dynamic_slice_in_dim(segments, k_lo, width, 0)
-        k_pos = k_lo + jnp.arange(width, dtype=jnp.int32)
-        scores = (
-            jnp.einsum("qhd,nd->hqn", q_block, k_rows, preferred_element_type=jnp.float32) * scale
-        )
-        q_pos = start + jnp.arange(block, dtype=jnp.int32)
-        allowed = (k_pos[None, :] <= q_pos[:, None]) & (k_seg[None, :] == seg_block[:, None])
-        scores = jnp.where(allowed[None], scores, jnp.float32(-1e30))
-        top = jnp.max(scores, axis=-1, keepdims=True)
-        expo = jnp.exp(scores - top)
-        total = jnp.sum(expo, axis=-1)
-        summed = jnp.einsum(
-            "hqn,nd->qhd", expo.astype(jnp.bfloat16), v_rows, preferred_element_type=jnp.float32
-        )
-        out = summed / jnp.transpose(total)[:, :, None]
-        return out.astype(jnp.bfloat16).reshape(block, -1)
-
-    outs = [one_block(i * block, 0, (i + 1) * block) for i in range(min(reach - 1, n_blocks))]
-    if n_blocks >= reach:
-        width = reach * block
-        rest = lax.map(
-            lambda i: one_block(i * block, (i + 1) * block - width, width),
-            jnp.arange(reach - 1, n_blocks, dtype=jnp.int32),
-        )
-        outs.append(rest.reshape((n_blocks - reach + 1) * block, -1))
-    return jnp.concatenate(outs, axis=0)
+    length, dim = key_rows.shape
+    bq = min(256, length)
+    bk = min(256, length)
+    n_q = length // bq
+    pos = jnp.arange(length, dtype=jnp.int32)
+    boundary = jnp.concatenate(
+        [jnp.ones((1,), jnp.bool_), segments[1:] != segments[:-1]]
+    )
+    doc_start = lax.cummax(jnp.where(boundary, pos, 0), axis=0)
+    lo_blk = doc_start[::bq] // bk
+    q_rows = queries.reshape(length, dim)
+    kernel = functools.partial(_attn_kernel, bq=bq, bk=bk, scale=dim ** (-0.5))
+    out = pl.pallas_call(
+        kernel,
+        out_shape=jax.ShapeDtypeStruct((length, dim), jnp.bfloat16),
+        grid_spec=pltpu.PrefetchScalarGridSpec(
+            num_scalar_prefetch=1,
+            grid=(n_q,),
+            in_specs=[
+                pl.BlockSpec((bq, dim), lambda i, lo: (i, 0)),
+                pl.BlockSpec((length, dim), lambda i, lo: (0, 0)),
+                pl.BlockSpec((length, dim), lambda i, lo: (0, 0)),
+                pl.BlockSpec((bq, 1), lambda i, lo: (i, 0)),
+            ],
+            out_specs=pl.BlockSpec((bq, dim), lambda i, lo: (i, 0)),
+        ),
+        cost_estimate=pl.CostEstimate(
+            flops=6 * length * MAX_DOC * dim,
+            transcendentals=length * MAX_DOC,
+            bytes_accessed=8 * length * dim,
+        ),
+    )(lo_blk, q_rows, key_rows, value_rows, doc_start.reshape(length, 1))
+    return out
 
 
 def local(queries, keys, values, segment_ids, route_ids, adapter_down, adapter_up):

time: 223 us -> 223 us (level); the launches traced: 222 us -> 225 us
  blocking collectives: 0 us -> 51.2 us
  Pallas kernels: 0 us -> 49.5 us
  waiting for transfers between devices: 104 us -> 63.1 us
  matrix products: 34.3 us -> 15.2 us
  local copies, waits for them, and re-layouts: 41.2 us -> 25.9 us
  starting transfers between devices: 21.6 us -> 9.11 us
  other arithmetic: 15.7 us -> 10.5 us
  loops' own time: 4.64 us -> 0 us
    all_to_all x0 -> x1, blocking collectives: none -> 51.2 us  [local(): lax.all_to_all(payload, 'seq', split_axis=1, concat_axis=0, tiled=True)]
    pallas_call x0 -> x1, Pallas kernels: none -> 49.5 us  [attend(): pl.pallas_call(kernel, out_shape=jax.ShapeDtypeStruct((length, dim), jnp....]
    all_to_all x1 -> x0, waiting for transfers between devices: 41 us -> none  [local(): lax.all_to_all(payload, 'seq', split_axis=1, concat_axis=0, tiled=True)]
    dot_general x16 -> x0, matrix products: 18.2 us -> none  [the longest x8 11.7 us: one_block(): jnp.einsum('qhd,nd->hqn', q_block, k_rows, preferred_element_type=jnp.flo...]
    all_to_all x1 -> x0, starting transfers between devices: 9.42 us -> none  [local(): lax.all_to_all(payload, 'seq', split_axis=1, concat_axis=0, tiled=True)]
    dynamic_slice x16 -> x0, local copies, waits for them, and re-layouts: 8.65 us -> none  [the longest x4 4.76 us: attend(): lax.map(lambda i: one_block(i * block, (i + 1) * block - width, width), j...]
    reduce_sum x8 -> x0, other arithmetic: 4.77 us -> none  [one_block(): total = jnp.sum(expo, axis=-1)]
    another operation x1 -> x0, loops' own time: 4.64 us -> none  [attend(): lax.map(lambda i: one_block(i * block, (i + 1) * block - width, width), j...]
  transfers between devices with their start and end apart: 3 -> 2, of which waited for: 3 -> 2; matrix products, arithmetic and copies ran while one was open for 0% -> 0% of each run, Pallas kernels for 0% -> 0%
where the time goes in v4:
time: 223 us; the launch traced here: 225 us
  waiting for transfers between devices  63.1 us (28%)
  blocking collectives  51.2 us (23%)
  Pallas kernels  49.5 us (22%)
  local copies, waits for them, and re-layouts  25.9 us (12%)
  matrix products  15.2 us (7%)
  other arithmetic  10.5 us (5%)
  starting transfers between devices  9.11 us (4%)
    all_to_all x1, blocking collectives, local(): lax.all_to_all(payload, 'seq', split_axis=1, concat_axis=0, tiled=True)  51.2 us
    pallas_call x1, Pallas kernels, attend(): pl.pallas_call(kernel, out_shape=jax.ShapeDtypeStruct((length, dim), jnp....  49.5 us
    all_to_all x1, waiting for transfers between devices, local(): lax.all_to_all(send, ('seq', 'store'), split_axis=0, concat_axis=0, tiled...  33.3 us
    all_to_all x1, waiting for transfers between devices, local(): lax.all_to_all(ret, ('seq', 'store'), split_axis=0, concat_axis=0, tiled=...  29.8 us
    dot_general x1, matrix products, local(): jnp.dot(low, adapter_up, preferred_element_type=jnp.float32)  12.1 us
    reshape x1, local copies, waits for them, and re-layouts, local(): mixed_rows.reshape(n_store, capacity, n_seq, width)  5.12 us
    all_to_all x1, starting transfers between devices, local(): lax.all_to_all(ret, ('seq', 'store'), split_axis=0, concat_axis=0, tiled=...  4.85 us
  transfers between devices with their start and end apart: 2, of which 2 were waited for; matrix products, arithmetic and copies ran while one was open for 0% of the time, Pallas kernels for 0%

profile of v4, /device:TPU:1, one launch (start us, length us, event | category | flops | bytes accessed | tf_op | source)
XLA Modules:
  0.0 224.8 jit_solution(24347488622348403)
XLA Ops:
  0.0 0.7 fusion.38
  0.7 0.7 convert_bitcast_fusion.1
  1.4 1.0 copy.35
  2.5 1.0 copy.34
  3.7 1.6 copy.33
  5.3 0.7 copy.38
  6.0 0.7 gather_fusion
  6.7 0.3 select_bitcast_fusion
  7.1 0.5 pad_maximum_fusion
  7.6 51.2 %all_to_all.25 = bf16[129,32,384]{2,0,1:T(8,128)(2,1)S(1)} all-to-all(bf16[129,32,384]{2,0,1:T(8,128)(2,1)S(1)} %pad_maximum_fusion), channel_id=1, replica_groups=mesh['seq'=32,'store'=4] {'seq'}, dimensions={1} | all-to-all | bytes 6340608 | tf_op jit(solution)/shard_map/all_to_all | solution.py:128
  58.8 2.2 fusion.39
  61.1 3.3 %select_reduce_fusion = s32[32,128]{0,1:T(8,128)S(1)} fusion(s32[32,128]{0,1:T(8,128)S(1)} %copy.40), kind=kOutput, calls=%fused_computation.18 | output fusion | flops 69201920 | bytes 32768 | tf_op jit(solution)/shard_map/jit(cumsum)/reduce_window_sum | solution.py:142
  64.7 0.3 reduce-window.9
  65.4 0.7 fusion.3
  66.6 0.6 and_select_fusion.1.lo_ref
  67.1 2.0 copy.39.qs_ref
  69.1 49.5 %shard_map.73 = bf16[4096,128]{1,0:T(8,128)(2,1)} custom-call(s32[16]{0:T(128)} %and_select_fusion.1.lo_ref, bf16[4096,128]{1,0:T(8,128)(2,1)} %bitcast.113, bf16[4096,128]{1,0:T(8,128)(2,1)} %bitcast.112, bf16[4096,128]{1,0:T(8,128)(2,1)} %bitcast.111, s32[4096,1]{1,0:T(8,128)} %copy.39.qs_ref), custom_call_target="tpu_custom_call" | custom-call | flops 6442450944 | bytes 4194304 | tf_op jit(solution)/shard_map/pallas_call | solution.py:73
  118.6 2.3 %convert_bitcast_fusion = bf16[256,32,128]{0,2,1:T(8,128)(2,1)S(1)} fusion(bf16[32,128,128]{2,1,0:T(8,128)(2,1)} %bitcast.110, s32[32,128]{1,0:T(8,128)S(1)} %get-tuple-element.11), kind=kOutput, calls=%fused_computation.15 | convolution fusion | flops 270532608 | bytes 3162112 | tf_op jit(solution)/shard_map/jmt,jtf->mjf/dot_general | solution.py:148
  120.9 3.1 %copy.43 = bf16[256,32,128]{2,1,0:T(8,128)(2,1)} copy(bf16[256,32,128]{0,2,1:T(8,128)(2,1)S(1)} %convert_bitcast_fusion) | data formatting | bytes 4194304 | tf_op jit(solution)/shard_map/convert_element_type | solution.py:153
  124.1 3.3 %pad_maximum_fusion.1 = bf16[128,65,128]{2,1,0:T(8,128)(2,1)} fusion(bf16[128,1,128]{2,1,0:T(2,128)(2,1)S(1)} %copy.44, bf16[128,64,128]{2,1,0:T(8,128)(2,1)} %bitcast.106), kind=kLoop, calls=%fused_computation.10 | loop fusion | flops 4259840 | bytes 4259840 | tf_op jit(solution)/shard_map/concatenate | solution.py:162
  127.3 4.3 %all-to-all-start.1 = ((bf16[128,65,128]{2,1,0:T(8,128)(2,1)}), bf16[128,65,128]{2,1,0:T(8,128)(2,1)S(1)}, u32[]{:S(2)}, u32[]{:S(2)}) async-start(bf16[128,65,128]{2,1,0:T(8,128)(2,1)} %pad_maximum_fusion.1), calls=%async_computation.1 | async-start | bytes 4718592 | tf_op jit(solution)/shard_map/all_to_all | solution.py:163
  131.6 33.3 %all-to-all-done.1 = bf16[128,65,128]{2,1,0:T(8,128)(2,1)S(1)} async-done(((bf16[128,65,128]{2,1,0:T(8,128)(2,1)}), bf16[128,65,128]{2,1,0:T(8,128)(2,1)S(1)}, u32[]{:S(2)}, u32[]{:S(2)}) %all-to-all-start.1) | async-done | bytes 2129952 | tf_op jit(solution)/shard_map/all_to_all | solution.py:163
  164.9 0.5 copy.45
  165.4 1.6 slice_bitcast_fusion
  167.0 0.4 copy.46
  167.5 12.1 %fusion.2 = bf16[256,4096]{1,0:T(8,128)(2,1)} fusion(bf16[1024,4096]{1,0:T(8,128)(2,1)} %param.13, bf16[32,8,32,128]{3,2,1,0:T(8,128)(2,1)S(1)} %bitcast.108, bf16[4096,1024]{1,0:T(8,128)(2,1)} %param.12, f32[1024]{0:T(1024)S(1)} %fusion.30, f32[256]{0:T(256)S(1)} %reshape.292), kind=kOutput, calls=%fused_computation.5 | convolution fusion | flops 4300996608 | bytes 20976640 | tf_op jit(solution)/shard_map/dot_general | solution.py:171
  179.6 5.1 %copy.47 = bf16[4,2,32,4096]{3,1,0,2:T(2,128)(2,1)} copy(bf16[4,2,32,4096]{3,2,1,0:T(8,128)(2,1)} %bitcast.109) | data formatting | bytes 4194304 | tf_op jit(solution)/shard_map/reshape | solution.py:174
  184.7 4.8 %all-to-all-start.2 = ((bf16[128,2,4096]{2,1,0:T(2,128)(2,1)}), bf16[128,2,4096]{2,1,0:T(2,128)(2,1)}, u32[]{:S(2)}, u32[]{:S(2)}) async-start(bf16[128,2,4096]{2,1,0:T(2,128)(2,1)} %bitcast.30), calls=%async_computation.2 | async-start | bytes 4194304 | tf_op jit(solution)/shard_map/all_to_all | solution.py:176
  189.6 0.2 reduce_window_sum.23
  190.0 29.8 %all-to-all-done.2 = bf16[128,2,4096]{2,1,0:T(2,128)(2,1)} async-done(((bf16[128,2,4096]{2,1,0:T(2,128)(2,1)}), bf16[128,2,4096]{2,1,0:T(2,128)(2,1)}, u32[]{:S(2)}, u32[]{:S(2)}) %all-to-all-start.2) | async-done | bytes 2097184 | tf_op jit(solution)/shard_map/all_to_all | solution.py:176
  219.9 2.7 %reshape.290 = bf16[256,4096]{1,0:T(8,128)(2,1)S(1)} reshape(bf16[128,2,4096]{2,1,0:T(2,128)(2,1)} %all-to-all-done.2) | data formatting | bytes 4194304 | tf_op jit(solution)/shard_map/reshape | solution.py:179
  222.6 2.2 gather_fusion.1
  (36 shorter events, 1.9 us)
Async XLA Ops:
  127.3 37.6 %all-to-all-start.1 = ((bf16[128,65,128]{2,1,0:T(8,128)(2,1)}), bf16[128,65,128]{2,1,0:T(8,128)(2,1)S(1)}, u32[]{:S(2)}, u32[]{:S(2)}) async-start(bf16[128,65,128]{2,1,0:T(8,128)(2,1)} %pad_maximum_fusion.1), calls=%async_computation.1 | async-start | bytes 4718592 | tf_op jit(solution)/shard_map/all_to_all | solution.py:163
  184.7 5.3 %copy-start = (s32[1,128]{1,0:T(1,128)S(1)}, s32[1,128]{1,0:T(1,128)}, u32[]{:S(2)}) copy-start(s32[1,128]{1,0:T(1,128)} %param.11) | copy-start | bytes 1540
  184.7 35.2 %all-to-all-start.2 = ((bf16[128,2,4096]{2,1,0:T(2,128)(2,1)}), bf16[128,2,4096]{2,1,0:T(2,128)(2,1)}, u32[]{:S(2)}, u32[]{:S(2)}) async-start(bf16[128,2,4096]{2,1,0:T(2,128)(2,1)} %bitcast.30), calls=%async_computation.2 | async-start | bytes 4194304 | tf_op jit(solution)/shard_map/all_to_all | solution.py:176

commit v5 on v4

--- a/solution.py
+++ b/solution.py
@@ -15,45 +15,54 @@
 MAX_DOC = 2048
 
 
-def _attn_kernel(lo_ref, q_ref, k_ref, v_ref, qs_ref, o_ref, *, bq, bk, scale):
+def _attn_kernel(lo_ref, full_ref, q_ref, k_ref, v_ref, qs_ref, o_ref, *, bq, bk, scale):
     i = pl.program_id(0)
+    lanes = 128
     q = q_ref[...]
     qs = qs_ref[...]
     qpos = i * bq + lax.broadcasted_iota(jnp.int32, (bq, 1), 0)
     lo = lo_ref[i]
-    hi = (i * bq + bq + bk - 1) // bk
-
-    def scores(kb):
+    mid = jnp.clip(full_ref[i], lo, i)
+
+    def raw(kb):
         start = pl.multiple_of(kb * bk, bk)
         k = k_ref[pl.ds(start, bk), :]
         s = lax.dot_general(
             q, k, (((1,), (1,)), ((), ())), preferred_element_type=jnp.float32
         ) * scale
+        return s, start
+
+    def masked(kb):
+        s, start = raw(kb)
         kpos = start + lax.broadcasted_iota(jnp.int32, (1, bk), 1)
         ok = (kpos >= qs) & (kpos <= qpos)
         return jnp.where(ok, s, jnp.float32(-1e30)), start
 
-    def max_body(kb, m):
-        s, _ = scores(kb)
-        return jnp.maximum(m, jnp.max(s, axis=1, keepdims=True))
-
-    m = lax.fori_loop(lo, hi, max_body, jnp.full((bq, 1), -1e30, jnp.float32))
-
-    def sum_body(kb, carry):
-        total, acc = carry
-        s, start = scores(kb)
-        p = jnp.exp(s - m)
-        total = total + jnp.sum(p, axis=1, keepdims=True)
+    def fold_max(m, s):
+        for c in range(bk // lanes):
+            m = jnp.maximum(m, s[:, c * lanes : (c + 1) * lanes])
+        return m
+
+    m = jnp.full((bq, lanes), -1e30, jnp.float32)
+    m = lax.fori_loop(lo, mid, lambda kb, m: fold_max(m, masked(kb)[0]), m)
+    m = lax.fori_loop(mid, i, lambda kb, m: fold_max(m, raw(kb)[0]), m)
+    m = fold_max(m, masked(i)[0])
+    top = jnp.max(m, axis=1, keepdims=True)
+
+    def accum(carry, s, start):
+        tot, acc = carry
+        p = jnp.exp(s - top)
+        for c in range(bk // lanes):
+            tot = tot + p[:, c * lanes : (c + 1) * lanes]
         v = v_ref[pl.ds(start, bk), :]
         acc = acc + jnp.dot(p.astype(jnp.bfloat16), v, preferred_element_type=jnp.float32)
-        return total, acc
-
-    total, acc = lax.fori_loop(
-        lo,
-        hi,
-        sum_body,
-        (jnp.zeros((bq, 1), jnp.float32), jnp.zeros((bq, q.shape[1]), jnp.float32)),
-    )
+        return tot, acc
+
+    carry = (jnp.zeros((bq, lanes), jnp.float32), jnp.zeros((bq, q.shape[1]), jnp.float32))
+    carry = lax.fori_loop(lo, mid, lambda kb, c: accum(c, *masked(kb)), carry)
+    carry = lax.fori_loop(mid, i, lambda kb, c: accum(c, *raw(kb)), carry)
+    tot, acc = accum(carry, *masked(i))
+    total = jnp.sum(tot, axis=1, keepdims=True)
     o_ref[...] = (acc / total).astype(o_ref.dtype)
 
 
@@ -68,28 +77,29 @@
     )
     doc_start = lax.cummax(jnp.where(boundary, pos, 0), axis=0)
     lo_blk = doc_start[::bq] // bk
+    full_blk = (doc_start[bq - 1 :: bq] + bk - 1) // bk
     q_rows = queries.reshape(length, dim)
     kernel = functools.partial(_attn_kernel, bq=bq, bk=bk, scale=dim ** (-0.5))
     out = pl.pallas_call(
         kernel,
         out_shape=jax.ShapeDtypeStruct((length, dim), jnp.bfloat16),
         grid_spec=pltpu.PrefetchScalarGridSpec(
-            num_scalar_prefetch=1,
+            num_scalar_prefetch=2,
             grid=(n_q,),
             in_specs=[
-                pl.BlockSpec((bq, dim), lambda i, lo: (i, 0)),
-                pl.BlockSpec((length, dim), lambda i, lo: (0, 0)),
-                pl.BlockSpec((length, dim), lambda i, lo: (0, 0)),
-                pl.BlockSpec((bq, 1), lambda i, lo: (i, 0)),
+                pl.BlockSpec((bq, dim), lambda i, lo, full: (i, 0)),
+                pl.BlockSpec((length, dim), lambda i, lo, full: (0, 0)),
+                pl.BlockSpec((length, dim), lambda i, lo, full: (0, 0)),
+                pl.BlockSpec((bq, 1), lambda i, lo, full: (i, 0)),
             ],
-            out_specs=pl.BlockSpec((bq, dim), lambda i, lo: (i, 0)),
+            out_specs=pl.BlockSpec((bq, dim), lambda i, lo, full: (i, 0)),
         ),
         cost_estimate=pl.CostEstimate(
             flops=6 * length * MAX_DOC * dim,
             transcendentals=length * MAX_DOC,
             bytes_accessed=8 * length * dim,
         ),
-    )(lo_blk, q_rows, key_rows, value_rows, doc_start.reshape(length, 1))
+    )(lo_blk, full_blk, q_rows, key_rows, value_rows, doc_start.reshape(length, 1))
     return out
 
 

time: 223 us -> 219 us (0.982)
  Pallas kernels: 49.5 us -> 40.2 us
  starting transfers between devices: 9.11 us -> 12.8 us
    pallas_call x1, Pallas kernels: 49.5 us -> 40.2 us  [attend(): pl.pallas_call(kernel, out_shape=jax.ShapeDtypeStruct((length, dim), jnp....]
    all_to_all x1, starting transfers between devices: 4.26 us -> 7.91 us  [local(): lax.all_to_all(send, ('seq', 'store'), split_axis=0, concat_axis=0, tiled...]
where the time goes in v5:
time: 219 us
  waiting for transfers between devices  63.1 us (29%)
  blocking collectives  51.2 us (23%)
  Pallas kernels  40.2 us (18%)
  local copies, waits for them, and re-layouts  26 us (12%)
  matrix products  15.2 us (7%)
  starting transfers between devices  12.8 us (6%)
  other arithmetic  10.6 us (5%)
    all_to_all x1, blocking collectives, local(): lax.all_to_all(payload, 'seq', split_axis=1, concat_axis=0, tiled=True)  51.2 us
    pallas_call x1, Pallas kernels, attend(): pl.pallas_call(kernel, out_shape=jax.ShapeDtypeStruct((length, dim), jnp....  40.2 us
    all_to_all x1, waiting for transfers between devices, local(): lax.all_to_all(send, ('seq', 'store'), split_axis=0, concat_axis=0, tiled...  33.3 us
    all_to_all x1, waiting for transfers between devices, local(): lax.all_to_all(ret, ('seq', 'store'), split_axis=0, concat_axis=0, tiled=...  29.8 us
    dot_general x1, matrix products, local(): jnp.dot(low, adapter_up, preferred_element_type=jnp.float32)  12.1 us
    all_to_all x1, starting transfers between devices, local(): lax.all_to_all(send, ('seq', 'store'), split_axis=0, concat_axis=0, tiled...  7.91 us
    reshape x1, local copies, waits for them, and re-layouts, local(): mixed_rows.reshape(n_store, capacity, n_seq, width)  5.12 us
    all_to_all x1, starting transfers between devices, local(): lax.all_to_all(ret, ('seq', 'store'), split_axis=0, concat_axis=0, tiled=...  4.85 us
  transfers between devices with their start and end apart: 2, of which 2 were waited for; matrix products, arithmetic and copies ran while one was open for 0% of the time, Pallas kernels for 0%

profile of v5, /device:TPU:1, one launch (start us, length us, event | category | flops | bytes accessed | tf_op | source)
XLA Modules:
  0.0 219.3 jit_solution(8259919062144844247)
XLA Ops:
  0.0 0.7 fusion.38
  0.7 0.7 convert_bitcast_fusion.1
  1.4 1.0 copy.35
  2.5 1.0 copy.34
  3.7 1.6 copy.33
  5.3 0.7 copy.38
  6.0 0.7 gather_fusion
  6.7 0.3 select_bitcast_fusion
  7.1 0.5 pad_maximum_fusion
  7.6 51.2 %all_to_all.25 = bf16[129,32,384]{2,0,1:T(8,128)(2,1)S(1)} all-to-all(bf16[129,32,384]{2,0,1:T(8,128)(2,1)S(1)} %pad_maximum_fusion), channel_id=1, replica_groups=mesh['seq'=32,'store'=4] {'seq'}, dimensions={1} | all-to-all | bytes 6340608 | tf_op jit(solution)/shard_map/all_to_all | solution.py:138
  58.9 3.3 %select_reduce_fusion = s32[32,128]{0,1:T(8,128)S(1)} fusion(s32[32,128]{0,1:T(8,128)S(1)} %copy.40), kind=kOutput, calls=%fused_computation.18 | output fusion | flops 69201920 | bytes 32768 | tf_op jit(solution)/shard_map/jit(cumsum)/reduce_window_sum | solution.py:152
  62.5 0.3 reduce-window.9
  63.3 2.2 %fusion.39 = (bf16[32,128,128]{2,1,0:T(8,128)(2,1)}, bf16[32,128,128]{2,1,0:T(8,128)(2,1)}, bf16[32,128,128]{2,1,0:T(8,128)(2,1)}) fusion(bf16[32,129,384]{2,1,0:T(8,128)(2,1)S(1)} %bitcast.103), kind=kLoop, calls=%fused_computation.100 | loop fusion | bytes 6291456 | tf_op jit(solution)/shard_map/slice | solution.py:142
  65.6 0.7 fusion.3
  66.7 2.0 copy.39.qs_ref
  68.7 0.6 and_select_fusion.1
  69.3 40.2 %shard_map.73 = bf16[4096,128]{1,0:T(8,128)(2,1)} custom-call(s32[16]{0:T(128)} %get-tuple-element.15.lo_ref, s32[16]{0:T(128)} %get-tuple-element.14.full_ref, bf16[4096,128]{1,0:T(8,128)(2,1)} %bitcast.113, bf16[4096,128]{1,0:T(8,128)(2,1)} %bitcast.112, bf16[4096,128]{1,0:T(8,128)(2,1)} %bitcast.111, s32[4096,1]{1,0:T(8,128)} %copy.39.qs_ref), custom_call_target="tpu_custom_call" | custom-call | flops 6442450944 | bytes 4194304 | tf_op jit(solution)/shard_map/pallas_call | solution.py:83
  109.5 2.3 %convert_bitcast_fusion = bf16[256,32,128]{0,2,1:T(8,128)(2,1)S(1)} fusion(bf16[32,128,128]{2,1,0:T(8,128)(2,1)} %bitcast.110, s32[32,128]{1,0:T(8,128)S(1)} %get-tuple-element.11), kind=kOutput, calls=%fused_computation.15 | convolution fusion | flops 270532608 | bytes 3162112 | tf_op jit(solution)/shard_map/jmt,jtf->mjf/dot_general | solution.py:158
  111.8 3.1 %copy.43 = bf16[256,32,128]{2,1,0:T(8,128)(2,1)} copy(bf16[256,32,128]{0,2,1:T(8,128)(2,1)S(1)} %convert_bitcast_fusion) | data formatting | bytes 4194304 | tf_op jit(solution)/shard_map/convert_element_type | solution.py:163
  115.0 3.3 %pad_maximum_fusion.1 = bf16[128,65,128]{2,1,0:T(8,128)(2,1)} fusion(bf16[128,1,128]{2,1,0:T(2,128)(2,1)S(1)} %copy.44, bf16[128,64,128]{2,1,0:T(8,128)(2,1)} %bitcast.106), kind=kLoop, calls=%fused_computation.10 | loop fusion | flops 4259840 | bytes 4259840 | tf_op jit(solution)/shard_map/concatenate | solution.py:172
  118.2 7.9 %all-to-all-start.1 = ((bf16[128,65,128]{2,1,0:T(8,128)(2,1)}), bf16[128,65,128]{2,1,0:T(8,128)(2,1)S(1)}, u32[]{:S(2)}, u32[]{:S(2)}) async-start(bf16[128,65,128]{2,1,0:T(8,128)(2,1)} %pad_maximum_fusion.1), calls=%async_computation.1 | async-start | bytes 4718592 | tf_op jit(solution)/shard_map/all_to_all | solution.py:173
  126.2 33.3 %all-to-all-done.1 = bf16[128,65,128]{2,1,0:T(8,128)(2,1)S(1)} async-done(((bf16[128,65,128]{2,1,0:T(8,128)(2,1)}), bf16[128,65,128]{2,1,0:T(8,128)(2,1)S(1)}, u32[]{:S(2)}, u32[]{:S(2)}) %all-to-all-start.1) | async-done | bytes 2129952 | tf_op jit(solution)/shard_map/all_to_all | solution.py:173
  159.5 0.5 copy.45
  160.0 1.6 slice_bitcast_fusion
  161.6 0.4 copy.46
  162.0 12.1 %fusion.2 = bf16[256,4096]{1,0:T(8,128)(2,1)} fusion(bf16[1024,4096]{1,0:T(8,128)(2,1)} %param.13, bf16[32,8,32,128]{3,2,1,0:T(8,128)(2,1)S(1)} %bitcast.108, bf16[4096,1024]{1,0:T(8,128)(2,1)} %param.12, f32[1024]{0:T(1024)S(1)} %fusion.30, f32[256]{0:T(256)S(1)} %reshape.292), kind=kOutput, calls=%fused_computation.5 | convolution fusion | flops 4300996608 | bytes 20976640 | tf_op jit(solution)/shard_map/dot_general | solution.py:181
  174.1 5.1 %copy.47 = bf16[4,2,32,4096]{3,1,0,2:T(2,128)(2,1)} copy(bf16[4,2,32,4096]{3,2,1,0:T(8,128)(2,1)} %bitcast.109) | data formatting | bytes 4194304 | tf_op jit(solution)/shard_map/reshape | solution.py:184
  179.3 4.8 %all-to-all-start.2 = ((bf16[128,2,4096]{2,1,0:T(2,128)(2,1)}), bf16[128,2,4096]{2,1,0:T(2,128)(2,1)}, u32[]{:S(2)}, u32[]{:S(2)}) async-start(bf16[128,2,4096]{2,1,0:T(2,128)(2,1)} %bitcast.30), calls=%async_computation.2 | async-start | bytes 4194304 | tf_op jit(solution)/shard_map/all_to_all | solution.py:186
  184.2 0.2 reduce_window_sum.23
  184.6 29.8 %all-to-all-done.2 = bf16[128,2,4096]{2,1,0:T(2,128)(2,1)} async-done(((bf16[128,2,4096]{2,1,0:T(2,128)(2,1)}), bf16[128,2,4096]{2,1,0:T(2,128)(2,1)}, u32[]{:S(2)}, u32[]{:S(2)}) %all-to-all-start.2) | async-done | bytes 2097184 | tf_op jit(solution)/shard_map/all_to_all | solution.py:186
  214.4 2.7 %reshape.290 = bf16[256,4096]{1,0:T(8,128)(2,1)S(1)} reshape(bf16[128,2,4096]{2,1,0:T(2,128)(2,1)} %all-to-all-done.2) | data formatting | bytes 4194304 | tf_op jit(solution)/shard_map/reshape | solution.py:189
  217.2 2.2 gather_fusion.1
  (37 shorter events, 2.0 us)
Async XLA Ops:
  118.2 41.2 %all-to-all-start.1 = ((bf16[128,65,128]{2,1,0:T(8,128)(2,1)}), bf16[128,65,128]{2,1,0:T(8,128)(2,1)S(1)}, u32[]{:S(2)}, u32[]{:S(2)}) async-start(bf16[128,65,128]{2,1,0:T(8,128)(2,1)} %pad_maximum_fusion.1), calls=%async_computation.1 | async-start | bytes 4718592 | tf_op jit(solution)/shard_map/all_to_all | solution.py:173
  179.3 5.3 %copy-start = (s32[1,128]{1,0:T(1,128)S(1)}, s32[1,128]{1,0:T(1,128)}, u32[]{:S(2)}) copy-start(s32[1,128]{1,0:T(1,128)} %param.11) | copy-start | bytes 1540
  179.3 35.2 %all-to-all-start.2 = ((bf16[128,2,4096]{2,1,0:T(2,128)(2,1)}), bf16[128,2,4096]{2,1,0:T(2,128)(2,1)}, u32[]{:S(2)}, u32[]{:S(2)}) async-start(bf16[128,2,4096]{2,1,0:T(2,128)(2,1)} %bitcast.30), calls=%async_computation.2 | async-start | bytes 4194304 | tf_op jit(solution)/shard_map/all_to_all | solution.py:186

commit v6 on v5

--- a/solution.py
+++ b/solution.py
@@ -15,61 +15,61 @@
 MAX_DOC = 2048
 
 
-def _attn_kernel(lo_ref, full_ref, q_ref, k_ref, v_ref, qs_ref, o_ref, *, bq, bk, scale):
+def _attn_kernel(lo_ref, full_ref, q_ref, kt_ref, v_ref, qs_ref, o_ref, *, bq, bk, rc, scale):
     i = pl.program_id(0)
     lanes = 128
-    q = q_ref[...]
-    qs = qs_ref[...]
-    qpos = i * bq + lax.broadcasted_iota(jnp.int32, (bq, 1), 0)
     lo = lo_ref[i]
     mid = jnp.clip(full_ref[i], lo, i)
 
-    def raw(kb):
-        start = pl.multiple_of(kb * bk, bk)
-        k = k_ref[pl.ds(start, bk), :]
-        s = lax.dot_general(
-            q, k, (((1,), (1,)), ((), ())), preferred_element_type=jnp.float32
-        ) * scale
-        return s, start
-
-    def masked(kb):
-        s, start = raw(kb)
-        kpos = start + lax.broadcasted_iota(jnp.int32, (1, bk), 1)
-        ok = (kpos >= qs) & (kpos <= qpos)
-        return jnp.where(ok, s, jnp.float32(-1e30)), start
-
-    def fold_max(m, s):
-        for c in range(bk // lanes):
-            m = jnp.maximum(m, s[:, c * lanes : (c + 1) * lanes])
-        return m
-
-    m = jnp.full((bq, lanes), -1e30, jnp.float32)
-    m = lax.fori_loop(lo, mid, lambda kb, m: fold_max(m, masked(kb)[0]), m)
-    m = lax.fori_loop(mid, i, lambda kb, m: fold_max(m, raw(kb)[0]), m)
-    m = fold_max(m, masked(i)[0])
-    top = jnp.max(m, axis=1, keepdims=True)
-
-    def accum(carry, s, start):
-        tot, acc = carry
-        p = jnp.exp(s - top)
-        for c in range(bk // lanes):
-            tot = tot + p[:, c * lanes : (c + 1) * lanes]
-        v = v_ref[pl.ds(start, bk), :]
-        acc = acc + jnp.dot(p.astype(jnp.bfloat16), v, preferred_element_type=jnp.float32)
-        return tot, acc
-
-    carry = (jnp.zeros((bq, lanes), jnp.float32), jnp.zeros((bq, q.shape[1]), jnp.float32))
-    carry = lax.fori_loop(lo, mid, lambda kb, c: accum(c, *masked(kb)), carry)
-    carry = lax.fori_loop(mid, i, lambda kb, c: accum(c, *raw(kb)), carry)
-    tot, acc = accum(carry, *masked(i))
-    total = jnp.sum(tot, axis=1, keepdims=True)
-    o_ref[...] = (acc / total).astype(o_ref.dtype)
+    for r in range(bq // rc):
+        rows = pl.ds(r * rc, rc)
+        q = q_ref[rows, :]
+        qs = qs_ref[rows, :]
+        qpos = i * bq + r * rc + lax.broadcasted_iota(jnp.int32, (rc, 1), 0)
+
+        def raw(kb, q=q):
+            start = pl.multiple_of(kb * bk, bk)
+            s = jnp.dot(q, kt_ref[:, pl.ds(start, bk)], preferred_element_type=jnp.float32)
+            return s * scale, start
+
+        def masked(kb, raw=raw, qs=qs, qpos=qpos):
+            s, start = raw(kb)
+            kpos = start + lax.broadcasted_iota(jnp.int32, (1, bk), 1)
+            ok = (kpos >= qs) & (kpos <= qpos)
+            return jnp.where(ok, s, jnp.float32(-1e30)), start
+
+        def fold_max(m, s):
+            for c in range(bk // lanes):
+                m = jnp.maximum(m, s[:, c * lanes : (c + 1) * lanes])
+            return m
+
+        m = jnp.full((rc, lanes), -1e30, jnp.float32)
+        m = lax.fori_loop(lo, mid, lambda kb, m, f=masked: fold_max(m, f(kb)[0]), m)
+        m = lax.fori_loop(mid, i, lambda kb, m, f=raw: fold_max(m, f(kb)[0]), m)
+        m = fold_max(m, masked(i)[0])
+        top = jnp.max(m, axis=1, keepdims=True)
+
+        def accum(carry, s, start, top=top):
+            tot, acc = carry
+            p = jnp.exp(s - top)
+            for c in range(bk // lanes):
+                tot = tot + p[:, c * lanes : (c + 1) * lanes]
+            v = v_ref[pl.ds(start, bk), :]
+            acc = acc + jnp.dot(p.astype(jnp.bfloat16), v, preferred_element_type=jnp.float32)
+            return tot, acc
+
+        carry = (jnp.zeros((rc, lanes), jnp.float32), jnp.zeros((rc, q.shape[1]), jnp.float32))
+        carry = lax.fori_loop(lo, mid, lambda kb, c, f=masked, a=accum: a(c, *f(kb)), carry)
+        carry = lax.fori_loop(mid, i, lambda kb, c, f=raw, a=accum: a(c, *f(kb)), carry)
+        tot, acc = accum(carry, *masked(i))
+        total = jnp.sum(tot, axis=1, keepdims=True)
+        o_ref[rows, :] = (acc / total).astype(o_ref.dtype)
 
 
 def attend(queries, key_rows, value_rows, segments):
     length, dim = key_rows.shape
-    bq = min(256, length)
-    bk = min(256, length)
+    bq = min(512, length)
+    bk = min(512, length)
     n_q = length // bq
     pos = jnp.arange(length, dtype=jnp.int32)
     boundary = jnp.concatenate(
@@ -79,7 +79,7 @@
     lo_blk = doc_start[::bq] // bk
     full_blk = (doc_start[bq - 1 :: bq] + bk - 1) // bk
     q_rows = queries.reshape(length, dim)
-    kernel = functools.partial(_attn_kernel, bq=bq, bk=bk, scale=dim ** (-0.5))
+    kernel = functools.partial(_attn_kernel, bq=bq, bk=bk, rc=bq, scale=dim ** (-0.5))
     out = pl.pallas_call(
         kernel,
         out_shape=jax.ShapeDtypeStruct((length, dim), jnp.bfloat16),
@@ -88,7 +88,7 @@
             grid=(n_q,),
             in_specs=[
                 pl.BlockSpec((bq, dim), lambda i, lo, full: (i, 0)),
-                pl.BlockSpec((length, dim), lambda i, lo, full: (0, 0)),
+                pl.BlockSpec((dim, length), lambda i, lo, full: (0, 0)),
                 pl.BlockSpec((length, dim), lambda i, lo, full: (0, 0)),
                 pl.BlockSpec((bq, 1), lambda i, lo, full: (i, 0)),
             ],
@@ -99,7 +99,7 @@
             transcendentals=length * MAX_DOC,
             bytes_accessed=8 * length * dim,
         ),
-    )(lo_blk, full_blk, q_rows, key_rows, value_rows, doc_start.reshape(length, 1))
+    )(lo_blk, full_blk, q_rows, key_rows.T, value_rows, doc_start.reshape(length, 1))
     return out
 
 

time: 219 us -> 203 us (0.927)
  Pallas kernels: 40.2 us -> 24 us
  starting transfers between devices: 12.8 us -> 10.5 us
    pallas_call x1, Pallas kernels: 40.2 us -> 24 us  [attend(): pl.pallas_call(kernel, out_shape=jax.ShapeDtypeStruct((length, dim), jnp....]
    all_to_all x1, starting transfers between devices: 7.91 us -> 5.68 us  [local(): lax.all_to_all(send, ('seq', 'store'), split_axis=0, concat_axis=0, tiled...]
where the time goes in v6:
time: 203 us; the launch traced here: 202 us
  waiting for transfers between devices  63.1 us (31%)
  blocking collectives  51.2 us (25%)
  local copies, waits for them, and re-layouts  27.5 us (14%)
  Pallas kernels  24 us (12%)
  matrix products  15.2 us (7%)
  other arithmetic  10.6 us (5%)
  starting transfers between devices  10.5 us (5%)
    all_to_all x1, blocking collectives, local(): lax.all_to_all(payload, 'seq', split_axis=1, concat_axis=0, tiled=True)  51.2 us
    all_to_all x1, waiting for transfers between devices, local(): lax.all_to_all(send, ('seq', 'store'), split_axis=0, concat_axis=0, tiled...  33.3 us
    all_to_all x1, waiting for transfers between devices, local(): lax.all_to_all(ret, ('seq', 'store'), split_axis=0, concat_axis=0, tiled=...  29.8 us
    pallas_call x1, Pallas kernels, attend(): pl.pallas_call(kernel, out_shape=jax.ShapeDtypeStruct((length, dim), jnp....  24 us
    dot_general x1, matrix products, local(): jnp.dot(low, adapter_up, preferred_element_type=jnp.float32)  12.1 us
    all_to_all x1, starting transfers between devices, local(): lax.all_to_all(send, ('seq', 'store'), split_axis=0, concat_axis=0, tiled...  5.68 us
    reshape x1, local copies, waits for them, and re-layouts, local(): mixed_rows.reshape(n_store, capacity, n_seq, width)  5.12 us
    all_to_all x1, starting transfers between devices, local(): lax.all_to_all(ret, ('seq', 'store'), split_axis=0, concat_axis=0, tiled=...  4.85 us
  transfers between devices with their start and end apart: 2, of which 2 were waited for; matrix products, arithmetic and copies ran while one was open for 0% of the time, Pallas kernels for 0%

profile of v6, /device:TPU:1, one launch (start us, length us, event | category | flops | bytes accessed | tf_op | source)
XLA Modules:
  0.0 202.3 jit_solution(3248651830997870071)
XLA Ops:
  0.0 0.7 fusion.38
  0.7 0.7 convert_bitcast_fusion.1
  1.4 1.0 copy.38
  2.5 1.0 copy.37
  3.7 1.6 copy.36
  5.3 0.7 copy.41
  6.0 0.7 gather_fusion
  6.7 0.3 select_bitcast_fusion
  7.1 0.5 pad_maximum_fusion
  7.6 51.2 %all_to_all.25 = bf16[129,32,384]{2,0,1:T(8,128)(2,1)S(1)} all-to-all(bf16[129,32,384]{2,0,1:T(8,128)(2,1)S(1)} %pad_maximum_fusion), channel_id=1, replica_groups=mesh['seq'=32,'store'=4] {'seq'}, dimensions={1} | all-to-all | bytes 6340608 | tf_op jit(solution)/shard_map/all_to_all | solution.py:138
  58.9 3.3 %select_reduce_fusion = s32[32,128]{0,1:T(8,128)S(1)} fusion(s32[32,128]{0,1:T(8,128)S(1)} %copy.44), kind=kOutput, calls=%fused_computation.18 | output fusion | flops 69201920 | bytes 32768 | tf_op jit(solution)/shard_map/jit(cumsum)/reduce_window_sum | solution.py:152
  62.5 0.3 reduce-window.9
  63.3 2.2 %fusion.39 = (bf16[32,128,128]{2,1,0:T(8,128)(2,1)}, bf16[32,128,128]{2,1,0:T(8,128)(2,1)}, bf16[32,128,128]{2,1,0:T(8,128)(2,1)}) fusion(bf16[32,129,384]{2,1,0:T(8,128)(2,1)S(1)} %bitcast.104), kind=kLoop, calls=%fused_computation.100 | loop fusion | bytes 6291456 | tf_op jit(solution)/shard_map/slice | solution.py:142
  65.6 0.7 fusion.3
  66.8 1.3 copy.55
  68.1 2.0 copy.43.qs_ref
  70.1 0.6 and_select_fusion.1
  70.7 24.0 %shard_map.73 = bf16[4096,128]{1,0:T(8,128)(2,1)} custom-call(s32[8]{0:T(128)} %get-tuple-element.15.lo_ref, s32[8]{0:T(128)} %get-tuple-element.14.full_ref, bf16[4096,128]{1,0:T(8,128)(2,1)} %bitcast.115, bf16[128,4096]{1,0:T(8,128)(2,1)} %bitcast.113, bf16[4096,128]{1,0:T(8,128)(2,1)} %bitcast.114, s32[4096,1]{1,0:T(8,128)} %copy.43.qs_ref), custom_call_target="tpu_custom_call" | custom-call | flops 6442450944 | bytes 4194304 | tf_op jit(solution)/shard_map/pallas_call | solution.py:83
  94.7 2.3 %convert_bitcast_fusion = bf16[256,32,128]{0,2,1:T(8,128)(2,1)S(1)} fusion(bf16[32,128,128]{2,1,0:T(8,128)(2,1)} %bitcast.112, s32[32,128]{1,0:T(8,128)S(1)} %get-tuple-element.11), kind=kOutput, calls=%fused_computation.15 | convolution fusion | flops 270532608 | bytes 3162112 | tf_op jit(solution)/shard_map/jmt,jtf->mjf/dot_general | solution.py:158
  97.0 3.1 %copy.47 = bf16[256,32,128]{2,1,0:T(8,128)(2,1)} copy(bf16[256,32,128]{0,2,1:T(8,128)(2,1)S(1)} %convert_bitcast_fusion) | data formatting | bytes 4194304 | tf_op jit(solution)/shard_map/convert_element_type | solution.py:163
  100.2 3.3 %pad_maximum_fusion.1 = bf16[128,65,128]{2,1,0:T(8,128)(2,1)} fusion(bf16[128,1,128]{2,1,0:T(2,128)(2,1)S(1)} %copy.48, bf16[128,64,128]{2,1,0:T(8,128)(2,1)} %bitcast.107), kind=kLoop, calls=%fused_computation.10 | loop fusion | flops 4259840 | bytes 4259840 | tf_op jit(solution)/shard_map/concatenate | solution.py:172
  103.4 5.7 %all-to-all-start.1 = ((bf16[128,65,128]{2,1,0:T(8,128)(2,1)}), bf16[128,65,128]{2,1,0:T(8,128)(2,1)S(1)}, u32[]{:S(2)}, u32[]{:S(2)}) async-start(bf16[128,65,128]{2,1,0:T(8,128)(2,1)} %pad_maximum_fusion.1), calls=%async_computation.1 | async-start | bytes 4718592 | tf_op jit(solution)/shard_map/all_to_all | solution.py:173
  109.1 33.3 %all-to-all-done.1 = bf16[128,65,128]{2,1,0:T(8,128)(2,1)S(1)} async-done(((bf16[128,65,128]{2,1,0:T(8,128)(2,1)}), bf16[128,65,128]{2,1,0:T(8,128)(2,1)S(1)}, u32[]{:S(2)}, u32[]{:S(2)}) %all-to-all-start.1) | async-done | bytes 2129952 | tf_op jit(solution)/shard_map/all_to_all | solution.py:173
  142.4 0.5 copy.49
  143.0 1.6 slice_bitcast_fusion
  144.6 0.4 copy.50
  145.0 12.1 %fusion.2 = bf16[256,4096]{1,0:T(8,128)(2,1)} fusion(bf16[1024,4096]{1,0:T(8,128)(2,1)} %param.13, bf16[32,8,32,128]{3,2,1,0:T(8,128)(2,1)S(1)} %bitcast.110, bf16[4096,1024]{1,0:T(8,128)(2,1)} %param.12, f32[1024]{0:T(1024)S(1)} %fusion.30, f32[256]{0:T(256)S(1)} %reshape.292), kind=kOutput, calls=%fused_computation.5 | convolution fusion | flops 4300996608 | bytes 20976640 | tf_op jit(solution)/shard_map/dot_general | solution.py:181
  157.1 5.1 %copy.51 = bf16[4,2,32,4096]{3,1,0,2:T(2,128)(2,1)} copy(bf16[4,2,32,4096]{3,2,1,0:T(8,128)(2,1)} %bitcast.111) | data formatting | bytes 4194304 | tf_op jit(solution)/shard_map/reshape | solution.py:184
  162.2 4.8 %all-to-all-start.2 = ((bf16[128,2,4096]{2,1,0:T(2,128)(2,1)}), bf16[128,2,4096]{2,1,0:T(2,128)(2,1)}, u32[]{:S(2)}, u32[]{:S(2)}) async-start(bf16[128,2,4096]{2,1,0:T(2,128)(2,1)} %bitcast.31), calls=%async_computation.2 | async-start | bytes 4194304 | tf_op jit(solution)/shard_map/all_to_all | solution.py:186
  167.6 29.8 %all-to-all-done.2 = bf16[128,2,4096]{2,1,0:T(2,128)(2,1)} async-done(((bf16[128,2,4096]{2,1,0:T(2,128)(2,1)}), bf16[128,2,4096]{2,1,0:T(2,128)(2,1)}, u32[]{:S(2)}, u32[]{:S(2)}) %all-to-all-start.2) | async-done | bytes 2097184 | tf_op jit(solution)/shard_map/all_to_all | solution.py:186
  197.4 2.7 %reshape.290 = bf16[256,4096]{1,0:T(8,128)(2,1)S(1)} reshape(bf16[128,2,4096]{2,1,0:T(2,128)(2,1)} %all-to-all-done.2) | data formatting | bytes 4194304 | tf_op jit(solution)/shard_map/reshape | solution.py:189
  200.1 2.2 %gather_fusion.1 = bf16[128,4096]{1,0:T(8,128)(2,1)} fusion(bf16[256,4096]{1,0:T(8,128)(2,1)S(1)} %reshape.290, s32[1024]{0:T(1024)S(1)} %pad_clamp_fusion), kind=kCustom, calls=%fused_computation.1 | custom fusion | bytes 2097664 | tf_op jit(solution)/shard_map/gather | solution.py:189
  (40 shorter events, 2.2 us)
Async XLA Ops:
  65.6 1.2 copy-start
  103.4 39.0 %all-to-all-start.1 = ((bf16[128,65,128]{2,1,0:T(8,128)(2,1)}), bf16[128,65,128]{2,1,0:T(8,128)(2,1)S(1)}, u32[]{:S(2)}, u32[]{:S(2)}) async-start(bf16[128,65,128]{2,1,0:T(8,128)(2,1)} %pad_maximum_fusion.1), calls=%async_computation.1 | async-start | bytes 4718592 | tf_op jit(solution)/shard_map/all_to_all | solution.py:173
  162.2 5.3 %copy-start.1 = (s32[1,128]{1,0:T(1,128)S(1)}, s32[1,128]{1,0:T(1,128)}, u32[]{:S(2)}) copy-start(s32[1,128]{1,0:T(1,128)} %param.11) | copy-start | bytes 1540
  162.2 35.2 %all-to-all-start.2 = ((bf16[128,2,4096]{2,1,0:T(2,128)(2,1)}), bf16[128,2,4096]{2,1,0:T(2,128)(2,1)}, u32[]{:S(2)}, u32[]{:S(2)}) async-start(bf16[128,2,4096]{2,1,0:T(2,128)(2,1)} %bitcast.31), calls=%async_computation.2 | async-start | bytes 4194304 | tf_op jit(solution)/shard_map/all_to_all | solution.py:186

commit v7 on v6

--- a/solution.py
+++ b/solution.py
@@ -13,9 +13,10 @@
 RANK = 64
 EXP_DEV = 16
 MAX_DOC = 2048
-
-
-def _attn_kernel(lo_ref, full_ref, q_ref, kt_ref, v_ref, qs_ref, o_ref, *, bq, bk, rc, scale):
+N_DOCS = 4
+
+
+def _attn_kernel(lo_ref, full_ref, bnd_ref, q_ref, kt_ref, v_ref, o_ref, *, bq, bk, rc, scale):
     i = pl.program_id(0)
     lanes = 128
     lo = lo_ref[i]
@@ -24,8 +25,10 @@
     for r in range(bq // rc):
         rows = pl.ds(r * rc, rc)
         q = q_ref[rows, :]
-        qs = qs_ref[rows, :]
         qpos = i * bq + r * rc + lax.broadcasted_iota(jnp.int32, (rc, 1), 0)
+        qs = jnp.zeros((rc, 1), jnp.int32)
+        for c in range(N_DOCS - 1):
+            qs = jnp.where(qpos >= bnd_ref[c], bnd_ref[c], qs)
 
         def raw(kb, q=q):
             start = pl.multiple_of(kb * bk, bk)
@@ -71,35 +74,40 @@
     bq = min(512, length)
     bk = min(512, length)
     n_q = length // bq
-    pos = jnp.arange(length, dtype=jnp.int32)
-    boundary = jnp.concatenate(
-        [jnp.ones((1,), jnp.bool_), segments[1:] != segments[:-1]]
-    )
-    doc_start = lax.cummax(jnp.where(boundary, pos, 0), axis=0)
-    lo_blk = doc_start[::bq] // bk
-    full_blk = (doc_start[bq - 1 :: bq] + bk - 1) // bk
+    bounds = jnp.sum(
+        segments[None, :] < jnp.arange(1, N_DOCS, dtype=jnp.int32)[:, None], axis=1
+    ).astype(jnp.int32)
+
+    def doc_start_at(t):
+        first = jnp.zeros_like(t)
+        for c in range(N_DOCS - 1):
+            first = jnp.where(t >= bounds[c], bounds[c], first)
+        return first
+
+    firsts = jnp.arange(n_q, dtype=jnp.int32) * bq
+    lo_blk = doc_start_at(firsts) // bk
+    full_blk = (doc_start_at(firsts + bq - 1) + bk - 1) // bk
     q_rows = queries.reshape(length, dim)
     kernel = functools.partial(_attn_kernel, bq=bq, bk=bk, rc=bq, scale=dim ** (-0.5))
     out = pl.pallas_call(
         kernel,
         out_shape=jax.ShapeDtypeStruct((length, dim), jnp.bfloat16),
         grid_spec=pltpu.PrefetchScalarGridSpec(
-            num_scalar_prefetch=2,
+            num_scalar_prefetch=3,
             grid=(n_q,),
             in_specs=[
-                pl.BlockSpec((bq, dim), lambda i, lo, full: (i, 0)),
-                pl.BlockSpec((dim, length), lambda i, lo, full: (0, 0)),
-                pl.BlockSpec((length, dim), lambda i, lo, full: (0, 0)),
-                pl.BlockSpec((bq, 1), lambda i, lo, full: (i, 0)),
+                pl.BlockSpec((bq, dim), lambda i, lo, full, bnd: (i, 0)),
+                pl.BlockSpec((dim, length), lambda i, lo, full, bnd: (0, 0)),
+                pl.BlockSpec((length, dim), lambda i, lo, full, bnd: (0, 0)),
             ],
-            out_specs=pl.BlockSpec((bq, dim), lambda i, lo, full: (i, 0)),
+            out_specs=pl.BlockSpec((bq, dim), lambda i, lo, full, bnd: (i, 0)),
         ),
         cost_estimate=pl.CostEstimate(
             flops=6 * length * MAX_DOC * dim,
             transcendentals=length * MAX_DOC,
             bytes_accessed=8 * length * dim,
         ),
-    )(lo_blk, full_blk, q_rows, key_rows.T, value_rows, doc_start.reshape(length, 1))
+    )(lo_blk, full_blk, bounds, q_rows, key_rows.T, value_rows)
     return out
 
 
@@ -123,9 +131,11 @@
     )
     kv_send = jnp.take(paired, (jnp.arange(n_seq) * heads_here) // group, axis=1)
     chosen = route_ids[0]
-    meta = jnp.concatenate(
-        [segment_ids[0], chosen // EXP_DEV, chosen % EXP_DEV]
-    ).astype(jnp.bfloat16)
+    owners = chosen // EXP_DEV
+    one_hot = (owners[:, None] == jnp.arange(devices, dtype=jnp.int32)[None, :]).astype(jnp.int32)
+    rank = jnp.sum(jnp.cumsum(one_hot, axis=0) * one_hot, axis=1) - 1
+    code = owners * capacity + rank
+    meta = jnp.concatenate([segment_ids[0], code, chosen % EXP_DEV]).astype(jnp.bfloat16)
     meta_w = feat + 2 * HEAD_DIM
     meta = jnp.pad(meta, (0, meta_w - meta.shape[0]))
     payload = jnp.concatenate(
@@ -142,18 +152,12 @@
     v_all = got_in[:, :tok_rows, feat + HEAD_DIM :].reshape(length, HEAD_DIM)
     meta_all = got_in[:, tok_rows, : 3 * tok_rows].astype(jnp.int32)
     segments = meta_all[:, :tok_rows].reshape(length)
-    owner_all = meta_all[:, tok_rows : 2 * tok_rows]
+    code_all = meta_all[:, tok_rows : 2 * tok_rows]
     adapter_all = meta_all[:, 2 * tok_rows :]
 
     context = attend(q_all, k_all, v_all, segments).reshape(length, feat)
 
-    def ranks(owner_rows):
-        one_hot = (owner_rows[..., None] == jnp.arange(devices, dtype=jnp.int32)).astype(jnp.int32)
-        return jnp.sum(jnp.cumsum(one_hot, axis=-2) * one_hot, axis=-1) - 1
-
-    pick = (
-        owner_all * capacity + ranks(owner_all)
-    )[:, None, :] == jnp.arange(devices * capacity, dtype=jnp.int32)[None, :, None]
+    pick = code_all[:, None, :] == jnp.arange(devices * capacity, dtype=jnp.int32)[None, :, None]
     pick = pick.astype(jnp.bfloat16)
     send = jnp.einsum(
         "jmt,jtf->mjf",
@@ -172,21 +176,21 @@
     send = jnp.concatenate([send, tag_row[:, None, :]], axis=1)
     got = lax.all_to_all(send, ("seq", "store"), split_axis=0, concat_axis=0, tiled=True)
     got = got.reshape(n_seq, n_store, slots + 1, feat)
-    rows = jnp.transpose(got[:, :, :slots, :], (1, 2, 0, 3)).reshape(n_store * slots, width)
-    row_tags = got[0, :, slots, :slots].reshape(n_store * slots, 1).astype(jnp.float32)
+    rows = jnp.transpose(
+        got[:, :, :slots, :].reshape(n_seq, n_store, capacity, n_seq, feat), (3, 1, 2, 0, 4)
+    ).reshape(n_store * slots, width)
+    row_tags = jnp.transpose(
+        got[0, :, slots, :slots].reshape(n_store, capacity, n_seq), (2, 0, 1)
+    ).reshape(n_store * slots, 1).astype(jnp.float32)
 
     low = jnp.dot(rows, adapter_down, preferred_element_type=jnp.float32)
     lane_owner = (jnp.arange(low.shape[1], dtype=jnp.int32) // RANK).astype(jnp.float32)
     low = jnp.where(row_tags == lane_owner[None, :], low, 0.0).astype(jnp.bfloat16)
     delta = jnp.dot(low, adapter_up, preferred_element_type=jnp.float32).astype(jnp.bfloat16)
     mixed_rows = (rows.astype(jnp.float32) + delta.astype(jnp.float32)).astype(jnp.bfloat16)
-    ret = jnp.transpose(
-        mixed_rows.reshape(n_store, capacity, n_seq, width), (2, 0, 1, 3)
-    ).reshape(devices, capacity, width)
+    ret = mixed_rows.reshape(devices, capacity, width)
     back = lax.all_to_all(ret, ("seq", "store"), split_axis=0, concat_axis=0, tiled=True)
-    owners = chosen // EXP_DEV
-    placed = owners * capacity + ranks(owners)
-    mixed = back.reshape(devices * capacity, width)[placed]
+    mixed = back[owners, rank]
     return mixed[None]
 
 

time: 203 us -> 199 us (0.980)
  blocking collectives: 51.2 us -> 0 us
  waiting for transfers between devices: 63.1 us -> 105 us
  starting transfers between devices: 10.5 us -> 19.7 us
  local copies, waits for them, and re-layouts: 27.5 us -> 24 us
  other arithmetic: 10.6 us -> 8.51 us
    all_to_all x1 -> x0, blocking collectives: 51.2 us -> none  [local(): lax.all_to_all(payload, 'seq', split_axis=1, concat_axis=0, tiled=True)]
    all_to_all x0 -> x1, waiting for transfers between devices: none -> 41.5 us  [local(): lax.all_to_all(payload, 'seq', split_axis=1, concat_axis=0, tiled=True)]
    all_to_all x0 -> x1, starting transfers between devices: none -> 9.42 us  [local(): lax.all_to_all(payload, 'seq', split_axis=1, concat_axis=0, tiled=True)]
    another operation x7 -> x2, other arithmetic: 4.66 us -> 0.18 us  [the longest x1 0.17 us: local(): rank = jnp.sum(jnp.cumsum(one_hot, axis=0) * one_hot, axis=1) - 1]
    reshape x2 -> x1, local copies, waits for them, and re-layouts: 7.87 us -> 4.4 us  [local(): ret = mixed_rows.reshape(devices, capacity, width)]
    select_n x3 -> x2, other arithmetic: 0.68 us -> 3.1 us  [the longest x1 2.43 us: attend(): full_blk = (doc_start_at(firsts + bq - 1) + bk - 1) // bk]
    another operation x2 -> x0, local copies, waits for them, and re-layouts: 2.11 us -> none  [the longest x1 2 us: attend(): doc_start = lax.cummax(jnp.where(boundary, pos, 0), axis=0)]
  transfers between devices with their start and end apart: 2 -> 3, of which waited for: 2 -> 3; matrix products, arithmetic and copies ran while one was open for 0% -> 0% of each run, Pallas kernels for 0% -> 0%
where the time goes in v7:
time: 199 us; the launch traced here: 198 us
  waiting for transfers between devices  105 us (53%)
  local copies, waits for them, and re-layouts  24 us (12%)
  Pallas kernels  24 us (12%)
  starting transfers between devices  19.7 us (10%)
  matrix products  16.6 us (8%)
  other arithmetic  8.51 us (4%)
    all_to_all x1, waiting for transfers between devices, local(): lax.all_to_all(payload, 'seq', split_axis=1, concat_axis=0, tiled=True)  41.5 us
    all_to_all x1, waiting for transfers between devices, local(): lax.all_to_all(send, ('seq', 'store'), split_axis=0, concat_axis=0, tiled...  33.4 us
    all_to_all x1, waiting for transfers between devices, local(): lax.all_to_all(ret, ('seq', 'store'), split_axis=0, concat_axis=0, tiled=...  30.5 us
    pallas_call x1, Pallas kernels, attend(): pl.pallas_call(kernel, out_shape=jax.ShapeDtypeStruct((length, dim), jnp....  24 us
    dot_general x1, matrix products, local(): jnp.dot(low, adapter_up, preferred_element_type=jnp.float32)  12.2 us
    all_to_all x1, starting transfers between devices, local(): lax.all_to_all(payload, 'seq', split_axis=1, concat_axis=0, tiled=True)  9.42 us
    all_to_all x1, starting transfers between devices, local(): lax.all_to_all(send, ('seq', 'store'), split_axis=0, concat_axis=0, tiled...  6.43 us
    reshape x1, local copies, waits for them, and re-layouts, local(): ret = mixed_rows.reshape(devices, capacity, width)  4.4 us
  transfers between devices with their start and end apart: 3, of which 3 were waited for; matrix products, arithmetic and copies ran while one was open for 0% of the time, Pallas kernels for 0%

profile of v7, /device:TPU:1, one launch (start us, length us, event | category | flops | bytes accessed | tf_op | source)
XLA Modules:
  0.0 198.5 jit_solution(978921548253925995)
XLA Ops:
  0.0 0.7 and_select_fusion.4
  0.8 0.2 reduce_window_sum.11
  1.0 0.2 select_reduce_fusion
  1.1 0.7 convert_bitcast_fusion.1
  1.8 1.0 copy.30
  3.0 1.0 copy.31
  4.2 1.6 copy.29
  5.8 0.7 copy.34
  6.5 0.7 gather_fusion
  7.2 0.3 select_bitcast_fusion
  7.5 2.0 pad_maximum_fusion
  9.5 9.4 %all-to-all-start = ((bf16[129,32,384]{2,0,1:T(8,128)(2,1)}), bf16[129,32,384]{2,0,1:T(8,128)(2,1)S(1)}, u32[]{:S(2)}, u32[]{:S(2)}) async-start(bf16[129,32,384]{2,0,1:T(8,128)(2,1)} %pad_maximum_fusion), calls=%async_computation | async-start | bytes 6684672 | tf_op jit(solution)/shard_map/all_to_all | solution.py:148
  18.9 41.5 %all-to-all-done = bf16[129,32,384]{2,0,1:T(8,128)(2,1)S(1)} async-done(((bf16[129,32,384]{2,0,1:T(8,128)(2,1)}), bf16[129,32,384]{2,0,1:T(8,128)(2,1)S(1)}, u32[]{:S(2)}, u32[]{:S(2)}) %all-to-all-start) | async-done | bytes 3170336 | tf_op jit(solution)/shard_map/all_to_all | solution.py:148
  60.5 2.2 %fusion.41 = (bf16[32,128,128]{2,1,0:T(8,128)(2,1)}, bf16[32,128,128]{2,1,0:T(8,128)(2,1)}, bf16[32,128,128]{2,1,0:T(8,128)(2,1)}) fusion(bf16[32,129,384]{2,1,0:T(8,128)(2,1)S(1)} %bitcast.105), kind=kLoop, calls=%fused_computation.102 | loop fusion | bytes 6291456 | tf_op jit(solution)/shard_map/slice | solution.py:152
  62.7 0.2 convert_reduce_fusion.bnd_ref
  62.9 0.6 fusion.42
  63.6 2.3 %copy.44 = bf16[4096,128]{0,1:T(8,128)(2,1)} copy(bf16[4096,128]{1,0:T(8,128)(2,1)} %bitcast.111) | data formatting | bytes 2097152 | tf_op jit(solution)/shard_map/reshape | solution.py:151
  65.8 2.4 %and_select_fusion.1 = (s32[8]{0:T(128)}, s32[8]{0:T(128)}) fusion(s32[]{:T(128)} %bitcast.13, s32[]{:T(128)} %bitcast.12, s32[]{:T(128)} %bitcast.11), kind=kLoop, calls=%fused_computation.55 | loop fusion | flops 360 | bytes 76 | tf_op jit(solution)/shard_map/jit(floor_divide)/jit(_where)/select_n | solution.py:89
  68.3 24.0 %shard_map.73 = bf16[4096,128]{1,0:T(8,128)(2,1)} custom-call(s32[8]{0:T(128)} %get-tuple-element.17.lo_ref, s32[8]{0:T(128)} %get-tuple-element.16.full_ref, s32[3]{0:T(128)} %copy-done, bf16[4096,128]{1,0:T(8,128)(2,1)} %bitcast.116, bf16[128,4096]{1,0:T(8,128)(2,1)} %bitcast.114, bf16[4096,128]{1,0:T(8,128)(2,1)} %bitcast.115), custom_call_target="tpu_custom_call" | custom-call | flops 6442450944 | bytes 4194304 | tf_op jit(solution)/shard_map/pallas_call | solution.py:92
  92.3 3.7 %convert_bitcast_fusion = bf16[256,32,128]{0,2,1:T(8,128)(2,1)} fusion(bf16[32,128,128]{2,1,0:T(8,128)(2,1)} %bitcast.113, s32[32,128]{1,0:T(8,128)S(1)} %get-tuple-element.10), kind=kOutput, calls=%fused_computation.14 | convolution fusion | flops 270532608 | bytes 3162112 | tf_op jit(solution)/shard_map/jmt,jtf->mjf/dot_general | solution.py:162
  96.0 3.4 %copy.37 = bf16[256,32,128]{2,1,0:T(8,128)(2,1)S(1)} copy(bf16[256,32,128]{0,2,1:T(8,128)(2,1)} %convert_bitcast_fusion) | data formatting | bytes 4194304 | tf_op jit(solution)/shard_map/convert_element_type | solution.py:167
  99.4 0.7 fusion.3
  100.5 1.7 pad_maximum_fusion.1
  102.2 6.4 %all-to-all-start.1 = ((bf16[128,65,128]{2,1,0:T(8,128)(2,1)}), bf16[128,65,128]{2,1,0:T(8,128)(2,1)S(1)}, u32[]{:S(2)}, u32[]{:S(2)}) async-start(bf16[128,65,128]{2,1,0:T(8,128)(2,1)} %pad_maximum_fusion.1), calls=%async_computation.1 | async-start | bytes 4718592 | tf_op jit(solution)/shard_map/all_to_all | solution.py:177
  108.6 33.4 %all-to-all-done.1 = bf16[128,65,128]{2,1,0:T(8,128)(2,1)S(1)} async-done(((bf16[128,65,128]{2,1,0:T(8,128)(2,1)}), bf16[128,65,128]{2,1,0:T(8,128)(2,1)S(1)}, u32[]{:S(2)}, u32[]{:S(2)}) %all-to-all-start.1) | async-done | bytes 2129952 | tf_op jit(solution)/shard_map/all_to_all | solution.py:177
  142.0 0.3 slice.68
  142.4 1.4 copy.39
  144.1 12.2 %fusion.2 = bf16[256,4096]{1,0:T(8,128)(2,1)} fusion(bf16[1024,4096]{1,0:T(8,128)(2,1)} %param.13, bf16[32,8,32,128]{3,2,1,0:T(8,128)(2,1)S(1)} %bitcast.112, bf16[4096,1024]{1,0:T(8,128)(2,1)} %param.12, f32[1024]{0:T(1024)S(1)} %fusion.27, f32[256]{0:T(256)S(1)} %reshape.259), kind=kOutput, calls=%fused_computation.5 | convolution fusion | flops 4300996608 | bytes 20976640 | tf_op jit(solution)/shard_map/dot_general | solution.py:189
  156.2 4.4 %reshape.257 = bf16[128,2,4096]{2,1,0:T(2,128)(2,1)} reshape(bf16[256,4096]{1,0:T(8,128)(2,1)} %fusion.2) | data formatting | bytes 4194304 | tf_op jit(solution)/shard_map/reshape | solution.py:191
  160.6 3.8 %all-to-all-start.2 = ((bf16[128,2,4096]{2,1,0:T(2,128)(2,1)}), bf16[128,2,4096]{2,1,0:T(2,128)(2,1)S(1)}, u32[]{:S(2)}, u32[]{:S(2)}) async-start(bf16[128,2,4096]{2,1,0:T(2,128)(2,1)} %reshape.257), calls=%async_computation.2 | async-start | bytes 4194304 | tf_op jit(solution)/shard_map/all_to_all | solution.py:192
  164.5 30.5 %all-to-all-done.2 = bf16[128,2,4096]{2,1,0:T(2,128)(2,1)S(1)} async-done(((bf16[128,2,4096]{2,1,0:T(2,128)(2,1)}), bf16[128,2,4096]{2,1,0:T(2,128)(2,1)S(1)}, u32[]{:S(2)}, u32[]{:S(2)}) %all-to-all-start.2) | async-done | bytes 2097184 | tf_op jit(solution)/shard_map/all_to_all | solution.py:192
  195.0 3.5 %gather_fusion.1 = bf16[128,4096]{1,0:T(8,128)(2,1)} fusion(bf16[128,2,4096]{2,1,0:T(2,128)(2,1)S(1)} %all-to-all-done.2, s32[128]{0:T(128)S(1)} %fusion.39), kind=kCustom, calls=%fused_computation.1 | custom fusion | bytes 2098176 | tf_op jit(solution)/shard_map/gather | solution.py:193
  (29 shorter events, 1.2 us)
Async XLA Ops:
  9.5 50.9 %all-to-all-start = ((bf16[129,32,384]{2,0,1:T(8,128)(2,1)}), bf16[129,32,384]{2,0,1:T(8,128)(2,1)S(1)}, u32[]{:S(2)}, u32[]{:S(2)}) async-start(bf16[129,32,384]{2,0,1:T(8,128)(2,1)} %pad_maximum_fusion), calls=%async_computation | async-start | bytes 6684672 | tf_op jit(solution)/shard_map/all_to_all | solution.py:148
  62.9 5.3 %copy-start = (s32[3]{0:T(128)}, s32[3]{0:T(128)S(1)}, u32[]{:S(2)}) copy-start(s32[3]{0:T(128)S(1)} %convert_reduce_fusion.bnd_ref) | copy-start | bytes 40
  102.2 39.9 %all-to-all-start.1 = ((bf16[128,65,128]{2,1,0:T(8,128)(2,1)}), bf16[128,65,128]{2,1,0:T(8,128)(2,1)S(1)}, u32[]{:S(2)}, u32[]{:S(2)}) async-start(bf16[128,65,128]{2,1,0:T(8,128)(2,1)} %pad_maximum_fusion.1), calls=%async_computation.1 | async-start | bytes 4718592 | tf_op jit(solution)/shard_map/all_to_all | solution.py:177
  156.2 8.2 %copy-start.1 = (s32[1,128]{1,0:T(1,128)S(1)}, s32[1,128]{1,0:T(1,128)}, u32[]{:S(2)}) copy-start(s32[1,128]{1,0:T(1,128)} %param.11) | copy-start | bytes 1540
  160.6 34.4 %all-to-all-start.2 = ((bf16[128,2,4096]{2,1,0:T(2,128)(2,1)}), bf16[128,2,4096]{2,1,0:T(2,128)(2,1)S(1)}, u32[]{:S(2)}, u32[]{:S(2)}) async-start(bf16[128,2,4096]{2,1,0:T(2,128)(2,1)} %reshape.257), calls=%async_computation.2 | async-start | bytes 4194304 | tf_op jit(solution)/shard_map/all_to_all | solution.py:192

commit v8 on v7

--- a/solution.py
+++ b/solution.py
@@ -124,33 +124,47 @@
     capacity = max(2, 2 * tok_rows // devices)
     slots = n_seq * capacity
 
+    half = tok_rows // 2
     q_send = queries[0].reshape(tok_rows, n_seq, feat)
     paired = jnp.concatenate(
         [keys[0].reshape(tok_rows, KV_HEADS, HEAD_DIM), values[0].reshape(tok_rows, KV_HEADS, HEAD_DIM)],
         axis=2,
     )
-    kv_send = jnp.take(paired, (jnp.arange(n_seq) * heads_here) // group, axis=1)
+    halves = jnp.transpose(paired.reshape(2, half, KV_HEADS, 2 * HEAD_DIM), (0, 2, 1, 3)).reshape(
+        2 * KV_HEADS, half, 2 * HEAD_DIM
+    )
+    dest = jnp.arange(n_seq, dtype=jnp.int32)
+    kv_send = jnp.take(halves, (dest % 2) * KV_HEADS + (dest * heads_here) // group, axis=0)
+    kv_send = jnp.transpose(kv_send.reshape(n_seq, tok_rows, HEAD_DIM), (1, 0, 2))
     chosen = route_ids[0]
     owners = chosen // EXP_DEV
     one_hot = (owners[:, None] == jnp.arange(devices, dtype=jnp.int32)[None, :]).astype(jnp.int32)
     rank = jnp.sum(jnp.cumsum(one_hot, axis=0) * one_hot, axis=1) - 1
     code = owners * capacity + rank
     meta = jnp.concatenate([segment_ids[0], code, chosen % EXP_DEV]).astype(jnp.bfloat16)
-    meta_w = feat + 2 * HEAD_DIM
-    meta = jnp.pad(meta, (0, meta_w - meta.shape[0]))
+    meta_w = feat + HEAD_DIM
+    meta_rows = -(-meta.shape[0] // meta_w)
+    meta = jnp.pad(meta, (0, meta_rows * meta_w - meta.shape[0])).reshape(meta_rows, meta_w)
     payload = jnp.concatenate(
         [
             jnp.concatenate([q_send, kv_send], axis=2),
-            jnp.broadcast_to(meta[None, None, :], (1, n_seq, meta_w)),
+            jnp.broadcast_to(meta[:, None, :], (meta_rows, n_seq, meta_w)),
         ],
         axis=0,
     )
     got_in = lax.all_to_all(payload, "seq", split_axis=1, concat_axis=0, tiled=True)
-    got_in = got_in.reshape(n_seq, tok_rows + 1, meta_w)
+    got_in = got_in.reshape(n_seq, tok_rows + meta_rows, meta_w)
     q_all = got_in[:, :tok_rows, :feat].reshape(length, heads_here, HEAD_DIM)
-    k_all = got_in[:, :tok_rows, feat : feat + HEAD_DIM].reshape(length, HEAD_DIM)
-    v_all = got_in[:, :tok_rows, feat + HEAD_DIM :].reshape(length, HEAD_DIM)
-    meta_all = got_in[:, tok_rows, : 3 * tok_rows].astype(jnp.int32)
+    kv_mine = got_in[:, :tok_rows, feat:].reshape(n_seq, half, 2 * HEAD_DIM)
+    kv_other = lax.ppermute(kv_mine, "seq", [(i, i ^ 1) for i in range(n_seq)])
+    even = lax.axis_index("seq") % 2 == 0
+    kv_all = jnp.stack(
+        [jnp.where(even, kv_mine, kv_other), jnp.where(even, kv_other, kv_mine)], axis=1
+    ).reshape(length, 2 * HEAD_DIM)
+    k_all = kv_all[:, :HEAD_DIM]
+    v_all = kv_all[:, HEAD_DIM:]
+    meta_all = got_in[:, tok_rows:, :].reshape(n_seq, meta_rows * meta_w)[:, : 3 * tok_rows]
+    meta_all = meta_all.astype(jnp.int32)
     segments = meta_all[:, :tok_rows].reshape(length)
     code_all = meta_all[:, tok_rows : 2 * tok_rows]
     adapter_all = meta_all[:, 2 * tok_rows :]

time: 199 us -> 184 us (0.925)
  waiting for transfers between devices: 105 us -> 93.8 us
  local copies, waits for them, and re-layouts: 24 us -> 22 us
    all_to_all x1, waiting for transfers between devices: 41.5 us -> 30.1 us  [local(): lax.all_to_all(payload, 'seq', split_axis=1, concat_axis=0, tiled=True)]
    unnamed x8, local copies, waits for them, and re-layouts: 3.67 us -> 0.42 us
    all_to_all x1, starting transfers between devices: 6.43 us -> 3.77 us  [local(): lax.all_to_all(send, ('seq', 'store'), split_axis=0, concat_axis=0, tiled...]
  transfers between devices with their start and end apart: 3 -> 4, of which waited for: 3 -> 3; matrix products, arithmetic and copies ran while one was open for 0% -> 2% of each run, Pallas kernels for 0% -> 0%
where the time goes in v8:
time: 184 us; the launch traced here: 185 us
  waiting for transfers between devices  93.8 us (51%)
  Pallas kernels  25 us (14%)
  local copies, waits for them, and re-layouts  22 us (12%)
  starting transfers between devices  18.8 us (10%)
  matrix products  15.2 us (8%)
  other arithmetic  10 us (5%)
    all_to_all x1, waiting for transfers between devices, local(): lax.all_to_all(send, ('seq', 'store'), split_axis=0, concat_axis=0, tiled...  33.1 us
    all_to_all x1, waiting for transfers between devices, local(): lax.all_to_all(ret, ('seq', 'store'), split_axis=0, concat_axis=0, tiled=...  30.6 us
    all_to_all x1, waiting for transfers between devices, local(): lax.all_to_all(payload, 'seq', split_axis=1, concat_axis=0, tiled=True)  30.1 us
    pallas_call x1, Pallas kernels, attend(): pl.pallas_call(kernel, out_shape=jax.ShapeDtypeStruct((length, dim), jnp....  25 us
    dot_general x1, matrix products, local(): jnp.dot(low, adapter_up, preferred_element_type=jnp.float32)  12.2 us
    all_to_all x1, starting transfers between devices, local(): lax.all_to_all(payload, 'seq', split_axis=1, concat_axis=0, tiled=True)  9.42 us
    reshape x1, local copies, waits for them, and re-layouts, local(): ret = mixed_rows.reshape(devices, capacity, width)  4.38 us
    all_to_all x1, starting transfers between devices, local(): lax.all_to_all(ret, ('seq', 'store'), split_axis=0, concat_axis=0, tiled=...  3.82 us
  transfers between devices with their start and end apart: 4, of which 3 were waited for; matrix products, arithmetic and copies ran while one was open for 2% of the time, Pallas kernels for 0%

profile of v8, /device:TPU:1, one launch (start us, length us, event | category | flops | bytes accessed | tf_op | source)
XLA Modules:
  0.0 185.2 jit_solution(9610934489114340140)
XLA Ops:
  0.0 0.7 convert_bitcast_fusion.1
  0.7 0.7 and_select_fusion.4
  1.8 0.9 concatenate.24
  2.8 0.9 concatenate.25
  3.9 0.6 gather_fusion
  4.5 0.4 gather.10
  5.1 0.2 copy.41
  5.4 0.4 copy.30
  6.0 1.7 pad_maximum_fusion.1
  7.6 9.4 %all-to-all-start = ((bf16[130,32,256]{2,0,1:T(8,128)(2,1)}), bf16[130,32,256]{2,0,1:T(8,128)(2,1)S(1)}, u32[]{:S(2)}, u32[]{:S(2)}) async-start(bf16[130,32,256]{2,0,1:T(8,128)(2,1)} %pad_maximum_fusion.1), calls=%async_computation | async-start | bytes 4456448 | tf_op jit(solution)/shard_map/all_to_all | solution.py:155
  17.1 30.1 %all-to-all-done = bf16[130,32,256]{2,0,1:T(8,128)(2,1)S(1)} async-done(((bf16[130,32,256]{2,0,1:T(8,128)(2,1)}), bf16[130,32,256]{2,0,1:T(8,128)(2,1)S(1)}, u32[]{:S(2)}, u32[]{:S(2)}) %all-to-all-start) | async-done | bytes 2129952 | tf_op jit(solution)/shard_map/all_to_all | solution.py:155
  47.2 1.6 fusion.50
  48.7 0.4 reshape.264
  49.2 1.8 collective-permute-start
  51.0 0.7 fusion.3
  52.2 0.6 fusion.52
  52.8 2.3 %and_select_fusion.1 = (s32[8]{0:T(128)}, s32[8]{0:T(128)}) fusion(s32[]{:T(128)} %bitcast.12, s32[]{:T(128)} %bitcast.11, s32[]{:T(128)} %bitcast.10), kind=kLoop, calls=%fused_computation.62 | loop fusion | flops 360 | bytes 76 | tf_op jit(solution)/shard_map/jit(floor_divide)/jit(_where)/select_n | solution.py:89
  55.5 1.1 fusion.51
  56.6 1.3 copy.32.kt_ref
  58.0 25.0 %shard_map.73 = bf16[4096,128]{1,0:T(8,128)(2,1)} custom-call(s32[8]{0:T(128)} %get-tuple-element.20.lo_ref, s32[8]{0:T(128)} %get-tuple-element.19.full_ref, s32[3]{0:T(128)} %copy-done.1, bf16[4096,128]{1,0:T(8,128)(2,1)} %bitcast.124, bf16[128,4096]{1,0:T(8,128)(2,1)} %copy.32.kt_ref, bf16[4096,128]{1,0:T(8,128)(2,1)} %get-tuple-element.7.v_ref), custom_call_target="tpu_custom_call" | custom-call | flops 6442450944 | bytes 4194304 | tf_op jit(solution)/shard_map/pallas_call | solution.py:92
  83.0 2.3 %convert_bitcast_fusion = bf16[256,32,128]{0,2,1:T(8,128)(2,1)S(1)} fusion(bf16[32,128,128]{2,1,0:T(8,128)(2,1)} %bitcast.122, s32[32,128]{1,0:T(8,128)S(1)} %get-tuple-element.13), kind=kOutput, calls=%fused_computation.14 | convolution fusion | flops 270532608 | bytes 3162112 | tf_op jit(solution)/shard_map/jmt,jtf->mjf/dot_general | solution.py:176
  85.4 3.1 %copy.34 = bf16[256,32,128]{2,1,0:T(8,128)(2,1)} copy(bf16[256,32,128]{0,2,1:T(8,128)(2,1)S(1)} %convert_bitcast_fusion) | data formatting | bytes 4194304 | tf_op jit(solution)/shard_map/convert_element_type | solution.py:181
  88.5 3.3 %pad_maximum_fusion = bf16[128,65,128]{2,1,0:T(8,128)(2,1)} fusion(bf16[128,1,128]{2,1,0:T(2,128)(2,1)S(1)} %copy.35, bf16[128,64,128]{2,1,0:T(8,128)(2,1)} %bitcast.117), kind=kLoop, calls=%fused_computation.9 | loop fusion | flops 4259840 | bytes 4259840 | tf_op jit(solution)/shard_map/concatenate | solution.py:190
  91.8 3.8 %all-to-all-start.1 = ((bf16[128,65,128]{2,1,0:T(8,128)(2,1)}), bf16[128,65,128]{2,1,0:T(8,128)(2,1)S(1)}, u32[]{:S(2)}, u32[]{:S(2)}) async-start(bf16[128,65,128]{2,1,0:T(8,128)(2,1)} %pad_maximum_fusion), calls=%async_computation.1 | async-start | bytes 4718592 | tf_op jit(solution)/shard_map/all_to_all | solution.py:191
  95.6 33.1 %all-to-all-done.1 = bf16[128,65,128]{2,1,0:T(8,128)(2,1)S(1)} async-done(((bf16[128,65,128]{2,1,0:T(8,128)(2,1)}), bf16[128,65,128]{2,1,0:T(8,128)(2,1)S(1)}, u32[]{:S(2)}, u32[]{:S(2)}) %all-to-all-start.1) | async-done | bytes 2129952 | tf_op jit(solution)/shard_map/all_to_all | solution.py:191
  128.7 0.3 slice.78
  129.0 1.4 copy.36
  130.7 12.2 %fusion.2 = bf16[256,4096]{1,0:T(8,128)(2,1)} fusion(bf16[1024,4096]{1,0:T(8,128)(2,1)} %param.13, bf16[32,8,32,128]{3,2,1,0:T(8,128)(2,1)S(1)} %bitcast.121, bf16[4096,1024]{1,0:T(8,128)(2,1)} %param.12, f32[1024]{0:T(1024)S(1)} %fusion.27, f32[256]{0:T(256)S(1)} %reshape.272), kind=kOutput, calls=%fused_computation.5 | convolution fusion | flops 4300996608 | bytes 20976640 | tf_op jit(solution)/shard_map/dot_general | solution.py:203
  142.9 4.4 %reshape.271 = bf16[128,2,4096]{2,1,0:T(2,128)(2,1)} reshape(bf16[256,4096]{1,0:T(8,128)(2,1)} %fusion.2) | data formatting | bytes 4194304 | tf_op jit(solution)/shard_map/reshape | solution.py:205
  147.2 3.8 %all-to-all-start.2 = ((bf16[128,2,4096]{2,1,0:T(2,128)(2,1)}), bf16[128,2,4096]{2,1,0:T(2,128)(2,1)S(1)}, u32[]{:S(2)}, u32[]{:S(2)}) async-start(bf16[128,2,4096]{2,1,0:T(2,128)(2,1)} %reshape.271), calls=%async_computation.2 | async-start | bytes 4194304 | tf_op jit(solution)/shard_map/all_to_all | solution.py:206
  151.1 30.6 %all-to-all-done.2 = bf16[128,2,4096]{2,1,0:T(2,128)(2,1)S(1)} async-done(((bf16[128,2,4096]{2,1,0:T(2,128)(2,1)}), bf16[128,2,4096]{2,1,0:T(2,128)(2,1)S(1)}, u32[]{:S(2)}, u32[]{:S(2)}) %all-to-all-start.2) | async-done | bytes 2097184 | tf_op jit(solution)/shard_map/all_to_all | solution.py:206
  181.7 3.5 %gather_fusion.1 = bf16[128,4096]{1,0:T(8,128)(2,1)} fusion(bf16[128,2,4096]{2,1,0:T(2,128)(2,1)S(1)} %all-to-all-done.2, s32[128]{0:T(128)S(1)} %fusion.48), kind=kCustom, calls=%fused_computation.1 | custom fusion | bytes 2098176 | tf_op jit(solution)/shard_map/gather | solution.py:207
  (39 shorter events, 2.3 us)
Async XLA Ops:
  3.9 1.2 copy-start
  7.6 39.5 %all-to-all-start = ((bf16[130,32,256]{2,0,1:T(8,128)(2,1)}), bf16[130,32,256]{2,0,1:T(8,128)(2,1)S(1)}, u32[]{:S(2)}, u32[]{:S(2)}) async-start(bf16[130,32,256]{2,0,1:T(8,128)(2,1)} %pad_maximum_fusion.1), calls=%async_computation | async-start | bytes 4456448 | tf_op jit(solution)/shard_map/all_to_all | solution.py:155
  49.2 6.0 %collective-permute-start = (bf16[32,64,256]{2,1,0:T(8,128)(2,1)S(1)}, bf16[32,64,256]{2,1,0:T(8,128)(2,1)S(1)}, u32[]{:S(2)}, u32[]{:S(2)}) collective-permute-start(bf16[32,64,256]{2,1,0:T(8,128)(2,1)S(1)} %reshape.264), channel_id=1, source_target_pairs={{0,4},{4,0},{8,12},{12,8},{16,20},{20,16},{24,28},{28,24},{32,36},... | collective-permute-start | bytes 3145736 | tf_op jit(solution)/shard_map/ppermute | solution.py:159
  52.2 3.3 %copy-start.1 = (s32[3]{0:T(128)}, s32[3]{0:T(128)S(1)}, u32[]{:S(2)}) copy-start(s32[3]{0:T(128)S(1)} %convert_reduce_fusion.bnd_ref) | copy-start | bytes 40
  91.8 36.9 %all-to-all-start.1 = ((bf16[128,65,128]{2,1,0:T(8,128)(2,1)}), bf16[128,65,128]{2,1,0:T(8,128)(2,1)S(1)}, u32[]{:S(2)}, u32[]{:S(2)}) async-start(bf16[128,65,128]{2,1,0:T(8,128)(2,1)} %pad_maximum_fusion), calls=%async_computation.1 | async-start | bytes 4718592 | tf_op jit(solution)/shard_map/all_to_all | solution.py:191
  147.2 3.8 %copy-start.2 = (s32[1,128]{1,0:T(1,128)S(1)}, s32[1,128]{1,0:T(1,128)}, u32[]{:S(2)}) copy-start(s32[1,128]{1,0:T(1,128)} %param.11) | copy-start | bytes 1540
  147.2 34.5 %all-to-all-start.2 = ((bf16[128,2,4096]{2,1,0:T(2,128)(2,1)}), bf16[128,2,4096]{2,1,0:T(2,128)(2,1)S(1)}, u32[]{:S(2)}, u32[]{:S(2)}) async-start(bf16[128,2,4096]{2,1,0:T(2,128)(2,1)} %reshape.271), calls=%async_computation.2 | async-start | bytes 4194304 | tf_op jit(solution)/shard_map/all_to_all | solution.py:206

commit v9 on v8

--- a/solution.py
+++ b/solution.py
@@ -16,57 +16,54 @@
 N_DOCS = 4
 
 
-def _attn_kernel(lo_ref, full_ref, bnd_ref, q_ref, kt_ref, v_ref, o_ref, *, bq, bk, rc, scale):
+def _attn_kernel(lo_ref, full_ref, bnd_ref, q_ref, kt_ref, v_ref, o_ref, s_ref, *, bq, bk, scale):
     i = pl.program_id(0)
     lanes = 128
-    lo = lo_ref[i]
+    nb = s_ref.shape[0]
+    lo = jnp.maximum(lo_ref[i], i - (nb - 1))
     mid = jnp.clip(full_ref[i], lo, i)
-
-    for r in range(bq // rc):
-        rows = pl.ds(r * rc, rc)
-        q = q_ref[rows, :]
-        qpos = i * bq + r * rc + lax.broadcasted_iota(jnp.int32, (rc, 1), 0)
-        qs = jnp.zeros((rc, 1), jnp.int32)
-        for c in range(N_DOCS - 1):
-            qs = jnp.where(qpos >= bnd_ref[c], bnd_ref[c], qs)
-
-        def raw(kb, q=q):
-            start = pl.multiple_of(kb * bk, bk)
-            s = jnp.dot(q, kt_ref[:, pl.ds(start, bk)], preferred_element_type=jnp.float32)
-            return s * scale, start
-
-        def masked(kb, raw=raw, qs=qs, qpos=qpos):
-            s, start = raw(kb)
-            kpos = start + lax.broadcasted_iota(jnp.int32, (1, bk), 1)
-            ok = (kpos >= qs) & (kpos <= qpos)
-            return jnp.where(ok, s, jnp.float32(-1e30)), start
-
-        def fold_max(m, s):
-            for c in range(bk // lanes):
-                m = jnp.maximum(m, s[:, c * lanes : (c + 1) * lanes])
-            return m
-
-        m = jnp.full((rc, lanes), -1e30, jnp.float32)
-        m = lax.fori_loop(lo, mid, lambda kb, m, f=masked: fold_max(m, f(kb)[0]), m)
-        m = lax.fori_loop(mid, i, lambda kb, m, f=raw: fold_max(m, f(kb)[0]), m)
-        m = fold_max(m, masked(i)[0])
-        top = jnp.max(m, axis=1, keepdims=True)
-
-        def accum(carry, s, start, top=top):
-            tot, acc = carry
-            p = jnp.exp(s - top)
-            for c in range(bk // lanes):
-                tot = tot + p[:, c * lanes : (c + 1) * lanes]
-            v = v_ref[pl.ds(start, bk), :]
-            acc = acc + jnp.dot(p.astype(jnp.bfloat16), v, preferred_element_type=jnp.float32)
-            return tot, acc
-
-        carry = (jnp.zeros((rc, lanes), jnp.float32), jnp.zeros((rc, q.shape[1]), jnp.float32))
-        carry = lax.fori_loop(lo, mid, lambda kb, c, f=masked, a=accum: a(c, *f(kb)), carry)
-        carry = lax.fori_loop(mid, i, lambda kb, c, f=raw, a=accum: a(c, *f(kb)), carry)
-        tot, acc = accum(carry, *masked(i))
-        total = jnp.sum(tot, axis=1, keepdims=True)
-        o_ref[rows, :] = (acc / total).astype(o_ref.dtype)
+    q = q_ref[...]
+    qpos = i * bq + lax.broadcasted_iota(jnp.int32, (bq, 1), 0)
+    qs = jnp.zeros((bq, 1), jnp.int32)
+    for c in range(N_DOCS - 1):
+        qs = jnp.where(qpos >= bnd_ref[c], bnd_ref[c], qs)
+
+    def raw(kb):
+        start = pl.multiple_of(kb * bk, bk)
+        s = jnp.dot(q, kt_ref[:, pl.ds(start, bk)], preferred_element_type=jnp.float32)
+        return s * scale, start
+
+    def masked(kb):
+        s, start = raw(kb)
+        kpos = start + lax.broadcasted_iota(jnp.int32, (1, bk), 1)
+        ok = (kpos >= qs) & (kpos <= qpos)
+        return jnp.where(ok, s, jnp.float32(-1e30)), start
+
+    def keep(kb, m, s):
+        s_ref[kb - lo] = s
+        for c in range(bk // lanes):
+            m = jnp.maximum(m, s[:, c * lanes : (c + 1) * lanes])
+        return m
+
+    m = jnp.full((bq, lanes), -1e30, jnp.float32)
+    m = lax.fori_loop(lo, mid, lambda kb, m: keep(kb, m, masked(kb)[0]), m)
+    m = lax.fori_loop(mid, i, lambda kb, m: keep(kb, m, raw(kb)[0]), m)
+    m = keep(i, m, masked(i)[0])
+    top = jnp.max(m, axis=1, keepdims=True)
+
+    def accum(kb, carry):
+        tot, acc = carry
+        p = jnp.exp(s_ref[kb - lo] - top)
+        for c in range(bk // lanes):
+            tot = tot + p[:, c * lanes : (c + 1) * lanes]
+        v = v_ref[pl.ds(pl.multiple_of(kb * bk, bk), bk), :]
+        acc = acc + jnp.dot(p.astype(jnp.bfloat16), v, preferred_element_type=jnp.float32)
+        return tot, acc
+
+    carry = (jnp.zeros((bq, lanes), jnp.float32), jnp.zeros((bq, q.shape[1]), jnp.float32))
+    tot, acc = lax.fori_loop(lo, i + 1, accum, carry)
+    total = jnp.sum(tot, axis=1, keepdims=True)
+    o_ref[...] = (acc / total).astype(o_ref.dtype)
 
 
 def attend(queries, key_rows, value_rows, segments):
@@ -88,7 +85,8 @@
     lo_blk = doc_start_at(firsts) // bk
     full_blk = (doc_start_at(firsts + bq - 1) + bk - 1) // bk
     q_rows = queries.reshape(length, dim)
-    kernel = functools.partial(_attn_kernel, bq=bq, bk=bk, rc=bq, scale=dim ** (-0.5))
+    kernel = functools.partial(_attn_kernel, bq=bq, bk=bk, scale=dim ** (-0.5))
+    band = (MAX_DOC + bq - 1) // bk + 1
     out = pl.pallas_call(
         kernel,
         out_shape=jax.ShapeDtypeStruct((length, dim), jnp.bfloat16),
@@ -101,7 +99,9 @@
                 pl.BlockSpec((length, dim), lambda i, lo, full, bnd: (0, 0)),
             ],
             out_specs=pl.BlockSpec((bq, dim), lambda i, lo, full, bnd: (i, 0)),
+            scratch_shapes=[pltpu.VMEM((min(band, n_q), bq, bk), jnp.float32)],
         ),
+        compiler_params=pltpu.CompilerParams(vmem_limit_bytes=48 * 1024 * 1024),
         cost_estimate=pl.CostEstimate(
             flops=6 * length * MAX_DOC * dim,
             transcendentals=length * MAX_DOC,

time: 184 us -> 181 us (0.984)
  Pallas kernels: 25 us -> 15.9 us
  starting transfers between devices: 18.8 us -> 24.3 us
    pallas_call x1, Pallas kernels: 25 us -> 15.9 us  [attend(): pl.pallas_call(kernel, out_shape=jax.ShapeDtypeStruct((length, dim), jnp....]
    all_to_all x1, starting transfers between devices: 3.77 us -> 9.23 us  [local(): lax.all_to_all(send, ('seq', 'store'), split_axis=0, concat_axis=0, tiled...]
where the time goes in v9:
time: 181 us
  waiting for transfers between devices  94 us (52%)
  starting transfers between devices  24.3 us (13%)
  local copies, waits for them, and re-layouts  23.2 us (13%)
  Pallas kernels  15.9 us (9%)
  matrix products  14 us (8%)
  other arithmetic  9.52 us (5%)
    all_to_all x1, waiting for transfers between devices, local(): lax.all_to_all(send, ('seq', 'store'), split_axis=0, concat_axis=0, tiled...  33.3 us
    all_to_all x1, waiting for transfers between devices, local(): lax.all_to_all(ret, ('seq', 'store'), split_axis=0, concat_axis=0, tiled=...  30.6 us
    all_to_all x1, waiting for transfers between devices, local(): lax.all_to_all(payload, 'seq', split_axis=1, concat_axis=0, tiled=True)  30.1 us
    pallas_call x1, Pallas kernels, attend(): pl.pallas_call(kernel, out_shape=jax.ShapeDtypeStruct((length, dim), jnp....  15.9 us
    dot_general x1, matrix products, local(): jnp.dot(low, adapter_up, preferred_element_type=jnp.float32)  12.1 us
    all_to_all x1, starting transfers between devices, local(): lax.all_to_all(payload, 'seq', split_axis=1, concat_axis=0, tiled=True)  9.42 us
    all_to_all x1, starting transfers between devices, local(): lax.all_to_all(send, ('seq', 'store'), split_axis=0, concat_axis=0, tiled...  9.23 us
    reshape x1, local copies, waits for them, and re-layouts, local(): ret = mixed_rows.reshape(devices, capacity, width)  4.38 us
  transfers between devices with their start and end apart: 4, of which 3 were waited for; matrix products, arithmetic and copies ran while one was open for 2% of the time, Pallas kernels for 0%

profile of v9, /device:TPU:1, one launch (start us, length us, event | category | flops | bytes accessed | tf_op | source)
XLA Modules:
  0.0 181.2 jit_solution(9130264401899725069)
XLA Ops:
  0.0 0.7 convert_bitcast_fusion.1
  0.7 0.7 and_select_fusion.4
  1.8 0.9 concatenate.24
  2.8 0.9 concatenate.25
  3.9 0.6 gather_fusion
  4.5 0.4 gather.10
  5.1 0.2 copy.41
  5.4 0.4 copy.30
  6.0 1.7 pad_maximum_fusion.1
  7.6 9.4 %all-to-all-start = ((bf16[130,32,256]{2,0,1:T(8,128)(2,1)}), bf16[130,32,256]{2,0,1:T(8,128)(2,1)S(1)}, u32[]{:S(2)}, u32[]{:S(2)}) async-start(bf16[130,32,256]{2,0,1:T(8,128)(2,1)} %pad_maximum_fusion.1), calls=%async_computation | async-start | bytes 4456448 | tf_op jit(solution)/shard_map/all_to_all | solution.py:155
  17.1 30.1 %all-to-all-done = bf16[130,32,256]{2,0,1:T(8,128)(2,1)S(1)} async-done(((bf16[130,32,256]{2,0,1:T(8,128)(2,1)}), bf16[130,32,256]{2,0,1:T(8,128)(2,1)S(1)}, u32[]{:S(2)}, u32[]{:S(2)}) %all-to-all-start) | async-done | bytes 2129952 | tf_op jit(solution)/shard_map/all_to_all | solution.py:155
  47.2 1.6 fusion.50
  48.7 1.4 reshape.264
  50.2 1.8 collective-permute-start
  52.0 0.7 fusion.3
  53.3 0.6 fusion.52
  53.9 1.8 %and_select_fusion.1 = (s32[8]{0:T(128)S(1)}, s32[8]{0:T(128)S(1)}) fusion(s32[]{:T(128)} %bitcast.12, s32[]{:T(128)} %bitcast.11, s32[]{:T(128)} %bitcast.10), kind=kLoop, calls=%fused_computation.62 | loop fusion | flops 360 | bytes 76 | tf_op jit(solution)/shard_map/jit(floor_divide)/jit(_where)/select_n | solution.py:86
  56.1 1.1 fusion.51
  57.2 1.5 copy.32.kt_ref
  58.7 15.9 %shard_map.73 = bf16[4096,128]{1,0:T(8,128)(2,1)S(1)} custom-call(s32[8]{0:T(128)S(1)} %get-tuple-element.20.lo_ref, s32[8]{0:T(128)S(1)} %get-tuple-element.19.full_ref, s32[3]{0:T(128)S(1)} %convert_reduce_fusion.bnd_ref, bf16[4096,128]{1,0:T(8,128)(2,1)S(1)} %bitcast.113, bf16[128,4096]{1,0:T(8,128)(2,1)S(1)} %copy.32.kt_ref, ...), custom_call_target="tpu_custom_call" | custom-call | flops 6442450944 | bytes 4194304 | tf_op jit(solution)/shard_map/pallas_call | solution.py:90
  74.6 1.1 convert_bitcast_fusion
  75.7 3.1 %copy.34 = bf16[256,32,128]{2,1,0:T(8,128)(2,1)} copy(bf16[256,32,128]{0,2,1:T(8,128)(2,1)S(1)} %convert_bitcast_fusion) | data formatting | bytes 4194304 | tf_op jit(solution)/shard_map/convert_element_type | solution.py:181
  78.9 3.3 %pad_maximum_fusion = bf16[128,65,128]{2,1,0:T(8,128)(2,1)} fusion(bf16[128,1,128]{2,1,0:T(2,128)(2,1)S(1)} %copy.35, bf16[128,64,128]{2,1,0:T(8,128)(2,1)} %bitcast.119), kind=kLoop, calls=%fused_computation.9 | loop fusion | flops 4259840 | bytes 4259840 | tf_op jit(solution)/shard_map/concatenate | solution.py:190
  82.2 9.2 %all-to-all-start.1 = ((bf16[128,65,128]{2,1,0:T(8,128)(2,1)}), bf16[128,65,128]{2,1,0:T(8,128)(2,1)S(1)}, u32[]{:S(2)}, u32[]{:S(2)}) async-start(bf16[128,65,128]{2,1,0:T(8,128)(2,1)} %pad_maximum_fusion), calls=%async_computation.1 | async-start | bytes 4718592 | tf_op jit(solution)/shard_map/all_to_all | solution.py:191
  91.4 33.3 %all-to-all-done.1 = bf16[128,65,128]{2,1,0:T(8,128)(2,1)S(1)} async-done(((bf16[128,65,128]{2,1,0:T(8,128)(2,1)}), bf16[128,65,128]{2,1,0:T(8,128)(2,1)S(1)}, u32[]{:S(2)}, u32[]{:S(2)}) %all-to-all-start.1) | async-done | bytes 2129952 | tf_op jit(solution)/shard_map/all_to_all | solution.py:191
  124.7 0.3 slice.78
  125.0 1.4 copy.36
  126.7 12.1 %fusion.2 = bf16[256,4096]{1,0:T(8,128)(2,1)} fusion(bf16[1024,4096]{1,0:T(8,128)(2,1)} %param.13, bf16[32,8,32,128]{3,2,1,0:T(8,128)(2,1)S(1)} %bitcast.123, bf16[4096,1024]{1,0:T(8,128)(2,1)} %param.12, f32[1024]{0:T(1024)S(1)} %fusion.27, f32[256]{0:T(256)S(1)} %reshape.272), kind=kOutput, calls=%fused_computation.5 | convolution fusion | flops 4300996608 | bytes 20976640 | tf_op jit(solution)/shard_map/dot_general | solution.py:203
  138.9 4.4 %reshape.271 = bf16[128,2,4096]{2,1,0:T(2,128)(2,1)} reshape(bf16[256,4096]{1,0:T(8,128)(2,1)} %fusion.2) | data formatting | bytes 4194304 | tf_op jit(solution)/shard_map/reshape | solution.py:205
  143.3 3.8 %all-to-all-start.2 = ((bf16[128,2,4096]{2,1,0:T(2,128)(2,1)}), bf16[128,2,4096]{2,1,0:T(2,128)(2,1)S(1)}, u32[]{:S(2)}, u32[]{:S(2)}) async-start(bf16[128,2,4096]{2,1,0:T(2,128)(2,1)} %reshape.271), calls=%async_computation.2 | async-start | bytes 4194304 | tf_op jit(solution)/shard_map/all_to_all | solution.py:206
  147.1 30.6 %all-to-all-done.2 = bf16[128,2,4096]{2,1,0:T(2,128)(2,1)S(1)} async-done(((bf16[128,2,4096]{2,1,0:T(2,128)(2,1)}), bf16[128,2,4096]{2,1,0:T(2,128)(2,1)S(1)}, u32[]{:S(2)}, u32[]{:S(2)}) %all-to-all-start.2) | async-done | bytes 2097184 | tf_op jit(solution)/shard_map/all_to_all | solution.py:206
  177.7 3.5 %gather_fusion.1 = bf16[128,4096]{1,0:T(8,128)(2,1)} fusion(bf16[128,2,4096]{2,1,0:T(2,128)(2,1)S(1)} %all-to-all-done.2, s32[128]{0:T(128)S(1)} %fusion.48), kind=kCustom, calls=%fused_computation.1 | custom fusion | bytes 2098176 | tf_op jit(solution)/shard_map/gather | solution.py:207
  (37 shorter events, 2.3 us)
Async XLA Ops:
  3.9 1.2 copy-start
  7.6 39.5 %all-to-all-start = ((bf16[130,32,256]{2,0,1:T(8,128)(2,1)}), bf16[130,32,256]{2,0,1:T(8,128)(2,1)S(1)}, u32[]{:S(2)}, u32[]{:S(2)}) async-start(bf16[130,32,256]{2,0,1:T(8,128)(2,1)} %pad_maximum_fusion.1), calls=%async_computation | async-start | bytes 4456448 | tf_op jit(solution)/shard_map/all_to_all | solution.py:155
  50.2 5.5 %collective-permute-start = (bf16[32,64,256]{2,1,0:T(8,128)(2,1)S(1)}, bf16[32,64,256]{2,1,0:T(8,128)(2,1)S(1)}, u32[]{:S(2)}, u32[]{:S(2)}) collective-permute-start(bf16[32,64,256]{2,1,0:T(8,128)(2,1)S(1)} %reshape.264), channel_id=1, source_target_pairs={{0,4},{4,0},{8,12},{12,8},{16,20},{20,16},{24,28},{28,24},{32,36},... | collective-permute-start | bytes 3145736 | tf_op jit(solution)/shard_map/ppermute | solution.py:159
  82.2 42.6 %all-to-all-start.1 = ((bf16[128,65,128]{2,1,0:T(8,128)(2,1)}), bf16[128,65,128]{2,1,0:T(8,128)(2,1)S(1)}, u32[]{:S(2)}, u32[]{:S(2)}) async-start(bf16[128,65,128]{2,1,0:T(8,128)(2,1)} %pad_maximum_fusion), calls=%async_computation.1 | async-start | bytes 4718592 | tf_op jit(solution)/shard_map/all_to_all | solution.py:191
  143.3 3.8 %copy-start.1 = (s32[1,128]{1,0:T(1,128)S(1)}, s32[1,128]{1,0:T(1,128)}, u32[]{:S(2)}) copy-start(s32[1,128]{1,0:T(1,128)} %param.11) | copy-start | bytes 1540
  143.3 34.5 %all-to-all-start.2 = ((bf16[128,2,4096]{2,1,0:T(2,128)(2,1)}), bf16[128,2,4096]{2,1,0:T(2,128)(2,1)S(1)}, u32[]{:S(2)}, u32[]{:S(2)}) async-start(bf16[128,2,4096]{2,1,0:T(2,128)(2,1)} %reshape.271), calls=%async_computation.2 | async-start | bytes 4194304 | tf_op jit(solution)/shard_map/all_to_all | solution.py:206

commit v10 on v9

--- a/solution.py
+++ b/solution.py
@@ -16,8 +16,8 @@
 N_DOCS = 4
 
 
-def _attn_kernel(lo_ref, full_ref, bnd_ref, q_ref, kt_ref, v_ref, o_ref, s_ref, *, bq, bk, scale):
-    i = pl.program_id(0)
+def _attn_kernel(lo_ref, full_ref, bnd_ref, q_ref, kt_ref, v_ref, o_ref, s_ref, *, bq, bk, first, scale):
+    i = pl.program_id(0) + first
     lanes = 128
     nb = s_ref.shape[0]
     lo = jnp.maximum(lo_ref[i], i - (nb - 1))
@@ -66,7 +66,7 @@
     o_ref[...] = (acc / total).astype(o_ref.dtype)
 
 
-def attend(queries, key_rows, value_rows, segments):
+def attend(queries, key_rows, value_rows, segments, parts):
     length, dim = key_rows.shape
     bq = min(512, length)
     bk = min(512, length)
@@ -85,30 +85,38 @@
     lo_blk = doc_start_at(firsts) // bk
     full_blk = (doc_start_at(firsts + bq - 1) + bk - 1) // bk
     q_rows = queries.reshape(length, dim)
-    kernel = functools.partial(_attn_kernel, bq=bq, bk=bk, scale=dim ** (-0.5))
+    key_cols = key_rows.T
     band = (MAX_DOC + bq - 1) // bk + 1
-    out = pl.pallas_call(
-        kernel,
-        out_shape=jax.ShapeDtypeStruct((length, dim), jnp.bfloat16),
-        grid_spec=pltpu.PrefetchScalarGridSpec(
-            num_scalar_prefetch=3,
-            grid=(n_q,),
-            in_specs=[
-                pl.BlockSpec((bq, dim), lambda i, lo, full, bnd: (i, 0)),
-                pl.BlockSpec((dim, length), lambda i, lo, full, bnd: (0, 0)),
-                pl.BlockSpec((length, dim), lambda i, lo, full, bnd: (0, 0)),
-            ],
-            out_specs=pl.BlockSpec((bq, dim), lambda i, lo, full, bnd: (i, 0)),
-            scratch_shapes=[pltpu.VMEM((min(band, n_q), bq, bk), jnp.float32)],
-        ),
-        compiler_params=pltpu.CompilerParams(vmem_limit_bytes=48 * 1024 * 1024),
-        cost_estimate=pl.CostEstimate(
-            flops=6 * length * MAX_DOC * dim,
-            transcendentals=length * MAX_DOC,
-            bytes_accessed=8 * length * dim,
-        ),
-    )(lo_blk, full_blk, bounds, q_rows, key_rows.T, value_rows)
-    return out
+    per = n_q // parts
+    outs = []
+    for part in range(parts):
+        kernel = functools.partial(
+            _attn_kernel, bq=bq, bk=bk, first=part * per, scale=dim ** (-0.5)
+        )
+        outs.append(
+            pl.pallas_call(
+                kernel,
+                out_shape=jax.ShapeDtypeStruct((per * bq, dim), jnp.bfloat16),
+                grid_spec=pltpu.PrefetchScalarGridSpec(
+                    num_scalar_prefetch=3,
+                    grid=(per,),
+                    in_specs=[
+                        pl.BlockSpec((bq, dim), lambda i, lo, full, bnd, f=part * per: (i + f, 0)),
+                        pl.BlockSpec((dim, length), lambda i, lo, full, bnd: (0, 0)),
+                        pl.BlockSpec((length, dim), lambda i, lo, full, bnd: (0, 0)),
+                    ],
+                    out_specs=pl.BlockSpec((bq, dim), lambda i, lo, full, bnd: (i, 0)),
+                    scratch_shapes=[pltpu.VMEM((min(band, n_q), bq, bk), jnp.float32)],
+                ),
+                compiler_params=pltpu.CompilerParams(vmem_limit_bytes=48 * 1024 * 1024),
+                cost_estimate=pl.CostEstimate(
+                    flops=6 * per * bq * MAX_DOC * dim,
+                    transcendentals=per * bq * MAX_DOC,
+                    bytes_accessed=(2 * per * bq + 2 * length) * dim * 2,
+                ),
+            )(lo_blk, full_blk, bounds, q_rows, key_cols, value_rows)
+        )
+    return outs
 
 
 def local(queries, keys, values, segment_ids, route_ids, adapter_down, adapter_up):
@@ -169,39 +177,50 @@
     code_all = meta_all[:, tok_rows : 2 * tok_rows]
     adapter_all = meta_all[:, 2 * tok_rows :]
 
-    context = attend(q_all, k_all, v_all, segments).reshape(length, feat)
-
-    pick = code_all[:, None, :] == jnp.arange(devices * capacity, dtype=jnp.int32)[None, :, None]
-    pick = pick.astype(jnp.bfloat16)
-    send = jnp.einsum(
-        "jmt,jtf->mjf",
-        pick,
-        context.reshape(n_seq, tok_rows, feat),
-        preferred_element_type=jnp.float32,
-    ).astype(jnp.bfloat16)
-    send = send.reshape(devices, slots, feat)
-    tags = jnp.einsum(
-        "jmt,jt->mj",
-        pick,
-        (adapter_all.reshape(n_seq, tok_rows) + 1).astype(jnp.bfloat16),
-        preferred_element_type=jnp.float32,
-    ).reshape(devices, slots) - 1.0
-    tag_row = jnp.pad(tags.astype(jnp.bfloat16), ((0, 0), (0, feat - slots)))
-    send = jnp.concatenate([send, tag_row[:, None, :]], axis=1)
-    got = lax.all_to_all(send, ("seq", "store"), split_axis=0, concat_axis=0, tiled=True)
-    got = got.reshape(n_seq, n_store, slots + 1, feat)
-    rows = jnp.transpose(
-        got[:, :, :slots, :].reshape(n_seq, n_store, capacity, n_seq, feat), (3, 1, 2, 0, 4)
-    ).reshape(n_store * slots, width)
-    row_tags = jnp.transpose(
-        got[0, :, slots, :slots].reshape(n_store, capacity, n_seq), (2, 0, 1)
-    ).reshape(n_store * slots, 1).astype(jnp.float32)
-
-    low = jnp.dot(rows, adapter_down, preferred_element_type=jnp.float32)
-    lane_owner = (jnp.arange(low.shape[1], dtype=jnp.int32) // RANK).astype(jnp.float32)
-    low = jnp.where(row_tags == lane_owner[None, :], low, 0.0).astype(jnp.bfloat16)
-    delta = jnp.dot(low, adapter_up, preferred_element_type=jnp.float32).astype(jnp.bfloat16)
-    mixed_rows = (rows.astype(jnp.float32) + delta.astype(jnp.float32)).astype(jnp.bfloat16)
+    parts = 2
+    blocks = n_seq // parts
+    contexts = attend(q_all, k_all, v_all, segments, parts)
+
+    def dispatch(part, context):
+        codes = code_all[part * blocks : (part + 1) * blocks]
+        pick = codes[:, None, :] == jnp.arange(devices * capacity, dtype=jnp.int32)[None, :, None]
+        pick = pick.astype(jnp.bfloat16)
+        send = jnp.einsum(
+            "jmt,jtf->mjf",
+            pick,
+            context.reshape(blocks, tok_rows, feat),
+            preferred_element_type=jnp.float32,
+        ).astype(jnp.bfloat16)
+        send = send.reshape(devices, capacity * blocks, feat)
+        adapters = adapter_all[part * blocks : (part + 1) * blocks]
+        tags = jnp.einsum(
+            "jmt,jt->mj",
+            pick,
+            (adapters + 1).astype(jnp.bfloat16),
+            preferred_element_type=jnp.float32,
+        ).reshape(devices, capacity * blocks) - 1.0
+        tag_row = jnp.pad(tags.astype(jnp.bfloat16), ((0, 0), (0, feat - capacity * blocks)))
+        send = jnp.concatenate([send, tag_row[:, None, :]], axis=1)
+        return lax.all_to_all(send, ("seq", "store"), split_axis=0, concat_axis=0, tiled=True)
+
+    def owner_rows(got):
+        got = got.reshape(n_seq, n_store, capacity * blocks + 1, feat)
+        rows = jnp.transpose(
+            got[:, :, : capacity * blocks, :].reshape(n_seq, n_store, capacity, blocks, feat),
+            (3, 1, 2, 0, 4),
+        ).reshape(blocks * n_store * capacity, width)
+        row_tags = jnp.transpose(
+            got[0, :, capacity * blocks, : capacity * blocks].reshape(n_store, capacity, blocks),
+            (2, 0, 1),
+        ).reshape(blocks * n_store * capacity, 1).astype(jnp.float32)
+        low = jnp.dot(rows, adapter_down, preferred_element_type=jnp.float32)
+        lane_owner = (jnp.arange(low.shape[1], dtype=jnp.int32) // RANK).astype(jnp.float32)
+        low = jnp.where(row_tags == lane_owner[None, :], low, 0.0).astype(jnp.bfloat16)
+        delta = jnp.dot(low, adapter_up, preferred_element_type=jnp.float32).astype(jnp.bfloat16)
+        return (rows.astype(jnp.float32) + delta.astype(jnp.float32)).astype(jnp.bfloat16)
+
+    gots = [dispatch(part, ctx) for part, ctx in enumerate(contexts)]
+    mixed_rows = jnp.concatenate([owner_rows(got) for got in gots], axis=0)
     ret = mixed_rows.reshape(devices, capacity, width)
     back = lax.all_to_all(ret, ("seq", "store"), split_axis=0, concat_axis=0, tiled=True)
     mixed = back[owners, rank]

time: 181 us -> 194 us (1.072)
  matrix products: 14 us -> 21.3 us
  starting transfers between devices: 24.3 us -> 28.1 us
  waiting for transfers between devices: 94 us -> 91.6 us
  other arithmetic: 9.52 us -> 11.5 us
    dot_general x3 -> x6, matrix products: 14 us -> 21.3 us  [the longest x2 18.2 us: owner_rows(): jnp.dot(low, adapter_up, preferred_element_type=jnp.float32)]
    all_to_all x1 -> x2, starting transfers between devices: 9.23 us -> 12.9 us  [dispatch(): lax.all_to_all(send, ('seq', 'store'), split_axis=0, concat_axis=0, tiled...]
    all_to_all x1 -> x2, waiting for transfers between devices: 33.3 us -> 30.9 us  [dispatch(): lax.all_to_all(send, ('seq', 'store'), split_axis=0, concat_axis=0, tiled...]
    concatenate x1 -> x3, other arithmetic: 3.29 us -> 5.17 us  [the longest x2 3.78 us: dispatch(): send = jnp.concatenate([send, tag_row[:, None, :]], axis=1)]
    convert_element_type x5 -> x10, local copies, waits for them, and re-layouts: 3.59 us -> 4.61 us  [the longest x2 3.72 us: dispatch(): send = jnp.einsum('jmt,jtf->mjf', pick, context.reshape(blocks, tok_rows,...]
    pallas_call x1 -> x2, Pallas kernels: 15.9 us -> 16.4 us  [attend(): pl.pallas_call(kernel, out_shape=jax.ShapeDtypeStruct((per * bq, dim), jn...]
  transfers between devices with their start and end apart: 4 -> 5, of which waited for: 3 -> 4; matrix products, arithmetic and copies ran while one was open for 2% -> 5% of each run, Pallas kernels for 0% -> 4%
where the time goes in v10:
time: 194 us
  waiting for transfers between devices  91.6 us (47%)
  starting transfers between devices  28.1 us (14%)
  local copies, waits for them, and re-layouts  24.3 us (13%)
  matrix products  21.3 us (11%)
  Pallas kernels  16.4 us (8%)
  other arithmetic  11.5 us (6%)
    all_to_all x2, waiting for transfers between devices, dispatch(): lax.all_to_all(send, ('seq', 'store'), split_axis=0, concat_axis=0, tiled...  30.9 us
    all_to_all x1, waiting for transfers between devices, local(): lax.all_to_all(ret, ('seq', 'store'), split_axis=0, concat_axis=0, tiled=...  30.6 us
    all_to_all x1, waiting for transfers between devices, local(): lax.all_to_all(payload, 'seq', split_axis=1, concat_axis=0, tiled=True)  30.1 us
    dot_general x2, matrix products, owner_rows(): jnp.dot(low, adapter_up, preferred_element_type=jnp.float32)  18.2 us
    pallas_call x2, Pallas kernels, attend(): pl.pallas_call(kernel, out_shape=jax.ShapeDtypeStruct((per * bq, dim), jn...  16.4 us
    all_to_all x2, starting transfers between devices, dispatch(): lax.all_to_all(send, ('seq', 'store'), split_axis=0, concat_axis=0, tiled...  12.9 us
    all_to_all x1, starting transfers between devices, local(): lax.all_to_all(payload, 'seq', split_axis=1, concat_axis=0, tiled=True)  9.42 us
    all_to_all x1, starting transfers between devices, local(): lax.all_to_all(ret, ('seq', 'store'), split_axis=0, concat_axis=0, tiled=...  3.98 us
  transfers between devices with their start and end apart: 5, of which 4 were waited for; matrix products, arithmetic and copies ran while one was open for 5% of the time, Pallas kernels for 4%

profile of v10, /device:TPU:1, one launch (start us, length us, event | category | flops | bytes accessed | tf_op | source)
XLA Modules:
  0.0 193.6 jit_solution(1573666974932832089)
XLA Ops:
  0.0 0.7 convert_bitcast_fusion
  0.7 0.7 and_select_fusion.4
  1.8 0.9 concatenate.30
  2.8 0.9 concatenate.31
  6.0 1.7 pad_maximum_fusion
  7.7 9.4 %all-to-all-start = ((bf16[130,32,256]{2,0,1:T(8,128)(2,1)}), bf16[130,32,256]{2,0,1:T(8,128)(2,1)S(1)}, u32[]{:S(2)}, u32[]{:S(2)}) async-start(bf16[130,32,256]{2,0,1:T(8,128)(2,1)} %pad_maximum_fusion), calls=%async_computation | async-start | bytes 4456448 | tf_op jit(solution)/shard_map/all_to_all | solution.py:163
  17.1 30.1 %all-to-all-done = bf16[130,32,256]{2,0,1:T(8,128)(2,1)S(1)} async-done(((bf16[130,32,256]{2,0,1:T(8,128)(2,1)}), bf16[130,32,256]{2,0,1:T(8,128)(2,1)S(1)}, u32[]{:S(2)}, u32[]{:S(2)}) %all-to-all-start) | async-done | bytes 2129952 | tf_op jit(solution)/shard_map/all_to_all | solution.py:163
  47.2 1.6 fusion.70
  48.8 1.4 reshape.296
  50.3 1.8 collective-permute-start
  53.7 1.9 and_select_fusion.1
  55.9 1.1 fusion.71
  57.1 1.5 copy.54.kt_ref
  58.5 9.1 %shard_map.74 = bf16[2048,128]{1,0:T(8,128)(2,1)S(1)} custom-call(s32[8]{0:T(128)S(1)} %get-tuple-element.21.lo_ref, s32[8]{0:T(128)S(1)} %get-tuple-element.20.full_ref, s32[3]{0:T(128)S(1)} %convert_reduce_fusion.bnd_ref, bf16[4096,128]{1,0:T(8,128)(2,1)S(1)} %bitcast.142, bf16[128,4096]{1,0:T(8,128)(2,1)S(1)} %copy.54.kt_ref, ...), custom_call_target="tpu_custom_call" | custom-call | flops 3221225472 | bytes 3145728 | tf_op jit(solution)/shard_map/pallas_call | solution.py:97
  67.7 1.6 fusion.12
  69.3 2.6 %copy.63 = bf16[256,16,128]{2,1,0:T(8,128)(2,1)} copy(bf16[256,16,128]{0,2,1:T(8,128)(2,1)} %fusion.12) | data formatting | bytes 2097152 | tf_op jit(solution)/shard_map/convert_element_type | solution.py:193
  71.9 2.5 %pad_maximum_fusion.4 = bf16[128,33,128]{2,1,0:T(8,128)(2,1)} fusion(bf16[128,1,128]{2,1,0:T(2,128)(2,1)S(1)} %copy.64, bf16[128,32,128]{2,1,0:T(8,128)(2,1)} %bitcast.156), kind=kLoop, calls=%fused_computation.24 | loop fusion | flops 2162688 | bytes 2162688 | tf_op jit(solution)/shard_map/concatenate | solution.py:203
  74.4 8.9 %all-to-all-start.2 = ((bf16[128,33,128]{2,1,0:T(8,128)(2,1)}), bf16[128,33,128]{2,1,0:T(8,128)(2,1)}, u32[]{:S(2)}, u32[]{:S(2)}) async-start(bf16[128,33,128]{2,1,0:T(8,128)(2,1)} %pad_maximum_fusion.4), calls=%async_computation.2 | async-start | bytes 2621440 | tf_op jit(solution)/shard_map/all_to_all | solution.py:204
  84.1 7.3 %shard_map.73 = bf16[2048,128]{1,0:T(8,128)(2,1)S(1)} custom-call(s32[8]{0:T(128)S(1)} %get-tuple-element.21.lo_ref, s32[8]{0:T(128)S(1)} %get-tuple-element.20.full_ref, s32[3]{0:T(128)S(1)} %convert_reduce_fusion.bnd_ref, bf16[4096,128]{1,0:T(8,128)(2,1)S(1)} %bitcast.143, bf16[128,4096]{1,0:T(8,128)(2,1)S(1)} %copy.54.kt_ref, ...), custom_call_target="tpu_custom_call" | custom-call | flops 3221225472 | bytes 3145728 | tf_op jit(solution)/shard_map/pallas_call | solution.py:97
  92.0 1.1 copy.56
  93.1 1.3 pad_maximum_fusion.3
  94.4 10.7 %all-to-all-done.2 = bf16[128,33,128]{2,1,0:T(8,128)(2,1)} async-done(((bf16[128,33,128]{2,1,0:T(8,128)(2,1)}), bf16[128,33,128]{2,1,0:T(8,128)(2,1)}, u32[]{:S(2)}, u32[]{:S(2)}) %all-to-all-start.2) | async-done | bytes 1081376 | tf_op jit(solution)/shard_map/all_to_all | solution.py:204
  105.1 4.0 %all-to-all-start.1 = ((bf16[128,33,128]{2,1,0:T(8,128)(2,1)}), bf16[128,33,128]{2,1,0:T(8,128)(2,1)S(1)}, u32[]{:S(2)}, u32[]{:S(2)}) async-start(bf16[128,33,128]{2,1,0:T(8,128)(2,1)} %pad_maximum_fusion.3), calls=%async_computation.1 | async-start | bytes 2621440 | tf_op jit(solution)/shard_map/all_to_all | solution.py:204
  109.1 1.6 copy.65
  111.1 20.2 %all-to-all-done.1 = bf16[128,33,128]{2,1,0:T(8,128)(2,1)S(1)} async-done(((bf16[128,33,128]{2,1,0:T(8,128)(2,1)}), bf16[128,33,128]{2,1,0:T(8,128)(2,1)S(1)}, u32[]{:S(2)}, u32[]{:S(2)}) %all-to-all-start.1) | async-done | bytes 1081376 | tf_op jit(solution)/shard_map/all_to_all | solution.py:204
  133.3 8.6 %fusion.2 = bf16[128,4096]{1,0:T(8,128)(2,1)S(1)} fusion(bf16[1024,4096]{1,0:T(8,128)(2,1)} %param.13, bf16[16,8,32,128]{3,2,1,0:T(8,128)(2,1)S(1)} %bitcast.154, bf16[4096,1024]{1,0:T(8,128)(2,1)} %param.12, f32[1024]{0:T(1024)S(1)} %fusion.45, f32[128]{0:T(128)S(1)} %reshape.310), kind=kOutput, calls=%fused_computation.5 | convolution fusion | flops 2150498304 | bytes 18878976 | tf_op jit(solution)/shard_map/dot_general | solution.py:219
  141.9 9.6 %fusion.5 = bf16[128,4096]{1,0:T(8,128)(2,1)} fusion(bf16[1024,4096]{1,0:T(8,128)(2,1)} %param.13, bf16[16,8,32,128]{3,2,1,0:T(8,128)(2,1)S(1)} %bitcast.155, bf16[4096,1024]{1,0:T(8,128)(2,1)} %param.12, f32[1024]{0:T(1024)S(1)} %fusion.45, f32[128]{0:T(128)S(1)} %reshape.309), kind=kOutput, calls=%fused_computation.9 | convolution fusion | flops 2150498304 | bytes 18878976 | tf_op jit(solution)/shard_map/dot_general | solution.py:219
  151.5 1.4 pad_maximum_fusion.2
  152.9 2.6 %reshape.308 = bf16[128,2,4096]{2,1,0:T(2,128)(2,1)} reshape(bf16[256,4096]{1,0:T(8,128)(2,1)S(1)} %pad_maximum_fusion.2) | data formatting | bytes 4194304 | tf_op jit(solution)/shard_map/reshape | solution.py:224
  155.5 4.0 %all-to-all-start.3 = ((bf16[128,2,4096]{2,1,0:T(2,128)(2,1)}), bf16[128,2,4096]{2,1,0:T(2,128)(2,1)S(1)}, u32[]{:S(2)}, u32[]{:S(2)}) async-start(bf16[128,2,4096]{2,1,0:T(2,128)(2,1)} %reshape.308), calls=%async_computation.3 | async-start | bytes 4194304 | tf_op jit(solution)/shard_map/all_to_all | solution.py:225
  159.5 30.6 %all-to-all-done.3 = bf16[128,2,4096]{2,1,0:T(2,128)(2,1)S(1)} async-done(((bf16[128,2,4096]{2,1,0:T(2,128)(2,1)}), bf16[128,2,4096]{2,1,0:T(2,128)(2,1)S(1)}, u32[]{:S(2)}, u32[]{:S(2)}) %all-to-all-start.3) | async-done | bytes 2097184 | tf_op jit(solution)/shard_map/all_to_all | solution.py:225
  190.1 3.5 %gather_fusion.1 = bf16[128,4096]{1,0:T(8,128)(2,1)} fusion(bf16[128,2,4096]{2,1,0:T(2,128)(2,1)S(1)} %all-to-all-done.3, s32[128]{0:T(128)S(1)} %fusion.67), kind=kCustom, calls=%fused_computation.1 | custom fusion | bytes 2098176 | tf_op jit(solution)/shard_map/gather | solution.py:226
  (60 shorter events, 8.3 us)
Async XLA Ops:
  3.9 1.2 copy-start
  7.7 39.5 %all-to-all-start = ((bf16[130,32,256]{2,0,1:T(8,128)(2,1)}), bf16[130,32,256]{2,0,1:T(8,128)(2,1)S(1)}, u32[]{:S(2)}, u32[]{:S(2)}) async-start(bf16[130,32,256]{2,0,1:T(8,128)(2,1)} %pad_maximum_fusion), calls=%async_computation | async-start | bytes 4456448 | tf_op jit(solution)/shard_map/all_to_all | solution.py:163
  50.3 5.3 %collective-permute-start = (bf16[32,64,256]{2,1,0:T(8,128)(2,1)S(1)}, bf16[32,64,256]{2,1,0:T(8,128)(2,1)S(1)}, u32[]{:S(2)}, u32[]{:S(2)}) collective-permute-start(bf16[32,64,256]{2,1,0:T(8,128)(2,1)S(1)} %reshape.296), channel_id=1, source_target_pairs={{0,4},{4,0},{8,12},{12,8},{16,20},{20,16},{24,28},{28,24},{32,36},... | collective-permute-start | bytes 3145736 | tf_op jit(solution)/shard_map/ppermute | solution.py:167
  74.4 30.7 %all-to-all-start.2 = ((bf16[128,33,128]{2,1,0:T(8,128)(2,1)}), bf16[128,33,128]{2,1,0:T(8,128)(2,1)}, u32[]{:S(2)}, u32[]{:S(2)}) async-start(bf16[128,33,128]{2,1,0:T(8,128)(2,1)} %pad_maximum_fusion.4), calls=%async_computation.2 | async-start | bytes 2621440 | tf_op jit(solution)/shard_map/all_to_all | solution.py:204
  105.1 26.2 %all-to-all-start.1 = ((bf16[128,33,128]{2,1,0:T(8,128)(2,1)}), bf16[128,33,128]{2,1,0:T(8,128)(2,1)S(1)}, u32[]{:S(2)}, u32[]{:S(2)}) async-start(bf16[128,33,128]{2,1,0:T(8,128)(2,1)} %pad_maximum_fusion.3), calls=%async_computation.1 | async-start | bytes 2621440 | tf_op jit(solution)/shard_map/all_to_all | solution.py:204
  155.5 4.0 %copy-start.1 = (s32[1,128]{1,0:T(1,128)S(1)}, s32[1,128]{1,0:T(1,128)}, u32[]{:S(2)}) copy-start(s32[1,128]{1,0:T(1,128)} %param.11) | copy-start | bytes 1540
  155.5 34.7 %all-to-all-start.3 = ((bf16[128,2,4096]{2,1,0:T(2,128)(2,1)}), bf16[128,2,4096]{2,1,0:T(2,128)(2,1)S(1)}, u32[]{:S(2)}, u32[]{:S(2)}) async-start(bf16[128,2,4096]{2,1,0:T(2,128)(2,1)} %reshape.308), calls=%async_computation.3 | async-start | bytes 4194304 | tf_op jit(solution)/shard_map/all_to_all | solution.py:225

commit v11 on v9

--- a/solution.py
+++ b/solution.py
@@ -125,7 +125,7 @@
     slots = n_seq * capacity
 
     half = tok_rows // 2
-    q_send = queries[0].reshape(tok_rows, n_seq, feat)
+    q_send = jnp.transpose(queries[0].reshape(tok_rows, n_seq, feat), (1, 0, 2))
     paired = jnp.concatenate(
         [keys[0].reshape(tok_rows, KV_HEADS, HEAD_DIM), values[0].reshape(tok_rows, KV_HEADS, HEAD_DIM)],
         axis=2,
@@ -135,7 +135,7 @@
     )
     dest = jnp.arange(n_seq, dtype=jnp.int32)
     kv_send = jnp.take(halves, (dest % 2) * KV_HEADS + (dest * heads_here) // group, axis=0)
-    kv_send = jnp.transpose(kv_send.reshape(n_seq, tok_rows, HEAD_DIM), (1, 0, 2))
+    kv_send = kv_send.reshape(n_seq, tok_rows, HEAD_DIM)
     chosen = route_ids[0]
     owners = chosen // EXP_DEV
     one_hot = (owners[:, None] == jnp.arange(devices, dtype=jnp.int32)[None, :]).astype(jnp.int32)
@@ -148,11 +148,11 @@
     payload = jnp.concatenate(
         [
             jnp.concatenate([q_send, kv_send], axis=2),
-            jnp.broadcast_to(meta[:, None, :], (meta_rows, n_seq, meta_w)),
+            jnp.broadcast_to(meta[None, :, :], (n_seq, meta_rows, meta_w)),
         ],
-        axis=0,
-    )
-    got_in = lax.all_to_all(payload, "seq", split_axis=1, concat_axis=0, tiled=True)
+        axis=1,
+    )
+    got_in = lax.all_to_all(payload, "seq", split_axis=0, concat_axis=0, tiled=True)
     got_in = got_in.reshape(n_seq, tok_rows + meta_rows, meta_w)
     q_all = got_in[:, :tok_rows, :feat].reshape(length, heads_here, HEAD_DIM)
     kv_mine = got_in[:, :tok_rows, feat:].reshape(n_seq, half, 2 * HEAD_DIM)

time: 181 us -> 181 us (level)
  starting transfers between devices: 24.3 us -> 20.2 us
  Pallas kernels: 15.9 us -> 19.8 us
    all_to_all x1, starting transfers between devices: 9.23 us -> 5.09 us  [local(): lax.all_to_all(send, ('seq', 'store'), split_axis=0, concat_axis=0, tiled...]
    pallas_call x1, Pallas kernels: 15.9 us -> 19.8 us  [attend(): pl.pallas_call(kernel, out_shape=jax.ShapeDtypeStruct((length, dim), jnp....]
where the time goes in v11:
time: 181 us
  waiting for transfers between devices  94 us (52%)
  local copies, waits for them, and re-layouts  23.2 us (13%)
  starting transfers between devices  20.2 us (11%)
  Pallas kernels  19.8 us (11%)
  matrix products  14 us (8%)
  other arithmetic  9.5 us (5%)
    all_to_all x1, waiting for transfers between devices, local(): lax.all_to_all(send, ('seq', 'store'), split_axis=0, concat_axis=0, tiled...  33.3 us
    all_to_all x1, waiting for transfers between devices, local(): lax.all_to_all(ret, ('seq', 'store'), split_axis=0, concat_axis=0, tiled=...  30.6 us
    all_to_all x1, waiting for transfers between devices, local(): lax.all_to_all(payload, 'seq', split_axis=0, concat_axis=0, tiled=True)  30.1 us
    pallas_call x1, Pallas kernels, attend(): pl.pallas_call(kernel, out_shape=jax.ShapeDtypeStruct((length, dim), jnp....  19.8 us
    dot_general x1, matrix products, local(): jnp.dot(low, adapter_up, preferred_element_type=jnp.float32)  12.1 us
    all_to_all x1, starting transfers between devices, local(): lax.all_to_all(payload, 'seq', split_axis=0, concat_axis=0, tiled=True)  9.47 us
    all_to_all x1, starting transfers between devices, local(): lax.all_to_all(send, ('seq', 'store'), split_axis=0, concat_axis=0, tiled...  5.09 us
    reshape x1, local copies, waits for them, and re-layouts, local(): ret = mixed_rows.reshape(devices, capacity, width)  4.38 us
  transfers between devices with their start and end apart: 4, of which 3 were waited for; matrix products, arithmetic and copies ran while one was open for 2% of the time, Pallas kernels for 0%

profile of v11, /device:TPU:1, one launch (start us, length us, event | category | flops | bytes accessed | tf_op | source)
XLA Modules:
  0.0 181.1 jit_solution(18358094481162581243)
XLA Ops:
  0.0 0.7 convert_bitcast_fusion.1
  0.7 0.7 and_select_fusion.4
  1.8 0.9 concatenate.24
  2.8 0.9 concatenate.25
  3.9 0.6 gather_fusion
  4.5 0.4 gather.10
  5.4 0.4 copy.58
  6.0 1.7 pad_maximum_fusion.1
  7.6 9.5 %all-to-all-start = ((bf16[32,130,256]{2,1,0:T(8,128)(2,1)}), bf16[32,130,256]{2,1,0:T(8,128)(2,1)}, u32[]{:S(2)}, u32[]{:S(2)}) async-start(bf16[32,130,256]{2,1,0:T(8,128)(2,1)} %pad_maximum_fusion.1), calls=%async_computation | async-start | bytes 4456448 | tf_op jit(solution)/shard_map/all_to_all | solution.py:155
  17.1 30.1 %all-to-all-done = bf16[32,130,256]{2,1,0:T(8,128)(2,1)} async-done(((bf16[32,130,256]{2,1,0:T(8,128)(2,1)}), bf16[32,130,256]{2,1,0:T(8,128)(2,1)}, u32[]{:S(2)}, u32[]{:S(2)}) %all-to-all-start) | async-done | bytes 2129952 | tf_op jit(solution)/shard_map/all_to_all | solution.py:155
  47.3 1.7 fusion.50
  48.9 0.4 reshape.259
  49.3 0.9 slice.69
  50.3 1.8 collective-permute-start
  52.1 0.7 fusion.3
  53.4 0.6 fusion.52
  54.0 1.8 %and_select_fusion.1 = (s32[8]{0:T(128)S(1)}, s32[8]{0:T(128)S(1)}) fusion(s32[]{:T(128)} %bitcast.9, s32[]{:T(128)} %bitcast.8, s32[]{:T(128)} %bitcast.7), kind=kLoop, calls=%fused_computation.63 | loop fusion | flops 360 | bytes 76 | tf_op jit(solution)/shard_map/jit(floor_divide)/jit(_where)/select_n | solution.py:86
  56.2 1.1 fusion.51
  57.3 1.5 copy.32.kt_ref
  58.8 19.8 %shard_map.73 = bf16[4096,128]{1,0:T(8,128)(2,1)S(1)} custom-call(s32[8]{0:T(128)S(1)} %get-tuple-element.20.lo_ref, s32[8]{0:T(128)S(1)} %get-tuple-element.19.full_ref, s32[3]{0:T(128)S(1)} %convert_reduce_fusion.bnd_ref, bf16[4096,128]{1,0:T(8,128)(2,1)S(1)} %bitcast.109, bf16[128,4096]{1,0:T(8,128)(2,1)S(1)} %copy.32.kt_ref, ...), custom_call_target="tpu_custom_call" | custom-call | flops 6442450944 | bytes 4194304 | tf_op jit(solution)/shard_map/pallas_call | solution.py:90
  78.6 1.1 convert_bitcast_fusion
  79.7 3.1 %copy.34 = bf16[256,32,128]{2,1,0:T(8,128)(2,1)} copy(bf16[256,32,128]{0,2,1:T(8,128)(2,1)S(1)} %convert_bitcast_fusion) | data formatting | bytes 4194304 | tf_op jit(solution)/shard_map/convert_element_type | solution.py:181
  82.9 3.3 %pad_maximum_fusion = bf16[128,65,128]{2,1,0:T(8,128)(2,1)} fusion(bf16[128,1,128]{2,1,0:T(2,128)(2,1)S(1)} %copy.35, bf16[128,64,128]{2,1,0:T(8,128)(2,1)} %bitcast.113), kind=kLoop, calls=%fused_computation.9 | loop fusion | flops 4259840 | bytes 4259840 | tf_op jit(solution)/shard_map/concatenate | solution.py:190
  86.2 5.1 %all-to-all-start.1 = ((bf16[128,65,128]{2,1,0:T(8,128)(2,1)}), bf16[128,65,128]{2,1,0:T(8,128)(2,1)S(1)}, u32[]{:S(2)}, u32[]{:S(2)}) async-start(bf16[128,65,128]{2,1,0:T(8,128)(2,1)} %pad_maximum_fusion), calls=%async_computation.1 | async-start | bytes 4718592 | tf_op jit(solution)/shard_map/all_to_all | solution.py:191
  91.3 33.3 %all-to-all-done.1 = bf16[128,65,128]{2,1,0:T(8,128)(2,1)S(1)} async-done(((bf16[128,65,128]{2,1,0:T(8,128)(2,1)}), bf16[128,65,128]{2,1,0:T(8,128)(2,1)S(1)}, u32[]{:S(2)}, u32[]{:S(2)}) %all-to-all-start.1) | async-done | bytes 2129952 | tf_op jit(solution)/shard_map/all_to_all | solution.py:191
  124.6 0.3 slice.78
  124.9 1.4 copy.36
  126.6 12.1 %fusion.2 = bf16[256,4096]{1,0:T(8,128)(2,1)} fusion(bf16[1024,4096]{1,0:T(8,128)(2,1)} %param.13, bf16[32,8,32,128]{3,2,1,0:T(8,128)(2,1)S(1)} %bitcast.118, bf16[4096,1024]{1,0:T(8,128)(2,1)} %param.12, f32[1024]{0:T(1024)S(1)} %fusion.27, f32[256]{0:T(256)S(1)} %reshape.267), kind=kOutput, calls=%fused_computation.5 | convolution fusion | flops 4300996608 | bytes 20976640 | tf_op jit(solution)/shard_map/dot_general | solution.py:203
  138.7 4.4 %reshape.266 = bf16[128,2,4096]{2,1,0:T(2,128)(2,1)} reshape(bf16[256,4096]{1,0:T(8,128)(2,1)} %fusion.2) | data formatting | bytes 4194304 | tf_op jit(solution)/shard_map/reshape | solution.py:205
  143.1 3.8 %all-to-all-start.2 = ((bf16[128,2,4096]{2,1,0:T(2,128)(2,1)}), bf16[128,2,4096]{2,1,0:T(2,128)(2,1)S(1)}, u32[]{:S(2)}, u32[]{:S(2)}) async-start(bf16[128,2,4096]{2,1,0:T(2,128)(2,1)} %reshape.266), calls=%async_computation.2 | async-start | bytes 4194304 | tf_op jit(solution)/shard_map/all_to_all | solution.py:206
  147.0 30.6 %all-to-all-done.2 = bf16[128,2,4096]{2,1,0:T(2,128)(2,1)S(1)} async-done(((bf16[128,2,4096]{2,1,0:T(2,128)(2,1)}), bf16[128,2,4096]{2,1,0:T(2,128)(2,1)S(1)}, u32[]{:S(2)}, u32[]{:S(2)}) %all-to-all-start.2) | async-done | bytes 2097184 | tf_op jit(solution)/shard_map/all_to_all | solution.py:206
  177.6 3.5 %gather_fusion.1 = bf16[128,4096]{1,0:T(8,128)(2,1)} fusion(bf16[128,2,4096]{2,1,0:T(2,128)(2,1)S(1)} %all-to-all-done.2, s32[128]{0:T(128)S(1)} %fusion.48), kind=kCustom, calls=%fused_computation.1 | custom fusion | bytes 2098176 | tf_op jit(solution)/shard_map/gather | solution.py:207
  (37 shorter events, 2.5 us)
Async XLA Ops:
  3.9 1.2 copy-start
  7.6 39.6 %all-to-all-start = ((bf16[32,130,256]{2,1,0:T(8,128)(2,1)}), bf16[32,130,256]{2,1,0:T(8,128)(2,1)}, u32[]{:S(2)}, u32[]{:S(2)}) async-start(bf16[32,130,256]{2,1,0:T(8,128)(2,1)} %pad_maximum_fusion.1), calls=%async_computation | async-start | bytes 4456448 | tf_op jit(solution)/shard_map/all_to_all | solution.py:155
  50.3 5.5 %collective-permute-start = (bf16[32,64,256]{2,1,0:T(8,128)(2,1)S(1)}, bf16[32,64,256]{2,1,0:T(8,128)(2,1)S(1)}, u32[]{:S(2)}, u32[]{:S(2)}) collective-permute-start(bf16[32,64,256]{2,1,0:T(8,128)(2,1)S(1)} %reshape.259), channel_id=1, source_target_pairs={{0,4},{4,0},{8,12},{12,8},{16,20},{20,16},{24,28},{28,24},{32,36},... | collective-permute-start | bytes 3145736 | tf_op jit(solution)/shard_map/ppermute | solution.py:159
  86.2 38.4 %all-to-all-start.1 = ((bf16[128,65,128]{2,1,0:T(8,128)(2,1)}), bf16[128,65,128]{2,1,0:T(8,128)(2,1)S(1)}, u32[]{:S(2)}, u32[]{:S(2)}) async-start(bf16[128,65,128]{2,1,0:T(8,128)(2,1)} %pad_maximum_fusion), calls=%async_computation.1 | async-start | bytes 4718592 | tf_op jit(solution)/shard_map/all_to_all | solution.py:191
  143.1 3.8 %copy-start.1 = (s32[1,128]{1,0:T(1,128)S(1)}, s32[1,128]{1,0:T(1,128)}, u32[]{:S(2)}) copy-start(s32[1,128]{1,0:T(1,128)} %param.11) | copy-start | bytes 1540
  143.1 34.5 %all-to-all-start.2 = ((bf16[128,2,4096]{2,1,0:T(2,128)(2,1)}), bf16[128,2,4096]{2,1,0:T(2,128)(2,1)S(1)}, u32[]{:S(2)}, u32[]{:S(2)}) async-start(bf16[128,2,4096]{2,1,0:T(2,128)(2,1)} %reshape.266), calls=%async_computation.2 | async-start | bytes 4194304 | tf_op jit(solution)/shard_map/all_to_all | solution.py:206

commit v12 on v9

--- a/solution.py
+++ b/solution.py
@@ -174,28 +174,27 @@
     pick = code_all[:, None, :] == jnp.arange(devices * capacity, dtype=jnp.int32)[None, :, None]
     pick = pick.astype(jnp.bfloat16)
     send = jnp.einsum(
-        "jmt,jtf->mjf",
+        "jmt,jtf->jmf",
         pick,
         context.reshape(n_seq, tok_rows, feat),
         preferred_element_type=jnp.float32,
     ).astype(jnp.bfloat16)
-    send = send.reshape(devices, slots, feat)
+    send = send.reshape(n_seq, devices, capacity, feat)
     tags = jnp.einsum(
         "jmt,jt->mj",
         pick,
         (adapter_all.reshape(n_seq, tok_rows) + 1).astype(jnp.bfloat16),
         preferred_element_type=jnp.float32,
-    ).reshape(devices, slots) - 1.0
-    tag_row = jnp.pad(tags.astype(jnp.bfloat16), ((0, 0), (0, feat - slots)))
-    send = jnp.concatenate([send, tag_row[:, None, :]], axis=1)
-    got = lax.all_to_all(send, ("seq", "store"), split_axis=0, concat_axis=0, tiled=True)
-    got = got.reshape(n_seq, n_store, slots + 1, feat)
+    ).reshape(devices, capacity, n_seq) - 1.0
+    tag_plane = jnp.pad(tags.astype(jnp.bfloat16), ((0, 0), (0, 0), (0, feat - n_seq)))
+    send = jnp.concatenate([send, tag_plane[None]], axis=0)
+    got = lax.all_to_all(send, ("seq", "store"), split_axis=1, concat_axis=1, tiled=True)
     rows = jnp.transpose(
-        got[:, :, :slots, :].reshape(n_seq, n_store, capacity, n_seq, feat), (3, 1, 2, 0, 4)
+        got[:n_seq].reshape(n_seq, n_seq, n_store, capacity, feat), (0, 2, 3, 1, 4)
     ).reshape(n_store * slots, width)
-    row_tags = jnp.transpose(
-        got[0, :, slots, :slots].reshape(n_store, capacity, n_seq), (2, 0, 1)
-    ).reshape(n_store * slots, 1).astype(jnp.float32)
+    row_tags = jnp.transpose(got[n_seq, :n_store, :, :n_seq], (2, 0, 1)).reshape(
+        n_store * slots, 1
+    ).astype(jnp.float32)
 
     low = jnp.dot(rows, adapter_down, preferred_element_type=jnp.float32)
     lane_owner = (jnp.arange(low.shape[1], dtype=jnp.int32) // RANK).astype(jnp.float32)

time: 181 us -> 177 us (0.978)
  waiting for transfers between devices: 94 us -> 91.9 us
    reshape x0 -> x1, local copies, waits for them, and re-layouts: none -> 3.78 us  [local(): got[:n_seq].reshape(n_seq, n_seq, n_store, capacity, feat)]
    convert_element_type x5 -> x2, local copies, waits for them, and re-layouts: 3.59 us -> 0.27 us  [local(): row_tags = jnp.transpose(got[n_seq, :n_store, :, :n_seq], (2, 0, 1)).resh...]
    all_to_all x1, waiting for transfers between devices: 33.3 us -> 31.2 us  [local(): lax.all_to_all(send, ('seq', 'store'), split_axis=1, concat_axis=1, tiled...]
    slice x1, local copies, waits for them, and re-layouts: 0.28 us -> 2.35 us  [local(): got[:n_seq].reshape(n_seq, n_seq, n_store, capacity, feat)]
where the time goes in v12:
time: 177 us
  waiting for transfers between devices  91.9 us (52%)
  starting transfers between devices  23.4 us (13%)
  local copies, waits for them, and re-layouts  22.8 us (13%)
  Pallas kernels  15.9 us (9%)
  matrix products  13.6 us (8%)
  other arithmetic  9.39 us (5%)
    all_to_all x1, waiting for transfers between devices, local(): lax.all_to_all(send, ('seq', 'store'), split_axis=1, concat_axis=1, tiled...  31.2 us
    all_to_all x1, waiting for transfers between devices, local(): lax.all_to_all(ret, ('seq', 'store'), split_axis=0, concat_axis=0, tiled=...  30.6 us
    all_to_all x1, waiting for transfers between devices, local(): lax.all_to_all(payload, 'seq', split_axis=1, concat_axis=0, tiled=True)  30.1 us
    pallas_call x1, Pallas kernels, attend(): pl.pallas_call(kernel, out_shape=jax.ShapeDtypeStruct((length, dim), jnp....  15.9 us
    dot_general x1, matrix products, local(): jnp.dot(low, adapter_up, preferred_element_type=jnp.float32)  12 us
    all_to_all x1, starting transfers between devices, local(): lax.all_to_all(payload, 'seq', split_axis=1, concat_axis=0, tiled=True)  9.42 us
    all_to_all x1, starting transfers between devices, local(): lax.all_to_all(send, ('seq', 'store'), split_axis=1, concat_axis=1, tiled...  8.33 us
    all_to_all x1, starting transfers between devices, local(): lax.all_to_all(ret, ('seq', 'store'), split_axis=0, concat_axis=0, tiled=...  3.81 us
  transfers between devices with their start and end apart: 4, of which 3 were waited for; matrix products, arithmetic and copies ran while one was open for 2% of the time, Pallas kernels for 0%

profile of v12, /device:TPU:1, one launch (start us, length us, event | category | flops | bytes accessed | tf_op | source)
XLA Modules:
  0.0 177.2 jit_solution(5641721302694196115)
XLA Ops:
  0.0 0.7 convert_bitcast_fusion.1
  0.7 0.7 and_select_fusion.4
  1.8 0.9 concatenate.24
  2.8 0.9 concatenate.25
  3.9 0.6 gather_fusion
  4.5 0.4 gather.10
  5.1 0.2 copy.43
  5.4 0.4 copy.34
  6.0 1.7 pad_maximum_fusion
  7.7 9.4 %all-to-all-start = ((bf16[130,32,256]{2,0,1:T(8,128)(2,1)}), bf16[130,32,256]{2,0,1:T(8,128)(2,1)S(1)}, u32[]{:S(2)}, u32[]{:S(2)}) async-start(bf16[130,32,256]{2,0,1:T(8,128)(2,1)} %pad_maximum_fusion), calls=%async_computation | async-start | bytes 4456448 | tf_op jit(solution)/shard_map/all_to_all | solution.py:155
  17.1 30.1 %all-to-all-done = bf16[130,32,256]{2,0,1:T(8,128)(2,1)S(1)} async-done(((bf16[130,32,256]{2,0,1:T(8,128)(2,1)}), bf16[130,32,256]{2,0,1:T(8,128)(2,1)S(1)}, u32[]{:S(2)}, u32[]{:S(2)}) %all-to-all-start) | async-done | bytes 2129952 | tf_op jit(solution)/shard_map/all_to_all | solution.py:155
  47.2 1.6 fusion.49
  48.8 1.4 reshape.261
  50.2 1.8 %collective-permute-start = (bf16[32,64,256]{2,1,0:T(8,128)(2,1)S(1)}, bf16[32,64,256]{2,1,0:T(8,128)(2,1)S(1)}, u32[]{:S(2)}, u32[]{:S(2)}) collective-permute-start(bf16[32,64,256]{2,1,0:T(8,128)(2,1)S(1)} %reshape.261), channel_id=1, source_target_pairs={{0,4},{4,0},{8,12},{12,8},{16,20},{20,16},{24,28},{28,24},{32,36},... | collective-permute-start | bytes 3145736 | tf_op jit(solution)/shard_map/ppermute | solution.py:159
  52.1 0.7 fusion.3
  52.9 0.2 convert_reduce_fusion.bnd_ref
  53.1 0.7 fusion.51
  53.8 1.9 %and_select_fusion.1 = (s32[8]{0:T(128)S(1)}, s32[8]{0:T(128)S(1)}) fusion(s32[]{:T(128)} %bitcast.12, s32[]{:T(128)} %bitcast.11, s32[]{:T(128)} %bitcast.10), kind=kLoop, calls=%fused_computation.61 | loop fusion | flops 360 | bytes 76 | tf_op jit(solution)/shard_map/jit(floor_divide)/jit(_where)/select_n | solution.py:86
  56.2 1.1 fusion.50
  57.3 1.5 copy.36.kt_ref
  58.8 15.9 %shard_map.73 = bf16[4096,128]{1,0:T(8,128)(2,1)S(1)} custom-call(s32[8]{0:T(128)S(1)} %get-tuple-element.20.lo_ref, s32[8]{0:T(128)S(1)} %get-tuple-element.19.full_ref, s32[3]{0:T(128)S(1)} %convert_reduce_fusion.bnd_ref, bf16[4096,128]{1,0:T(8,128)(2,1)S(1)} %bitcast.116, bf16[128,4096]{1,0:T(8,128)(2,1)S(1)} %copy.36.kt_ref, ...), custom_call_target="tpu_custom_call" | custom-call | flops 6442450944 | bytes 4194304 | tf_op jit(solution)/shard_map/pallas_call | solution.py:90
  74.7 0.9 fusion.9
  75.6 3.1 %pad_maximum_fusion.1 = bf16[33,128,2,128]{3,2,0,1:T(2,128)(2,1)} fusion(bf16[1,128,2,128]{3,2,0,1:T(2,128)(2,1)S(1)} %pad_bitcast_fusion, bf16[32,128,2,128]{3,2,1,0:T(2,128)(2,1)S(1)} %bitcast.120), kind=kLoop, calls=%fused_computation.10 | loop fusion | flops 4325376 | bytes 4325376 | tf_op jit(solution)/shard_map/concatenate | solution.py:190
  78.7 8.3 %all-to-all-start.1 = ((bf16[33,128,2,128]{3,2,0,1:T(2,128)(2,1)}), bf16[33,128,2,128]{3,2,0,1:T(2,128)(2,1)S(1)}, u32[]{:S(2)}, u32[]{:S(2)}) async-start(bf16[33,128,2,128]{3,2,0,1:T(2,128)(2,1)} %pad_maximum_fusion.1), calls=%async_computation.1 | async-start | bytes 4325376 | tf_op jit(solution)/shard_map/all_to_all | solution.py:191
  87.0 31.2 %all-to-all-done.1 = bf16[33,128,2,128]{3,2,0,1:T(2,128)(2,1)S(1)} async-done(((bf16[33,128,2,128]{3,2,0,1:T(2,128)(2,1)}), bf16[33,128,2,128]{3,2,0,1:T(2,128)(2,1)S(1)}, u32[]{:S(2)}, u32[]{:S(2)}) %all-to-all-start.1) | async-done | bytes 2162720 | tf_op jit(solution)/shard_map/all_to_all | solution.py:191
  118.2 2.4 %slice.78 = bf16[32,128,2,128]{3,2,0,1:T(2,128)(2,1)S(1)} slice(bf16[33,128,2,128]{3,2,0,1:T(2,128)(2,1)S(1)} %all-to-all-done.1), slice={[0:32], [0:128], [0:2], [0:128]} | slice | bytes 4194304 | tf_op jit(solution)/shard_map/slice | solution.py:193
  120.6 3.8 %copy.39 = bf16[32,32,4,2,128]{4,1,3,2,0:T(8,128)(2,1)} copy(bf16[32,32,4,2,128]{4,3,0,2,1:T(2,128)(2,1)S(1)} %bitcast.121) | data formatting | bytes 4194304 | tf_op jit(solution)/shard_map/reshape | solution.py:193
  124.7 12.0 %fusion.2 = bf16[256,4096]{1,0:T(8,128)(2,1)S(1)} fusion(bf16[1024,4096]{1,0:T(8,128)(2,1)} %param.13, bf16[32,8,32,128]{3,2,1,0:T(8,128)(2,1)} %bitcast.124, bf16[4096,1024]{1,0:T(8,128)(2,1)} %param.12, f32[1024]{0:T(1024)S(1)} %fusion.27, f32[256]{0:T(256)S(1)} %reshape.268), kind=kOutput, calls=%fused_computation.5 | convolution fusion | flops 4300996608 | bytes 20976640 | tf_op jit(solution)/shard_map/dot_general | solution.py:202
  136.7 2.6 %reshape.267 = bf16[128,2,4096]{2,1,0:T(2,128)(2,1)} reshape(bf16[256,4096]{1,0:T(8,128)(2,1)S(1)} %fusion.2) | data formatting | bytes 4194304 | tf_op jit(solution)/shard_map/reshape | solution.py:204
  139.3 3.8 %all-to-all-start.2 = ((bf16[128,2,4096]{2,1,0:T(2,128)(2,1)}), bf16[128,2,4096]{2,1,0:T(2,128)(2,1)S(1)}, u32[]{:S(2)}, u32[]{:S(2)}) async-start(bf16[128,2,4096]{2,1,0:T(2,128)(2,1)} %reshape.267), calls=%async_computation.2 | async-start | bytes 4194304 | tf_op jit(solution)/shard_map/all_to_all | solution.py:205
  143.1 30.6 %all-to-all-done.2 = bf16[128,2,4096]{2,1,0:T(2,128)(2,1)S(1)} async-done(((bf16[128,2,4096]{2,1,0:T(2,128)(2,1)}), bf16[128,2,4096]{2,1,0:T(2,128)(2,1)S(1)}, u32[]{:S(2)}, u32[]{:S(2)}) %all-to-all-start.2) | async-done | bytes 2097184 | tf_op jit(solution)/shard_map/all_to_all | solution.py:205
  173.7 3.5 %gather_fusion.1 = bf16[128,4096]{1,0:T(8,128)(2,1)} fusion(bf16[128,2,4096]{2,1,0:T(2,128)(2,1)S(1)} %all-to-all-done.2, s32[128]{0:T(128)S(1)} %fusion.47), kind=kCustom, calls=%fused_computation.1 | custom fusion | bytes 2098176 | tf_op jit(solution)/shard_map/gather | solution.py:206
  (33 shorter events, 1.9 us)
Async XLA Ops:
  3.9 1.2 copy-start
  7.7 39.5 %all-to-all-start = ((bf16[130,32,256]{2,0,1:T(8,128)(2,1)}), bf16[130,32,256]{2,0,1:T(8,128)(2,1)S(1)}, u32[]{:S(2)}, u32[]{:S(2)}) async-start(bf16[130,32,256]{2,0,1:T(8,128)(2,1)} %pad_maximum_fusion), calls=%async_computation | async-start | bytes 4456448 | tf_op jit(solution)/shard_map/all_to_all | solution.py:155
  50.2 5.5 %collective-permute-start = (bf16[32,64,256]{2,1,0:T(8,128)(2,1)S(1)}, bf16[32,64,256]{2,1,0:T(8,128)(2,1)S(1)}, u32[]{:S(2)}, u32[]{:S(2)}) collective-permute-start(bf16[32,64,256]{2,1,0:T(8,128)(2,1)S(1)} %reshape.261), channel_id=1, source_target_pairs={{0,4},{4,0},{8,12},{12,8},{16,20},{20,16},{24,28},{28,24},{32,36},... | collective-permute-start | bytes 3145736 | tf_op jit(solution)/shard_map/ppermute | solution.py:159
  78.7 39.6 %all-to-all-start.1 = ((bf16[33,128,2,128]{3,2,0,1:T(2,128)(2,1)}), bf16[33,128,2,128]{3,2,0,1:T(2,128)(2,1)S(1)}, u32[]{:S(2)}, u32[]{:S(2)}) async-start(bf16[33,128,2,128]{3,2,0,1:T(2,128)(2,1)} %pad_maximum_fusion.1), calls=%async_computation.1 | async-start | bytes 4325376 | tf_op jit(solution)/shard_map/all_to_all | solution.py:191
  139.3 3.8 %copy-start.1 = (s32[1,128]{1,0:T(1,128)S(1)}, s32[1,128]{1,0:T(1,128)}, u32[]{:S(2)}) copy-start(s32[1,128]{1,0:T(1,128)} %param.11) | copy-start | bytes 1540
  139.3 34.5 %all-to-all-start.2 = ((bf16[128,2,4096]{2,1,0:T(2,128)(2,1)}), bf16[128,2,4096]{2,1,0:T(2,128)(2,1)S(1)}, u32[]{:S(2)}, u32[]{:S(2)}) async-start(bf16[128,2,4096]{2,1,0:T(2,128)(2,1)} %reshape.267), calls=%async_computation.2 | async-start | bytes 4194304 | tf_op jit(solution)/shard_map/all_to_all | solution.py:205

commit v13 on v9

--- a/solution.py
+++ b/solution.py
@@ -133,8 +133,14 @@
     halves = jnp.transpose(paired.reshape(2, half, KV_HEADS, 2 * HEAD_DIM), (0, 2, 1, 3)).reshape(
         2 * KV_HEADS, half, 2 * HEAD_DIM
     )
-    dest = jnp.arange(n_seq, dtype=jnp.int32)
-    kv_send = jnp.take(halves, (dest % 2) * KV_HEADS + (dest * heads_here) // group, axis=0)
+    if heads_here == 1 and group % 2 == 0 and n_seq == KV_HEADS * group:
+        kv_send = jnp.broadcast_to(
+            jnp.transpose(halves.reshape(2, KV_HEADS, half, 2 * HEAD_DIM), (1, 0, 2, 3))[:, None],
+            (KV_HEADS, group // 2, 2, half, 2 * HEAD_DIM),
+        ).reshape(n_seq, half, 2 * HEAD_DIM)
+    else:
+        dest = jnp.arange(n_seq, dtype=jnp.int32)
+        kv_send = jnp.take(halves, (dest % 2) * KV_HEADS + (dest * heads_here) // group, axis=0)
     kv_send = jnp.transpose(kv_send.reshape(n_seq, tok_rows, HEAD_DIM), (1, 0, 2))
     chosen = route_ids[0]
     owners = chosen // EXP_DEV

time: 181 us -> 181 us (level)
  starting transfers between devices: 24.3 us -> 21 us
  Pallas kernels: 15.9 us -> 19.1 us
    all_to_all x1, starting transfers between devices: 9.23 us -> 5.96 us  [local(): lax.all_to_all(send, ('seq', 'store'), split_axis=0, concat_axis=0, tiled...]
    pallas_call x1, Pallas kernels: 15.9 us -> 19.1 us  [attend(): pl.pallas_call(kernel, out_shape=jax.ShapeDtypeStruct((length, dim), jnp....]
where the time goes in v13:
time: 181 us; the launch traced here: 180 us
  waiting for transfers between devices  94 us (52%)
  local copies, waits for them, and re-layouts  22.6 us (12%)
  starting transfers between devices  21 us (12%)
  Pallas kernels  19.1 us (11%)
  matrix products  14 us (8%)
  other arithmetic  9.31 us (5%)
    all_to_all x1, waiting for transfers between devices, local(): lax.all_to_all(send, ('seq', 'store'), split_axis=0, concat_axis=0, tiled...  33.3 us
    all_to_all x1, waiting for transfers between devices, local(): lax.all_to_all(ret, ('seq', 'store'), split_axis=0, concat_axis=0, tiled=...  30.6 us
    all_to_all x1, waiting for transfers between devices, local(): lax.all_to_all(payload, 'seq', split_axis=1, concat_axis=0, tiled=True)  30.1 us
    pallas_call x1, Pallas kernels, attend(): pl.pallas_call(kernel, out_shape=jax.ShapeDtypeStruct((length, dim), jnp....  19.1 us
    dot_general x1, matrix products, local(): jnp.dot(low, adapter_up, preferred_element_type=jnp.float32)  12.1 us
    all_to_all x1, starting transfers between devices, local(): lax.all_to_all(payload, 'seq', split_axis=1, concat_axis=0, tiled=True)  9.42 us
    all_to_all x1, starting transfers between devices, local(): lax.all_to_all(send, ('seq', 'store'), split_axis=0, concat_axis=0, tiled...  5.96 us
    reshape x1, local copies, waits for them, and re-layouts, local(): ret = mixed_rows.reshape(devices, capacity, width)  4.38 us
  transfers between devices with their start and end apart: 4, of which 3 were waited for; matrix products, arithmetic and copies ran while one was open for 2% of the time, Pallas kernels for 0%

profile of v13, /device:TPU:1, one launch (start us, length us, event | category | flops | bytes accessed | tf_op | source)
XLA Modules:
  0.0 180.3 jit_solution(10388627324930289590)
XLA Ops:
  0.0 0.7 convert_bitcast_fusion.1
  0.7 0.7 and_select_fusion.4
  1.8 0.9 concatenate.24
  2.8 1.0 concatenate.25
  4.1 0.4 reshape_reshape.6
  4.5 0.2 copy.34
  4.8 0.4 copy.23
  5.2 1.7 pad_maximum_fusion.1
  6.9 9.4 %all-to-all-start = ((bf16[130,32,256]{2,0,1:T(8,128)(2,1)}), bf16[130,32,256]{2,0,1:T(8,128)(2,1)S(1)}, u32[]{:S(2)}, u32[]{:S(2)}) async-start(bf16[130,32,256]{2,0,1:T(8,128)(2,1)} %pad_maximum_fusion.1), calls=%async_computation | async-start | bytes 4456448 | tf_op jit(solution)/shard_map/all_to_all | solution.py:161
  16.3 30.1 %all-to-all-done = bf16[130,32,256]{2,0,1:T(8,128)(2,1)S(1)} async-done(((bf16[130,32,256]{2,0,1:T(8,128)(2,1)}), bf16[130,32,256]{2,0,1:T(8,128)(2,1)S(1)}, u32[]{:S(2)}, u32[]{:S(2)}) %all-to-all-start) | async-done | bytes 2129952 | tf_op jit(solution)/shard_map/all_to_all | solution.py:161
  46.4 1.6 fusion.45
  48.0 1.4 reshape.184
  49.4 1.8 %collective-permute-start = (bf16[32,64,256]{2,1,0:T(8,128)(2,1)S(1)}, bf16[32,64,256]{2,1,0:T(8,128)(2,1)S(1)}, u32[]{:S(2)}, u32[]{:S(2)}) collective-permute-start(bf16[32,64,256]{2,1,0:T(8,128)(2,1)S(1)} %reshape.184), channel_id=1, source_target_pairs={{0,4},{4,0},{8,12},{12,8},{16,20},{20,16},{24,28},{28,24},{32,36},... | collective-permute-start | bytes 3145736 | tf_op jit(solution)/shard_map/ppermute | solution.py:165
  51.2 0.7 fusion.3
  52.3 0.2 convert_reduce_fusion.bnd_ref
  52.5 0.6 fusion.47
  53.1 1.8 %and_select_fusion.1 = (s32[8]{0:T(128)S(1)}, s32[8]{0:T(128)S(1)}) fusion(s32[]{:T(128)} %bitcast.10, s32[]{:T(128)} %bitcast.9, s32[]{:T(128)} %bitcast.8), kind=kLoop, calls=%fused_computation.57 | loop fusion | flops 360 | bytes 76 | tf_op jit(solution)/shard_map/jit(floor_divide)/jit(_where)/select_n | solution.py:86
  55.3 1.1 fusion.46
  56.4 1.5 copy.25.kt_ref
  57.9 19.1 %shard_map.73 = bf16[4096,128]{1,0:T(8,128)(2,1)S(1)} custom-call(s32[8]{0:T(128)S(1)} %get-tuple-element.20.lo_ref, s32[8]{0:T(128)S(1)} %get-tuple-element.19.full_ref, s32[3]{0:T(128)S(1)} %convert_reduce_fusion.bnd_ref, bf16[4096,128]{1,0:T(8,128)(2,1)S(1)} %bitcast.111, bf16[128,4096]{1,0:T(8,128)(2,1)S(1)} %copy.25.kt_ref, ...), custom_call_target="tpu_custom_call" | custom-call | flops 6442450944 | bytes 4194304 | tf_op jit(solution)/shard_map/pallas_call | solution.py:90
  77.0 1.1 convert_bitcast_fusion
  78.1 3.1 %copy.27 = bf16[256,32,128]{2,1,0:T(8,128)(2,1)} copy(bf16[256,32,128]{0,2,1:T(8,128)(2,1)S(1)} %convert_bitcast_fusion) | data formatting | bytes 4194304 | tf_op jit(solution)/shard_map/convert_element_type | solution.py:187
  81.3 3.3 %pad_maximum_fusion = bf16[128,65,128]{2,1,0:T(8,128)(2,1)} fusion(bf16[128,1,128]{2,1,0:T(2,128)(2,1)S(1)} %copy.28, bf16[128,64,128]{2,1,0:T(8,128)(2,1)} %bitcast.117), kind=kLoop, calls=%fused_computation.8 | loop fusion | flops 4259840 | bytes 4259840 | tf_op jit(solution)/shard_map/concatenate | solution.py:196
  84.6 6.0 %all-to-all-start.1 = ((bf16[128,65,128]{2,1,0:T(8,128)(2,1)}), bf16[128,65,128]{2,1,0:T(8,128)(2,1)S(1)}, u32[]{:S(2)}, u32[]{:S(2)}) async-start(bf16[128,65,128]{2,1,0:T(8,128)(2,1)} %pad_maximum_fusion), calls=%async_computation.1 | async-start | bytes 4718592 | tf_op jit(solution)/shard_map/all_to_all | solution.py:197
  90.5 33.3 %all-to-all-done.1 = bf16[128,65,128]{2,1,0:T(8,128)(2,1)S(1)} async-done(((bf16[128,65,128]{2,1,0:T(8,128)(2,1)}), bf16[128,65,128]{2,1,0:T(8,128)(2,1)S(1)}, u32[]{:S(2)}, u32[]{:S(2)}) %all-to-all-start.1) | async-done | bytes 2129952 | tf_op jit(solution)/shard_map/all_to_all | solution.py:197
  123.9 0.3 slice.76
  124.2 1.4 copy.29
  125.9 12.1 %fusion.2 = bf16[256,4096]{1,0:T(8,128)(2,1)} fusion(bf16[1024,4096]{1,0:T(8,128)(2,1)} %param.13, bf16[32,8,32,128]{3,2,1,0:T(8,128)(2,1)S(1)} %bitcast.121, bf16[4096,1024]{1,0:T(8,128)(2,1)} %param.12, f32[1024]{0:T(1024)S(1)} %fusion.27, f32[256]{0:T(256)S(1)} %reshape.192), kind=kOutput, calls=%fused_computation.4 | convolution fusion | flops 4300996608 | bytes 20976640 | tf_op jit(solution)/shard_map/dot_general | solution.py:209
  138.0 4.4 %reshape.191 = bf16[128,2,4096]{2,1,0:T(2,128)(2,1)} reshape(bf16[256,4096]{1,0:T(8,128)(2,1)} %fusion.2) | data formatting | bytes 4194304 | tf_op jit(solution)/shard_map/reshape | solution.py:211
  142.4 3.8 %all-to-all-start.2 = ((bf16[128,2,4096]{2,1,0:T(2,128)(2,1)}), bf16[128,2,4096]{2,1,0:T(2,128)(2,1)S(1)}, u32[]{:S(2)}, u32[]{:S(2)}) async-start(bf16[128,2,4096]{2,1,0:T(2,128)(2,1)} %reshape.191), calls=%async_computation.2 | async-start | bytes 4194304 | tf_op jit(solution)/shard_map/all_to_all | solution.py:212
  146.3 30.6 %all-to-all-done.2 = bf16[128,2,4096]{2,1,0:T(2,128)(2,1)S(1)} async-done(((bf16[128,2,4096]{2,1,0:T(2,128)(2,1)}), bf16[128,2,4096]{2,1,0:T(2,128)(2,1)S(1)}, u32[]{:S(2)}, u32[]{:S(2)}) %all-to-all-start.2) | async-done | bytes 2097184 | tf_op jit(solution)/shard_map/all_to_all | solution.py:212
  176.9 3.5 %gather_fusion = bf16[128,4096]{1,0:T(8,128)(2,1)} fusion(bf16[128,2,4096]{2,1,0:T(2,128)(2,1)S(1)} %all-to-all-done.2, s32[128]{0:T(128)S(1)} %fusion.43), kind=kCustom, calls=%fused_computation | custom fusion | bytes 2098176 | tf_op jit(solution)/shard_map/gather | solution.py:213
  (33 shorter events, 1.8 us)
Async XLA Ops:
  2.8 1.7 copy-start
  6.9 39.5 %all-to-all-start = ((bf16[130,32,256]{2,0,1:T(8,128)(2,1)}), bf16[130,32,256]{2,0,1:T(8,128)(2,1)S(1)}, u32[]{:S(2)}, u32[]{:S(2)}) async-start(bf16[130,32,256]{2,0,1:T(8,128)(2,1)} %pad_maximum_fusion.1), calls=%async_computation | async-start | bytes 4456448 | tf_op jit(solution)/shard_map/all_to_all | solution.py:161
  49.4 5.5 %collective-permute-start = (bf16[32,64,256]{2,1,0:T(8,128)(2,1)S(1)}, bf16[32,64,256]{2,1,0:T(8,128)(2,1)S(1)}, u32[]{:S(2)}, u32[]{:S(2)}) collective-permute-start(bf16[32,64,256]{2,1,0:T(8,128)(2,1)S(1)} %reshape.184), channel_id=1, source_target_pairs={{0,4},{4,0},{8,12},{12,8},{16,20},{20,16},{24,28},{28,24},{32,36},... | collective-permute-start | bytes 3145736 | tf_op jit(solution)/shard_map/ppermute | solution.py:165
  84.6 39.3 %all-to-all-start.1 = ((bf16[128,65,128]{2,1,0:T(8,128)(2,1)}), bf16[128,65,128]{2,1,0:T(8,128)(2,1)S(1)}, u32[]{:S(2)}, u32[]{:S(2)}) async-start(bf16[128,65,128]{2,1,0:T(8,128)(2,1)} %pad_maximum_fusion), calls=%async_computation.1 | async-start | bytes 4718592 | tf_op jit(solution)/shard_map/all_to_all | solution.py:197
  142.4 3.8 %copy-start.1 = (s32[1,128]{1,0:T(1,128)S(1)}, s32[1,128]{1,0:T(1,128)}, u32[]{:S(2)}) copy-start(s32[1,128]{1,0:T(1,128)} %param.11) | copy-start | bytes 1540
  142.4 34.5 %all-to-all-start.2 = ((bf16[128,2,4096]{2,1,0:T(2,128)(2,1)}), bf16[128,2,4096]{2,1,0:T(2,128)(2,1)S(1)}, u32[]{:S(2)}, u32[]{:S(2)}) async-start(bf16[128,2,4096]{2,1,0:T(2,128)(2,1)} %reshape.191), calls=%async_computation.2 | async-start | bytes 4194304 | tf_op jit(solution)/shard_map/all_to_all | solution.py:212

commit v14 on v9

--- a/solution.py
+++ b/solution.py
@@ -68,8 +68,8 @@
 
 def attend(queries, key_rows, value_rows, segments):
     length, dim = key_rows.shape
-    bq = min(512, length)
-    bk = min(512, length)
+    bq = min(1024, length)
+    bk = min(1024, length)
     n_q = length // bq
     bounds = jnp.sum(
         segments[None, :] < jnp.arange(1, N_DOCS, dtype=jnp.int32)[:, None], axis=1

time: 181 us -> 182 us (level)
  starting transfers between devices: 24.3 us -> 18.8 us
  Pallas kernels: 15.9 us -> 20.6 us
    all_to_all x1, starting transfers between devices: 9.23 us -> 3.77 us  [local(): lax.all_to_all(send, ('seq', 'store'), split_axis=0, concat_axis=0, tiled...]
    pallas_call x1, Pallas kernels: 15.9 us -> 20.6 us  [attend(): pl.pallas_call(kernel, out_shape=jax.ShapeDtypeStruct((length, dim), jnp....]
where the time goes in v14:
time: 182 us; the launch traced here: 180 us
  waiting for transfers between devices  94 us (52%)
  local copies, waits for them, and re-layouts  23.2 us (13%)
  Pallas kernels  20.6 us (11%)
  starting transfers between devices  18.8 us (10%)
  matrix products  14 us (8%)
  other arithmetic  9.52 us (5%)
    all_to_all x1, waiting for transfers between devices, local(): lax.all_to_all(send, ('seq', 'store'), split_axis=0, concat_axis=0, tiled...  33.3 us
    all_to_all x1, waiting for transfers between devices, local(): lax.all_to_all(ret, ('seq', 'store'), split_axis=0, concat_axis=0, tiled=...  30.6 us
    all_to_all x1, waiting for transfers between devices, local(): lax.all_to_all(payload, 'seq', split_axis=1, concat_axis=0, tiled=True)  30.1 us
    pallas_call x1, Pallas kernels, attend(): pl.pallas_call(kernel, out_shape=jax.ShapeDtypeStruct((length, dim), jnp....  20.6 us
    dot_general x1, matrix products, local(): jnp.dot(low, adapter_up, preferred_element_type=jnp.float32)  12.1 us
    all_to_all x1, starting transfers between devices, local(): lax.all_to_all(payload, 'seq', split_axis=1, concat_axis=0, tiled=True)  9.42 us
    reshape x1, local copies, waits for them, and re-layouts, local(): ret = mixed_rows.reshape(devices, capacity, width)  4.38 us
    all_to_all x1, starting transfers between devices, local(): lax.all_to_all(ret, ('seq', 'store'), split_axis=0, concat_axis=0, tiled=...  3.82 us
  transfers between devices with their start and end apart: 4, of which 3 were waited for; matrix products, arithmetic and copies ran while one was open for 2% of the time, Pallas kernels for 0%

profile of v14, /device:TPU:1, one launch (start us, length us, event | category | flops | bytes accessed | tf_op | source)
XLA Modules:
  0.0 180.4 jit_solution(10410656204215588236)
XLA Ops:
  0.0 0.7 convert_bitcast_fusion.1
  0.7 0.7 and_select_fusion.4
  1.8 0.9 concatenate.24
  2.8 0.9 concatenate.25
  3.9 0.6 gather_fusion
  4.5 0.4 gather.10
  5.1 0.2 copy.41
  5.4 0.4 copy.30
  6.0 1.7 pad_maximum_fusion.1
  7.6 9.4 %all-to-all-start = ((bf16[130,32,256]{2,0,1:T(8,128)(2,1)}), bf16[130,32,256]{2,0,1:T(8,128)(2,1)S(1)}, u32[]{:S(2)}, u32[]{:S(2)}) async-start(bf16[130,32,256]{2,0,1:T(8,128)(2,1)} %pad_maximum_fusion.1), calls=%async_computation | async-start | bytes 4456448 | tf_op jit(solution)/shard_map/all_to_all | solution.py:155
  17.1 30.1 %all-to-all-done = bf16[130,32,256]{2,0,1:T(8,128)(2,1)S(1)} async-done(((bf16[130,32,256]{2,0,1:T(8,128)(2,1)}), bf16[130,32,256]{2,0,1:T(8,128)(2,1)S(1)}, u32[]{:S(2)}, u32[]{:S(2)}) %all-to-all-start) | async-done | bytes 2129952 | tf_op jit(solution)/shard_map/all_to_all | solution.py:155
  47.2 1.6 fusion.50
  48.7 1.4 reshape.264
  50.2 1.8 %collective-permute-start = (bf16[32,64,256]{2,1,0:T(8,128)(2,1)S(1)}, bf16[32,64,256]{2,1,0:T(8,128)(2,1)S(1)}, u32[]{:S(2)}, u32[]{:S(2)}) collective-permute-start(bf16[32,64,256]{2,1,0:T(8,128)(2,1)S(1)} %reshape.264), channel_id=1, source_target_pairs={{0,4},{4,0},{8,12},{12,8},{16,20},{20,16},{24,28},{28,24},{32,36},... | collective-permute-start | bytes 3145736 | tf_op jit(solution)/shard_map/ppermute | solution.py:159
  52.0 0.7 fusion.3
  53.3 0.6 fusion.52
  53.9 1.8 %and_select_fusion.1 = (s32[4]{0:T(128)S(1)}, s32[4]{0:T(128)S(1)}) fusion(s32[]{:T(128)} %bitcast.12, s32[]{:T(128)} %bitcast.11, s32[]{:T(128)} %bitcast.10), kind=kLoop, calls=%fused_computation.62 | loop fusion | flops 180 | bytes 44 | tf_op jit(solution)/shard_map/jit(floor_divide)/jit(_where)/select_n | solution.py:86
  56.1 1.1 fusion.51
  57.2 1.5 copy.32.kt_ref
  58.7 20.6 %shard_map.73 = bf16[4096,128]{1,0:T(8,128)(2,1)S(1)} custom-call(s32[4]{0:T(128)S(1)} %get-tuple-element.20.lo_ref, s32[4]{0:T(128)S(1)} %get-tuple-element.19.full_ref, s32[3]{0:T(128)S(1)} %convert_reduce_fusion.bnd_ref, bf16[4096,128]{1,0:T(8,128)(2,1)S(1)} %bitcast.113, bf16[128,4096]{1,0:T(8,128)(2,1)S(1)} %copy.32.kt_ref, ...), custom_call_target="tpu_custom_call" | custom-call | flops 6442450944 | bytes 4194304 | tf_op jit(solution)/shard_map/pallas_call | solution.py:90
  79.3 1.1 convert_bitcast_fusion
  80.4 3.1 %copy.34 = bf16[256,32,128]{2,1,0:T(8,128)(2,1)} copy(bf16[256,32,128]{0,2,1:T(8,128)(2,1)S(1)} %convert_bitcast_fusion) | data formatting | bytes 4194304 | tf_op jit(solution)/shard_map/convert_element_type | solution.py:181
  83.5 3.3 %pad_maximum_fusion = bf16[128,65,128]{2,1,0:T(8,128)(2,1)} fusion(bf16[128,1,128]{2,1,0:T(2,128)(2,1)S(1)} %copy.35, bf16[128,64,128]{2,1,0:T(8,128)(2,1)} %bitcast.119), kind=kLoop, calls=%fused_computation.9 | loop fusion | flops 4259840 | bytes 4259840 | tf_op jit(solution)/shard_map/concatenate | solution.py:190
  86.8 3.8 %all-to-all-start.1 = ((bf16[128,65,128]{2,1,0:T(8,128)(2,1)}), bf16[128,65,128]{2,1,0:T(8,128)(2,1)S(1)}, u32[]{:S(2)}, u32[]{:S(2)}) async-start(bf16[128,65,128]{2,1,0:T(8,128)(2,1)} %pad_maximum_fusion), calls=%async_computation.1 | async-start | bytes 4718592 | tf_op jit(solution)/shard_map/all_to_all | solution.py:191
  90.6 33.3 %all-to-all-done.1 = bf16[128,65,128]{2,1,0:T(8,128)(2,1)S(1)} async-done(((bf16[128,65,128]{2,1,0:T(8,128)(2,1)}), bf16[128,65,128]{2,1,0:T(8,128)(2,1)S(1)}, u32[]{:S(2)}, u32[]{:S(2)}) %all-to-all-start.1) | async-done | bytes 2129952 | tf_op jit(solution)/shard_map/all_to_all | solution.py:191
  123.9 0.3 slice.78
  124.2 1.4 copy.36
  126.0 12.1 %fusion.2 = bf16[256,4096]{1,0:T(8,128)(2,1)} fusion(bf16[1024,4096]{1,0:T(8,128)(2,1)} %param.13, bf16[32,8,32,128]{3,2,1,0:T(8,128)(2,1)S(1)} %bitcast.123, bf16[4096,1024]{1,0:T(8,128)(2,1)} %param.12, f32[1024]{0:T(1024)S(1)} %fusion.27, f32[256]{0:T(256)S(1)} %reshape.272), kind=kOutput, calls=%fused_computation.5 | convolution fusion | flops 4300996608 | bytes 20976640 | tf_op jit(solution)/shard_map/dot_general | solution.py:203
  138.1 4.4 %reshape.271 = bf16[128,2,4096]{2,1,0:T(2,128)(2,1)} reshape(bf16[256,4096]{1,0:T(8,128)(2,1)} %fusion.2) | data formatting | bytes 4194304 | tf_op jit(solution)/shard_map/reshape | solution.py:205
  142.5 3.8 %all-to-all-start.2 = ((bf16[128,2,4096]{2,1,0:T(2,128)(2,1)}), bf16[128,2,4096]{2,1,0:T(2,128)(2,1)S(1)}, u32[]{:S(2)}, u32[]{:S(2)}) async-start(bf16[128,2,4096]{2,1,0:T(2,128)(2,1)} %reshape.271), calls=%async_computation.2 | async-start | bytes 4194304 | tf_op jit(solution)/shard_map/all_to_all | solution.py:206
  146.3 30.6 %all-to-all-done.2 = bf16[128,2,4096]{2,1,0:T(2,128)(2,1)S(1)} async-done(((bf16[128,2,4096]{2,1,0:T(2,128)(2,1)}), bf16[128,2,4096]{2,1,0:T(2,128)(2,1)S(1)}, u32[]{:S(2)}, u32[]{:S(2)}) %all-to-all-start.2) | async-done | bytes 2097184 | tf_op jit(solution)/shard_map/all_to_all | solution.py:206
  176.9 3.5 %gather_fusion.1 = bf16[128,4096]{1,0:T(8,128)(2,1)} fusion(bf16[128,2,4096]{2,1,0:T(2,128)(2,1)S(1)} %all-to-all-done.2, s32[128]{0:T(128)S(1)} %fusion.48), kind=kCustom, calls=%fused_computation.1 | custom fusion | bytes 2098176 | tf_op jit(solution)/shard_map/gather | solution.py:207
  (37 shorter events, 2.3 us)
Async XLA Ops:
  3.9 1.2 copy-start
  7.6 39.5 %all-to-all-start = ((bf16[130,32,256]{2,0,1:T(8,128)(2,1)}), bf16[130,32,256]{2,0,1:T(8,128)(2,1)S(1)}, u32[]{:S(2)}, u32[]{:S(2)}) async-start(bf16[130,32,256]{2,0,1:T(8,128)(2,1)} %pad_maximum_fusion.1), calls=%async_computation | async-start | bytes 4456448 | tf_op jit(solution)/shard_map/all_to_all | solution.py:155
  50.2 5.5 %collective-permute-start = (bf16[32,64,256]{2,1,0:T(8,128)(2,1)S(1)}, bf16[32,64,256]{2,1,0:T(8,128)(2,1)S(1)}, u32[]{:S(2)}, u32[]{:S(2)}) collective-permute-start(bf16[32,64,256]{2,1,0:T(8,128)(2,1)S(1)} %reshape.264), channel_id=1, source_target_pairs={{0,4},{4,0},{8,12},{12,8},{16,20},{20,16},{24,28},{28,24},{32,36},... | collective-permute-start | bytes 3145736 | tf_op jit(solution)/shard_map/ppermute | solution.py:159
  86.8 37.1 %all-to-all-start.1 = ((bf16[128,65,128]{2,1,0:T(8,128)(2,1)}), bf16[128,65,128]{2,1,0:T(8,128)(2,1)S(1)}, u32[]{:S(2)}, u32[]{:S(2)}) async-start(bf16[128,65,128]{2,1,0:T(8,128)(2,1)} %pad_maximum_fusion), calls=%async_computation.1 | async-start | bytes 4718592 | tf_op jit(solution)/shard_map/all_to_all | solution.py:191
  142.5 3.8 %copy-start.1 = (s32[1,128]{1,0:T(1,128)S(1)}, s32[1,128]{1,0:T(1,128)}, u32[]{:S(2)}) copy-start(s32[1,128]{1,0:T(1,128)} %param.11) | copy-start | bytes 1540
  142.5 34.5 %all-to-all-start.2 = ((bf16[128,2,4096]{2,1,0:T(2,128)(2,1)}), bf16[128,2,4096]{2,1,0:T(2,128)(2,1)S(1)}, u32[]{:S(2)}, u32[]{:S(2)}) async-start(bf16[128,2,4096]{2,1,0:T(2,128)(2,1)} %reshape.271), calls=%async_computation.2 | async-start | bytes 4194304 | tf_op jit(solution)/shard_map/all_to_all | solution.py:206

commit v15 on v9

--- a/solution.py
+++ b/solution.py
@@ -158,8 +158,12 @@
     kv_mine = got_in[:, :tok_rows, feat:].reshape(n_seq, half, 2 * HEAD_DIM)
     kv_other = lax.ppermute(kv_mine, "seq", [(i, i ^ 1) for i in range(n_seq)])
     even = lax.axis_index("seq") % 2 == 0
-    kv_all = jnp.stack(
-        [jnp.where(even, kv_mine, kv_other), jnp.where(even, kv_other, kv_mine)], axis=1
+    kv_all = lax.cond(
+        even,
+        lambda a, b: jnp.stack([a, b], axis=1),
+        lambda a, b: jnp.stack([b, a], axis=1),
+        kv_mine,
+        kv_other,
     ).reshape(length, 2 * HEAD_DIM)
     k_all = kv_all[:, :HEAD_DIM]
     v_all = kv_all[:, HEAD_DIM:]

time: 181 us -> 196 us (1.083)
  local copies, waits for them, and re-layouts: 23.2 us -> 34.5 us
  starting transfers between devices: 24.3 us -> 21 us
  Pallas kernels: 15.9 us -> 19.1 us
  other arithmetic: 9.52 us -> 12.7 us
    concatenate x0 -> x1, local copies, waits for them, and re-layouts: none -> 5.63 us  [local(): jnp.concatenate([jnp.concatenate([q_send, kv_send], axis=2), jnp.broadcas...]
    all_to_all x1, starting transfers between devices: 9.23 us -> 6.04 us  [local(): lax.all_to_all(send, ('seq', 'store'), split_axis=0, concat_axis=0, tiled...]
    pallas_call x1, Pallas kernels: 15.9 us -> 19.1 us  [attend(): pl.pallas_call(kernel, out_shape=jax.ShapeDtypeStruct((length, dim), jnp....]
    cond x0 -> x3, local copies, waits for them, and re-layouts: none -> 2.69 us  [the longest x1 1.73 us: local(): lax.cond(even, lambda a, b: jnp.stack([a, b], axis=1), lambda a, b: jnp.s...]
    another operation x3 -> x2, other arithmetic: 0.35 us -> 2.77 us  [the longest x1 2.76 us: local(): jnp.stack([b, a], axis=1)]
where the time goes in v15:
time: 196 us
  waiting for transfers between devices  94 us (48%)
  local copies, waits for them, and re-layouts  34.5 us (18%)
  starting transfers between devices  21 us (11%)
  Pallas kernels  19.1 us (10%)
  matrix products  14 us (7%)
  other arithmetic  12.7 us (6%)
    all_to_all x1, waiting for transfers between devices, local(): lax.all_to_all(send, ('seq', 'store'), split_axis=0, concat_axis=0, tiled...  33.3 us
    all_to_all x1, waiting for transfers between devices, local(): lax.all_to_all(ret, ('seq', 'store'), split_axis=0, concat_axis=0, tiled=...  30.6 us
    all_to_all x1, waiting for transfers between devices, local(): lax.all_to_all(payload, 'seq', split_axis=1, concat_axis=0, tiled=True)  30.1 us
    pallas_call x1, Pallas kernels, attend(): pl.pallas_call(kernel, out_shape=jax.ShapeDtypeStruct((length, dim), jnp....  19.1 us
    dot_general x1, matrix products, local(): jnp.dot(low, adapter_up, preferred_element_type=jnp.float32)  12.2 us
    all_to_all x1, starting transfers between devices, local(): lax.all_to_all(payload, 'seq', split_axis=1, concat_axis=0, tiled=True)  9.42 us
    all_to_all x1, starting transfers between devices, local(): lax.all_to_all(send, ('seq', 'store'), split_axis=0, concat_axis=0, tiled...  6.04 us
    concatenate x1, local copies, waits for them, and re-layouts, local(): jnp.concatenate([jnp.concatenate([q_send, kv_send], axis=2), jnp.broadcas...  5.63 us
  transfers between devices with their start and end apart: 4, of which 3 were waited for; matrix products, arithmetic and copies ran while one was open for 2% of the time, Pallas kernels for 0%

profile of v15, /device:TPU:1, one launch (start us, length us, event | category | flops | bytes accessed | tf_op | source)
XLA Modules:
  0.0 195.7 jit_solution(9929861027050473258)
XLA Ops:
  0.0 0.7 and_select_fusion.4
  2.0 0.9 concatenate.25
  2.9 0.9 concatenate.24
  5.1 0.7 copy.52
  7.2 2.4 %pad_maximum_fusion.2 = bf16[130,32,256]{0,2,1:T(8,128)(2,1)} fusion(bf16[2,32,256]{0,2,1:T(8,128)(2,1)S(1)} %broadcast_in_dim.45, bf16[128,32,128]{0,2,1:T(8,128)(2,1)S(1)} %select_bitcast_fusion, bf16[128,32,128]{0,2,1:T(8,128)(2,1)S(1)} %bitcast.118), kind=kLoop, calls=%fused_computation.8 | loop fusion | flops 6389760 | bytes 4259840 | tf_op jit(solution)/shard_map/concatenate | solution.py:148
  9.7 5.6 %copy.54 = bf16[130,32,256]{2,0,1:T(8,128)(2,1)} copy(bf16[130,32,256]{0,2,1:T(8,128)(2,1)} %pad_maximum_fusion.2) | data formatting | bytes 4259840 | tf_op jit(solution)/shard_map/concatenate | solution.py:148
  15.3 9.4 %all-to-all-start = ((bf16[130,32,256]{2,0,1:T(8,128)(2,1)}), bf16[130,32,256]{2,0,1:T(8,128)(2,1)S(1)}, u32[]{:S(2)}, u32[]{:S(2)}) async-start(bf16[130,32,256]{2,0,1:T(8,128)(2,1)} %copy.54), calls=%async_computation | async-start | bytes 4456448 | tf_op jit(solution)/shard_map/all_to_all | solution.py:155
  24.7 30.1 %all-to-all-done = bf16[130,32,256]{2,0,1:T(8,128)(2,1)S(1)} async-done(((bf16[130,32,256]{2,0,1:T(8,128)(2,1)}), bf16[130,32,256]{2,0,1:T(8,128)(2,1)S(1)}, u32[]{:S(2)}, u32[]{:S(2)}) %all-to-all-start) | async-done | bytes 2129952 | tf_op jit(solution)/shard_map/all_to_all | solution.py:155
  54.8 1.4 copy-done
  56.2 1.7 fusion.50
  57.9 1.2 reshape.264
  59.1 1.7 collective-permute-start
  60.8 0.7 fusion.3
  62.8 1.9 and_select_fusion.1
  64.7 4.1 %conditional.1 = (bf16[32,2,64,256]{3,2,0,1:T(8,128)(2,1)}) conditional(s32[]{:T(128)} %convert_element_type.78, (bf16[32,64,256]{2,1,0:T(8,128)(2,1)S(1)}, bf16[32,128,128]{2,1,0:T(8,128)(2,1)S(1)}) %tuple.11, (bf16[32,128,128]{2,1,0:T(8,128)(2,1)S(1)}, bf16[32,64,256]{2,1,0:T(8,128)(2,1)S(1)}) %tuple.12), branch_computations={%region_3.4_spmd, %region_4.5_spmd} | conditional | flops 1048576 | bytes 10485796 | solution.py:161
  64.7 1.0 copy-done.1
  66.0 2.8 %pad_maximum_fusion = bf16[32,2,64,256]{3,2,0,1:T(8,128)(2,1)} fusion(bf16[32,1,64,256]{3,2,0,1:T(8,128)(2,1)S(1)} %stack_reshape.4, bf16[32,1,64,256]{3,2,0,1:T(8,128)(2,1)} %bitcast.116), kind=kLoop, calls=%fused_computation.2 | loop fusion | flops 1048576 | bytes 4194304 | tf_op jit(solution)/shard_map/cond/branch_0_fun/stack | solution.py:164
  68.8 1.7 copy.55
  70.5 1.1 fusion.51
  71.6 1.5 copy.56.kt_ref
  73.1 19.1 %shard_map.73 = bf16[4096,128]{1,0:T(8,128)(2,1)S(1)} custom-call(s32[8]{0:T(128)S(1)} %get-tuple-element.41.lo_ref, s32[8]{0:T(128)S(1)} %get-tuple-element.40.full_ref, s32[3]{0:T(128)S(1)} %convert_reduce_fusion.bnd_ref, bf16[4096,128]{1,0:T(8,128)(2,1)S(1)} %bitcast.107, bf16[128,4096]{1,0:T(8,128)(2,1)S(1)} %copy.56.kt_ref, ...), custom_call_target="tpu_custom_call" | custom-call | flops 6442450944 | bytes 4194304 | tf_op jit(solution)/shard_map/pallas_call | solution.py:90
  92.2 1.1 convert_bitcast_fusion
  93.4 3.1 %copy.58 = bf16[256,32,128]{2,1,0:T(8,128)(2,1)} copy(bf16[256,32,128]{0,2,1:T(8,128)(2,1)S(1)} %convert_bitcast_fusion) | data formatting | bytes 4194304 | tf_op jit(solution)/shard_map/convert_element_type | solution.py:185
  96.5 3.3 %pad_maximum_fusion.3 = bf16[128,65,128]{2,1,0:T(8,128)(2,1)} fusion(bf16[128,1,128]{2,1,0:T(2,128)(2,1)S(1)} %copy.59, bf16[128,64,128]{2,1,0:T(8,128)(2,1)} %bitcast.113), kind=kLoop, calls=%fused_computation.12 | loop fusion | flops 4259840 | bytes 4259840 | tf_op jit(solution)/shard_map/concatenate | solution.py:194
  99.8 6.0 %all-to-all-start.1 = ((bf16[128,65,128]{2,1,0:T(8,128)(2,1)}), bf16[128,65,128]{2,1,0:T(8,128)(2,1)S(1)}, u32[]{:S(2)}, u32[]{:S(2)}) async-start(bf16[128,65,128]{2,1,0:T(8,128)(2,1)} %pad_maximum_fusion.3), calls=%async_computation.1 | async-start | bytes 4718592 | tf_op jit(solution)/shard_map/all_to_all | solution.py:195
  105.8 33.3 %all-to-all-done.1 = bf16[128,65,128]{2,1,0:T(8,128)(2,1)S(1)} async-done(((bf16[128,65,128]{2,1,0:T(8,128)(2,1)}), bf16[128,65,128]{2,1,0:T(8,128)(2,1)S(1)}, u32[]{:S(2)}, u32[]{:S(2)}) %all-to-all-start.1) | async-done | bytes 2129952 | tf_op jit(solution)/shard_map/all_to_all | solution.py:195
  139.5 1.4 copy.60
  141.2 12.2 %fusion.2 = bf16[256,4096]{1,0:T(8,128)(2,1)} fusion(bf16[1024,4096]{1,0:T(8,128)(2,1)} %param.15, bf16[32,8,32,128]{3,2,1,0:T(8,128)(2,1)S(1)} %bitcast.119, bf16[4096,1024]{1,0:T(8,128)(2,1)} %param.14, f32[1024]{0:T(1024)S(1)} %fusion.27, f32[256]{0:T(256)S(1)} %reshape.272), kind=kOutput, calls=%fused_computation.7 | convolution fusion | flops 4300996608 | bytes 20976640 | tf_op jit(solution)/shard_map/dot_general | solution.py:207
  153.3 4.4 %reshape.271 = bf16[128,2,4096]{2,1,0:T(2,128)(2,1)} reshape(bf16[256,4096]{1,0:T(8,128)(2,1)} %fusion.2) | data formatting | bytes 4194304 | tf_op jit(solution)/shard_map/reshape | solution.py:209
  157.7 3.8 %all-to-all-start.2 = ((bf16[128,2,4096]{2,1,0:T(2,128)(2,1)}), bf16[128,2,4096]{2,1,0:T(2,128)(2,1)S(1)}, u32[]{:S(2)}, u32[]{:S(2)}) async-start(bf16[128,2,4096]{2,1,0:T(2,128)(2,1)} %reshape.271), calls=%async_computation.2 | async-start | bytes 4194304 | tf_op jit(solution)/shard_map/all_to_all | solution.py:210
  161.6 30.6 %all-to-all-done.2 = bf16[128,2,4096]{2,1,0:T(2,128)(2,1)S(1)} async-done(((bf16[128,2,4096]{2,1,0:T(2,128)(2,1)}), bf16[128,2,4096]{2,1,0:T(2,128)(2,1)S(1)}, u32[]{:S(2)}, u32[]{:S(2)}) %all-to-all-start.2) | async-done | bytes 2097184 | tf_op jit(solution)/shard_map/all_to_all | solution.py:210
  192.2 3.5 %gather_fusion.1 = bf16[128,4096]{1,0:T(8,128)(2,1)} fusion(bf16[128,2,4096]{2,1,0:T(2,128)(2,1)S(1)} %all-to-all-done.2, s32[128]{0:T(128)S(1)} %fusion.48), kind=kCustom, calls=%fused_computation.1 | custom fusion | bytes 2098176 | tf_op jit(solution)/shard_map/gather | solution.py:211
  (45 shorter events, 6.1 us)
Async XLA Ops:
  4.7 1.2 copy-start.3
  15.3 39.5 %all-to-all-start = ((bf16[130,32,256]{2,0,1:T(8,128)(2,1)}), bf16[130,32,256]{2,0,1:T(8,128)(2,1)S(1)}, u32[]{:S(2)}, u32[]{:S(2)}) async-start(bf16[130,32,256]{2,0,1:T(8,128)(2,1)} %copy.54), calls=%async_computation | async-start | bytes 4456448 | tf_op jit(solution)/shard_map/all_to_all | solution.py:155
  54.8 1.4 copy-start
  59.1 5.5 %collective-permute-start = (bf16[32,64,256]{2,1,0:T(8,128)(2,1)}, bf16[32,64,256]{2,1,0:T(8,128)(2,1)S(1)}, u32[]{:S(2)}, u32[]{:S(2)}) collective-permute-start(bf16[32,64,256]{2,1,0:T(8,128)(2,1)} %reshape.264), channel_id=1, source_target_pairs={{0,4},{4,0},{8,12},{12,8},{16,20},{20,16},{24,28},{28,24},{32,36},... | collective-permute-start | bytes 3145736 | tf_op jit(solution)/shard_map/ppermute | solution.py:159
  64.7 1.0 copy-start.1
  99.8 39.4 %all-to-all-start.1 = ((bf16[128,65,128]{2,1,0:T(8,128)(2,1)}), bf16[128,65,128]{2,1,0:T(8,128)(2,1)S(1)}, u32[]{:S(2)}, u32[]{:S(2)}) async-start(bf16[128,65,128]{2,1,0:T(8,128)(2,1)} %pad_maximum_fusion.3), calls=%async_computation.1 | async-start | bytes 4718592 | tf_op jit(solution)/shard_map/all_to_all | solution.py:195
  157.7 3.8 %copy-start.4 = (s32[1,128]{1,0:T(1,128)S(1)}, s32[1,128]{1,0:T(1,128)}, u32[]{:S(2)}) copy-start(s32[1,128]{1,0:T(1,128)} %param.13) | copy-start | bytes 1540
  157.7 34.5 %all-to-all-start.2 = ((bf16[128,2,4096]{2,1,0:T(2,128)(2,1)}), bf16[128,2,4096]{2,1,0:T(2,128)(2,1)S(1)}, u32[]{:S(2)}, u32[]{:S(2)}) async-start(bf16[128,2,4096]{2,1,0:T(2,128)(2,1)} %reshape.271), calls=%async_computation.2 | async-start | bytes 4194304 | tf_op jit(solution)/shard_map/all_to_all | solution.py:210
